TPU v7x, 128 devices: a whole 4x4x4 slice. The times are simulated.
128 devices in a mesh: dp: 4 (over x), head: 8 (over y, core), blk: 4 (over z).
Axes of the slice: x: 4, y: 4, z: 4, core: 2. Of those that a mesh axis runs over, the one named last changes fastest.
Arguments:
- query: bfloat16 [65536, 2048], P(('dp', 'head', 'blk')), parts along dimension 0, may hold values from -7 to 7
- key: bfloat16 [65536, 2048], P(('dp', 'head', 'blk')), parts along dimension 0, may hold values from -7 to 7
- value: bfloat16 [65536, 2048], P(('dp', 'head', 'blk')), parts along dimension 0, may hold values from -30 to 30
- dout: bfloat16 [65536, 2048], P(('dp', 'head', 'blk')), parts along dimension 0, may hold values from -30 to 30
- rand: int32 [1024, 3], P('dp'), parts along dimension 0, may hold values from 0 to 255, as said below
Outputs:
- out: bfloat16 [65536, 2048], P(('dp', 'head', 'blk')), parts along dimension 0
- dq: bfloat16 [65536, 2048], P(('dp', 'head', 'blk')), parts along dimension 0
- dk: bfloat16 [65536, 2048], P(('dp', 'head', 'blk')), parts along dimension 0
- dv: bfloat16 [65536, 2048], P(('dp', 'head', 'blk')), parts along dimension 0
There are 4 independent parts, one for each index of `dp`. A program takes and returns all parts, laid end to end along the dimension named above; each array names one. Nothing has to cross between parts.
Inputs may be any that keep to these rules, and one draw needn't show every extreme that they name: `rand`: for each group of 8 consecutive query blocks (the rows of one device), at most 1 of its 24 random blocks fall in any one group of 8 consecutive blocks.
All inputs are finite; a program needn't handle non-finite values.
Results may differ from a plain program's by a relative error of at most 0.023.
Values may be sent and summed in bfloat16 or wider, within the bound.
No kernel may reach another device: no remote copies, remote signals or barrier semaphores. Data moves between devices by JAX's collectives and lax.ppermute only.
A program may use at most 448 MiB of HBM per device.

v0:
```python
import math

import jax
import jax.numpy as jnp
from jax import lax
from jax.sharding import PartitionSpec as P

HD = 128
BS = 64
R = 3


NEG = -1e30


def extended(block, sides, width):
    for axis, dim in sides:
        count = lax.axis_size(axis)
        forward = [(i, i + 1) for i in range(count - 1)]
        backward = [(target, source) for source, target in forward]
        low = lax.ppermute(
            lax.slice_in_dim(block, block.shape[dim] - width, None, axis=dim), axis, forward
        )
        high = lax.ppermute(lax.slice_in_dim(block, 0, width, axis=dim), axis, backward)
        block = jnp.concatenate([low, block, high], axis=dim)
    return block


def from_root(value, axis, source):
    kept = jnp.where(lax.axis_index(axis) == source, value, 0).astype(value.dtype)
    return lax.psum(kept, axis)


def body(query, key, value, dout, rand):
    rows, width = query.shape
    heads = width // HD
    both = 2 * width
    ndev = lax.axis_size(("head", "blk"))
    me = lax.axis_index(("head", "blk"))
    nbd = rows // BS
    total = nbd * ndev
    cap = (R * nbd + ndev - 1) // ndev
    scale = 1.0 / math.sqrt(HD)
    pf = jnp.float32
    span = (5 + R) * BS
    pair = jnp.concatenate([key, value], axis=1)
    padded = extended(pair, ((("head", "blk"), 0),), BS)
    glob = from_root(pair[: 2 * BS], ("head", "blk"), 0)
    flat = rand.reshape(ndev, nbd * R)
    owner = flat // nbd
    local = flat - owner * nbd
    hit = owner == me
    order = jnp.cumsum(hit.astype(jnp.int32), axis=1) - 1
    slot_ids = jnp.arange(cap, dtype=jnp.int32)
    chosen = hit[:, None, :] & (order[:, None, :] == slot_ids[None, :, None])
    block_id = jnp.sum(jnp.where(chosen, local[:, None, :], 0), axis=2).reshape(-1)
    filled = jnp.any(chosen, axis=2).reshape(-1)
    tiles = pair.reshape(nbd, BS, both)
    outgoing = jnp.where(
        filled[:, None, None], jnp.take(tiles, block_id, axis=0), jnp.zeros((), pair.dtype)
    )
    fetched = lax.all_to_all(outgoing, ("head", "blk"), split_axis=0, concat_axis=0, tiled=True)
    mine = lax.dynamic_slice_in_dim(rand, me * nbd, nbd, 0).reshape(-1)
    mine_owner = mine // nbd
    count = mine.shape[0]
    earlier = jnp.arange(count)[:, None] > jnp.arange(count)[None, :]
    same = mine_owner[:, None] == mine_owner[None, :]
    mine_rank = jnp.sum(earlier & same, axis=1)
    mine_slot = mine_owner * cap + mine_rank
    remote = jnp.take(fetched, mine_slot, axis=0).reshape(nbd, R * BS, both)
    ptiles = padded.reshape(nbd + 2, BS, both)
    window = jnp.concatenate([ptiles[:-2], ptiles[1:-1], ptiles[2:]], axis=1)
    glob_rows = jnp.broadcast_to(glob[None], (nbd, 2 * BS, both))
    listed = jnp.concatenate([window, glob_rows, remote], axis=1)
    all_key = listed[..., :width].reshape(nbd, span, heads, HD)
    all_value = listed[..., width:].reshape(nbd, span, heads, HD)
    q4 = query.reshape(nbd, BS, heads, HD)
    scores = jnp.einsum("nqhd,nkhd->nhqk", q4, all_key, preferred_element_type=pf) * scale
    first = me * nbd + jnp.arange(nbd, dtype=jnp.int32)
    always = first >= 0
    valid = jnp.concatenate(
        [
            jnp.stack([first > 0, always, first < total - 1, always, always], axis=1),
            jnp.ones((nbd, R), bool),
        ],
        axis=1,
    )
    valid_keys = jnp.repeat(valid, BS, axis=1)
    scores = jnp.where(valid_keys[:, None, None, :], scores, NEG)
    top = jnp.max(scores, axis=3, keepdims=True)
    expo = jnp.exp(scores - top)
    probs = expo / jnp.sum(expo, axis=3, keepdims=True)
    probs_b = probs.astype(jnp.bfloat16)
    result = jnp.einsum("nhqk,nkhd->nqhd", probs_b, all_value, preferred_element_type=pf)
    result_b = result.astype(jnp.bfloat16)
    out = result_b.reshape(rows, width)
    d4 = dout.reshape(nbd, BS, heads, HD)
    delta = jnp.einsum("nqhd,nqhd->nhq", d4, result_b, preferred_element_type=pf)
    dprob = jnp.einsum("nqhd,nkhd->nhqk", d4, all_value, preferred_element_type=pf)
    dscore = probs * (dprob - delta[:, :, :, None])
    dscore_b = dscore.astype(jnp.bfloat16)
    grad_query = jnp.einsum("nhqk,nkhd->nqhd", dscore_b, all_key, preferred_element_type=pf) * scale
    dq = grad_query.astype(jnp.bfloat16).reshape(rows, width)
    key_terms = (
        jnp.einsum("nhqk,nqhd->nkhd", dscore_b, q4, preferred_element_type=pf) * scale
    ).reshape(nbd, span, width)
    value_terms = jnp.einsum("nhqk,nqhd->nkhd", probs_b, d4, preferred_element_type=pf).reshape(
        nbd, span, width
    )
    win_grad = jnp.concatenate([key_terms[:, : 3 * BS], value_terms[:, : 3 * BS]], axis=-1).reshape(
        nbd, 3, BS, both
    )
    summed = jnp.zeros((nbd + 2, BS, both), pf)
    summed = (
        summed.at[:nbd]
        .add(win_grad[:, 0])
        .at[1 : nbd + 1]
        .add(win_grad[:, 1])
        .at[2:]
        .add(win_grad[:, 2])
    )
    rims = jnp.concatenate([summed[0], summed[nbd + 1]], axis=0)
    arrived = extended(rims.astype(jnp.bfloat16), ((("head", "blk"), 0),), BS).astype(rims.dtype)
    own = summed[1 : nbd + 1]
    own = own.at[0].add(arrived[:BS]).at[nbd - 1].add(arrived[3 * BS :])
    glob_grad = jnp.concatenate(
        [
            jnp.sum(key_terms[:, 3 * BS : 5 * BS], axis=0),
            jnp.sum(value_terms[:, 3 * BS : 5 * BS], axis=0),
        ],
        axis=-1,
    ).reshape(2, BS, both)
    glob_total = lax.psum(glob_grad.astype(jnp.bfloat16), ("head", "blk")).astype(jnp.float32)
    own = own.at[:2].add(jnp.where(me == 0, glob_total, 0.0))
    rand_grad = jnp.concatenate([key_terms[:, 5 * BS :], value_terms[:, 5 * BS :]], axis=-1)
    rand_grad = rand_grad.astype(jnp.bfloat16).reshape(nbd * R, BS, both)
    returning = jnp.zeros((ndev * cap, BS, both), jnp.bfloat16).at[mine_slot].set(rand_grad)
    back = lax.all_to_all(returning, ("head", "blk"), split_axis=0, concat_axis=0, tiled=True)
    onehot = (
        (block_id[None, :] == jnp.arange(nbd, dtype=jnp.int32)[:, None]) & filled[None, :]
    ).astype(jnp.bfloat16)
    own = own + jnp.dot(
        onehot, back.reshape(ndev * cap, BS * both), preferred_element_type=pf
    ).reshape(nbd, BS, both)
    dk = own[..., :width].astype(jnp.bfloat16).reshape(rows, width)
    dv = own[..., width:].astype(jnp.bfloat16).reshape(rows, width)
    return (out, dq, dk, dv)


def solution(mesh):
    placed = (
        P(("dp", "head", "blk"), None),
        P(("dp", "head", "blk"), None),
        P(("dp", "head", "blk"), None),
        P(("dp", "head", "blk"), None),
        P("dp", None),
    )
    return jax.shard_map(
        body,
        mesh=mesh,
        in_specs=placed,
        out_specs=(
            P(("dp", "head", "blk"), None),
            P(("dp", "head", "blk"), None),
            P(("dp", "head", "blk"), None),
            P(("dp", "head", "blk"), None),
        ),
        check_vma=False,
    )
```

profile of v0, /device:TPU:14, one launch (start us, length us, event | category | flops | bytes accessed | tf_op | source)
XLA Modules:
  0.0 989.5 jit_solution(15961484770271441336)
XLA Ops:
  24.4 14.3 %select_select_fusion = bf16[32,64,4096]{2,1,0:T(8,128)(2,1)} fusion(bf16[32,64,4096]{2,1,0:T(8,128)(2,1)} %gather_fusion, pred[32]{0:T(512)(128)(4,1)S(1)} %compare_and_fusion.1, pred[32]{0:T(512)(128)(4,1)S(1)} %get-tuple-element.76), kind=kLoop, calls=%fused_computation.16 | loop fusion | flops 16777216 | bytes 33554496 | tf_op jit(solution)/shard_map/jit(_where)/select_n | solution.py:59
  62.5 218.2 %collective-permute-done.1 = bf16[64,4096]{1,0:T(8,128)(2,1)} collective-permute-done((bf16[64,4096]{1,0:T(8,128)(2,1)S(1)}, bf16[64,4096]{1,0:T(8,128)(2,1)}, u32[]{:S(2)}, u32[]{:S(2)}) %collective-permute-start.1) | collective-permute-done | bytes 524320 | tf_op jit(solution)/shard_map/ppermute | solution.py:24
  299.5 31.2 %all-reduce.4.cloned.1.call-done = bf16[128,4096]{1,0:T(8,128)(2,1)} async-done(((bf16[128,4096]{1,0:T(8,128)(2,1)}), bf16[128,4096]{1,0:T(8,128)(2,1)}) %all-reduce.4.cloned.1.call-update) | async-done | bytes 1048592 | tf_op jit(solution)/shard_map/psum | solution.py:31
  336.2 11.8 %gather_fusion.1 = bf16[24,64,4096]{2,1,0:T(8,128)(2,1)} fusion(bf16[32,64,4096]{2,1,0:T(8,128)(2,1)} %all-to-all-done, s32[1024]{0:T(1024)S(1)} %pad_clamp_fusion), kind=kCustom, calls=%fused_computation.1 | custom fusion | bytes 25165920 | tf_op jit(solution)/shard_map/jit(_take)/gather | solution.py:70
  348.0 11.5 %fusion.9 = bf16[8,512,4096]{2,1,0:T(8,128)(2,1)} fusion(bf16[8,512,4096]{2,1,0:T(8,128)(2,1)} %broadcast_dynamic-update-slice_fusion, pred[8,192]{1,0:T(8,128)(4,1)S(1)} %broadcast_in_dim.86, bf16[8,192,4096]{2,1,0:T(8,128)(2,1)} %bitcast.137), kind=kLoop, calls=%fused_computation.19 | loop fusion | flops 6291456 | bytes 25167360 | tf_op jit(solution)/shard_map/concatenate | solution.py:74
  359.5 23.5 %fusion.60 = (bf16[8,512,2048]{2,1,0:T(8,128)(2,1)}, bf16[8,512,2048]{2,1,0:T(8,128)(2,1)}) fusion(bf16[8,512,4096]{2,1,0:T(8,128)(2,1)} %fusion.9), kind=kLoop, calls=%fused_computation.135 | loop fusion | bytes 67108864 | tf_op jit(solution)/shard_map/slice | solution.py:75
  383.0 21.6 %copy.108 = bf16[8,512,2048]{1,2,0:T(8,128)(2,1)} copy(bf16[8,512,2048]{2,1,0:T(8,128)(2,1)} %get-tuple-element.78) | data formatting | bytes 33554432 | tf_op jit(solution)/shard_map/slice | solution.py:75
  404.6 21.6 %copy.107 = bf16[8,512,2048]{1,2,0:T(8,128)(2,1)} copy(bf16[8,512,2048]{2,1,0:T(8,128)(2,1)} %get-tuple-element.79) | data formatting | bytes 33554432 | tf_op jit(solution)/shard_map/slice | solution.py:76
  426.1 13.9 %fusion.25 = f32[8,16,512,64]{2,3,1,0:T(8,128)} fusion(bf16[8,512,16,128]{1,3,2,0:T(8,128)(2,1)} %bitcast.132, bf16[8,64,16,128]{3,2,1,0:T(8,128)(2,1)S(1)} %bitcast.143), kind=kOutput, calls=%fused_computation.50 | convolution fusion | flops 1073741824 | bytes 35651584 | tf_op jit(solution)/shard_map/nqhd,nkhd->nhqk/dot_general | solution.py:78
  440.1 19.2 %fusion.63 = (f32[8,16,64]{2,1,0:T(8,128)S(1)}, f32[8,16,64,512]{3,2,1,0:T(8,128)}) fusion(f32[8,16,512,64]{2,3,1,0:T(8,128)} %fusion.25, pred[8,512]{1,0:T(8,128)(4,1)S(1)} %broadcast_in_dim.94), kind=kOutput, calls=%fused_computation.138 | output fusion | flops 25166336 | bytes 33591296 | tf_op jit(solution)/shard_map/sub | solution.py:91
  459.2 20.8 %bitcast_convert_fusion = (f32[8,16,64,128]{3,2,1,0:T(8,128)}, bf16[8,16,128,64]{2,3,1,0:T(8,128)(2,1)}) fusion(bf16[8,512,16,128]{1,3,2,0:T(8,128)(2,1)} %bitcast.145, f32[8,16,64,512]{3,2,1,0:T(8,128)} %get-tuple-element.87, f32[8,16,64]{2,1,0:T(8,128)S(1)} %get-tuple-element.86), kind=kOutput, calls=%fused_computation.44 | convolution fusion | flops 1084227584 | bytes 39878656 | tf_op jit(solution)/shard_map/nhqk,nkhd->nqhd/dot_general | solution.py:94
  484.9 19.6 %fusion.21 = f32[8,16,512,128]{2,3,1,0:T(8,128)} fusion(bf16[8,64,16,128]{3,2,1,0:T(8,128)(2,1)} %bitcast.149, f32[8,16,64,512]{3,2,1,0:T(8,128)} %get-tuple-element.87, f32[8,16,64]{2,1,0:T(8,128)S(1)} %get-tuple-element.86), kind=kOutput, calls=%fused_computation.46 | convolution fusion | flops 1082130432 | bytes 52461568 | tf_op jit(solution)/shard_map/nhqk,nqhd->nkhd/dot_general | solution.py:107
  504.5 16.1 %fusion.4 = bf16[8,16,64,512]{3,2,1,0:T(8,128)(2,1)} fusion(bf16[8,512,16,128]{1,3,2,0:T(8,128)(2,1)} %bitcast.146, f32[8,16,64]{2,1,0:T(8,128)S(1)} %copy.142, f32[8,16,64,512]{3,2,1,0:T(8,128)} %get-tuple-element.87, f32[8,16,64]{2,1,0:T(8,128)S(1)} %get-tuple-element.86, bf16[8,64,16,128]{3,2,1,0:T(8,128)(2,1)} %bitcast.150), kind=kOutput, calls=%fused_computation.9 | convolution fusion | flops 1090519040 | bytes 44105728 | tf_op jit(solution)/shard_map/nqhd,nkhd->nhqk/dot_general | solution.py:99
  530.5 11.1 %copy.150 = bf16[8,192,2048]{2,1,0:T(8,128)(2,1)} copy(bf16[8,192,2048]{1,2,0:T(8,128)(2,1)} %slice.283) | data formatting | bytes 12582912
  541.6 15.3 %broadcast_multiply_fusion = f32[8,16,512,128]{2,3,1,0:T(8,128)} fusion(bf16[8,16,64,512]{3,2,1,0:T(8,128)(2,1)} %fusion.4, bf16[8,64,16,128]{3,2,1,0:T(8,128)(2,1)S(1)} %bitcast.144), kind=kOutput, calls=%fused_computation.14 | convolution fusion | flops 1082130432 | bytes 44040192 | tf_op jit(solution)/shard_map/nhqk,nqhd->nkhd/dot_general | solution.py:105
  566.7 11.0 %copy.149 = bf16[8,192,2048]{2,1,0:T(8,128)(2,1)} copy(bf16[8,192,2048]{1,2,0:T(8,128)(2,1)} %slice.282) | data formatting | bytes 12582912
  577.8 10.5 %pad_maximum_fusion.1 = bf16[24,64,4096]{2,1,0:T(8,128)(2,1)} fusion(bf16[24,64,2048]{2,1,0:T(8,128)(2,1)} %bitcast.141, bf16[24,64,2048]{2,1,0:T(8,128)(2,1)} %bitcast.142), kind=kLoop, calls=%fused_computation.17 | loop fusion | flops 25165824 | bytes 25165824 | tf_op jit(solution)/shard_map/concatenate | solution.py:135
  594.2 31.9 %scatter_fusion = bf16[32,64,4096]{2,1,0:T(8,128)(2,1)} fusion(bf16[32,64,4096]{2,1,0:T(8,128)(2,1)} %broadcast_in_dim.91, s32[24]{0:T(128)S(1)} %copy-done.6, bf16[24,64,4096]{2,1,0:T(8,128)(2,1)} %pad_maximum_fusion.1), kind=kCustom, calls=%fused_computation.2 | custom fusion | bytes 37748832 | tf_op jit(solution)/shard_map/scatter | solution.py:137
  632.8 11.3 %slice.269 = f32[8,192,2048]{1,2,0:T(8,128)} slice(f32[8,512,2048]{1,2,0:T(8,128)} %bitcast.139), slice={[0:8], [0:192], [0:2048]} | slice | bytes 25165824 | tf_op jit(solution)/shard_map/slice | solution.py:110
  644.1 11.3 %slice.268 = f32[8,192,2048]{1,2,0:T(8,128)} slice(f32[8,512,2048]{1,2,0:T(8,128)} %bitcast.130), slice={[0:8], [0:192], [0:2048]} | slice | bytes 25165824 | tf_op jit(solution)/shard_map/slice | solution.py:110
  655.4 15.9 %copy.148 = f32[8,192,2048]{2,1,0:T(8,128)} copy(f32[8,192,2048]{1,2,0:T(8,128)} %slice.269) | data formatting | bytes 25165824
  671.3 15.9 %copy.147 = f32[8,192,2048]{2,1,0:T(8,128)} copy(f32[8,192,2048]{1,2,0:T(8,128)} %slice.268) | data formatting | bytes 25165824
  687.2 17.4 %pad_maximum_fusion = f32[8,192,4096]{2,1,0:T(8,128)} fusion(f32[8,192,2048]{2,1,0:T(8,128)} %copy.148, f32[8,192,2048]{2,1,0:T(8,128)} %copy.147), kind=kLoop, calls=%fused_computation.4 | loop fusion | flops 6291456 | bytes 50331648 | tf_op jit(solution)/shard_map/concatenate | solution.py:110
  713.7 11.1 %fusion.12 = f32[10,64,4096]{2,1,0:T(8,128)} fusion(f32[10,64,4096]{2,1,0:T(8,128)} %scatter-add.20, f32[8,3,64,4096]{3,2,1,0:T(8,128)} %bitcast.135), kind=kLoop, calls=%fused_computation.26 | loop fusion | flops 2097152 | bytes 25165824 | tf_op jit(solution)/shard_map/scatter-add | solution.py:118
  724.8 11.2 %fusion.10 = f32[8,64,4096]{2,1,0:T(8,128)} fusion(f32[8,3,64,4096]{3,2,1,0:T(8,128)} %bitcast.136, f32[10,64,4096]{2,1,0:T(8,128)} %fusion.12), kind=kLoop, calls=%fused_computation.23 | loop fusion | flops 2097152 | bytes 25165824 | tf_op jit(solution)/shard_map/add | solution.py:120
  761.2 11.5 %fusion.19 = bf16[8,64,16,128]{3,1,2,0:T(8,128)(2,1)S(1)} fusion(bf16[8,512,16,128]{1,3,2,0:T(8,128)(2,1)} %bitcast.133, bf16[8,16,64,512]{3,2,1,0:T(8,128)(2,1)} %fusion.4), kind=kOutput, calls=%fused_computation.39 | convolution fusion | flops 1075838976 | bytes 27262976 | tf_op jit(solution)/shard_map/nhqk,nkhd->nqhd/dot_general | solution.py:102
  798.4 57.4 %collective-permute-done.3 = bf16[64,4096]{1,0:T(8,128)(2,1)} collective-permute-done((bf16[64,4096]{1,0:T(8,128)(2,1)S(1)}, bf16[64,4096]{1,0:T(8,128)(2,1)}, u32[]{:S(2)}, u32[]{:S(2)}) %collective-permute-start.3) | collective-permute-done | bytes 524320 | tf_op jit(solution)/shard_map/ppermute | solution.py:24
  855.8 19.1 %collective-permute-done.2 = bf16[64,4096]{1,0:T(8,128)(2,1)} collective-permute-done((bf16[64,4096]{1,0:T(8,128)(2,1)S(1)}, bf16[64,4096]{1,0:T(8,128)(2,1)}, u32[]{:S(2)}, u32[]{:S(2)}) %collective-permute-start.2) | collective-permute-done | bytes 524320 | tf_op jit(solution)/shard_map/ppermute | solution.py:21
  878.6 11.5 %copy.125 = f32[8,64,4096]{2,0,1:T(8,128)} copy(f32[8,64,4096]{2,1,0:T(8,128)} %fusion.28) | data formatting | bytes 16777216 | tf_op jit(solution)/shard_map/scatter-add | solution.py:125
  892.7 20.2 %scatter-add.26 = f32[8,64,4096]{2,0,1:T(8,128)} dynamic-update-slice(f32[8,64,4096]{2,0,1:T(8,128)} %copy.125, f32[1,64,4096]{2,0,1:T(1,128)S(1)} %copy_add_fusion, s32[]{:T(128)} %constant.237.clone.1, s32[]{:T(128)} %constant.232.clone.1, s32[]{:T(128)} %constant.232.clone.1) | dynamic-update-slice | bytes 2097156 | tf_op jit(solution)/shard_map/scatter-add | solution.py:125
  912.9 28.4 %all-reduce.6.cloned.1.call-done = bf16[2,64,4096]{2,0,1:T(2,128)(2,1)} async-done(((bf16[2,64,4096]{2,0,1:T(2,128)(2,1)}), bf16[2,64,4096]{2,0,1:T(2,128)(2,1)}) %all-reduce.6.cloned.1.call-update) | async-done | bytes 1048592 | tf_op jit(solution)/shard_map/psum | solution.py:133
  947.6 29.2 %add_convert_fusion = bf16[8,64,4096]{2,0,1:T(8,128)(2,1)S(1)} fusion(f32[8,64,4096]{2,0,1:T(8,128)} %fusion.20, s32[32]{0:T(128)S(1)} %copy-done.8, pred[32]{0:T(512)(128)(4,1)S(1)} %copy-done.4, bf16[4,8,64,4096]{3,2,1,0:T(8,128)(2,1)} %bitcast.58), kind=kOutput, calls=%fused_computation.28 | convolution fusion | flops 138412544 | bytes 29360288 | tf_op jit(solution)/shard_map/dot_general | solution.py:142
  (98 shorter events, 180.2 us)
Async XLA Ops:
  8.5 15.9 %copy-start.3 = (pred[32]{0:T(512)(128)(4,1)}, pred[32]{0:T(512)(128)(4,1)S(1)}, u32[]{:S(2)}) copy-start(pred[32]{0:T(512)(128)(4,1)S(1)} %get-tuple-element.76) | copy-start | bytes 100
  8.7 15.8 %copy-start.7 = (s32[32]{0:T(128)}, s32[32]{0:T(128)S(1)}, u32[]{:S(2)}) copy-start(s32[32]{0:T(128)S(1)} %select_reduce_fusion) | copy-start | bytes 388
  38.7 19.5 %copy-start.1 = (bf16[512,2048]{1,0:T(8,128)(2,1)S(1)}, bf16[512,2048]{1,0:T(8,128)(2,1)}, u32[]{:S(2)}) copy-start(bf16[512,2048]{1,0:T(8,128)(2,1)} %param.20) | copy-start | bytes 6291460
  38.7 297.5 %all-to-all-start = ((bf16[32,64,4096]{2,1,0:T(8,128)(2,1)}), bf16[32,64,4096]{2,1,0:T(8,128)(2,1)}, u32[]{:S(2)}, u32[]{:S(2)}) async-start(bf16[32,64,4096]{2,1,0:T(8,128)(2,1)} %select_select_fusion), calls=%async_computation | async-start | bytes 33554432 | tf_op jit(solution)/shard_map/all_to_all | solution.py:62
  47.4 283.3 %all-reduce.4.cloned.1.call-start = ((), (), s32[]{:S(2)}) async-start(), calls=%async_computation.2 | async-start | bytes 2097152 | tf_op jit(solution)/shard_map/psum | solution.py:31
  51.1 229.7 %collective-permute-start.1 = (bf16[64,4096]{1,0:T(8,128)(2,1)S(1)}, bf16[64,4096]{1,0:T(8,128)(2,1)}, u32[]{:S(2)}, u32[]{:S(2)}) collective-permute-start(bf16[64,4096]{1,0:T(8,128)(2,1)S(1)} %get-tuple-element.84), channel_id=1, source_target_pairs={{1,0},{2,1},{3,2},{4,3},{5,4},{6,5},{7,6},{8,7},{9,8},{10,9},{11,1... | collective-permute-start | bytes 1572872 | tf_op jit(solution)/shard_map/ppermute | solution.py:24
  55.4 231.2 %collective-permute-start = (bf16[64,4096]{1,0:T(8,128)(2,1)S(1)}, bf16[64,4096]{1,0:T(8,128)(2,1)}, u32[]{:S(2)}, u32[]{:S(2)}) collective-permute-start(bf16[64,4096]{1,0:T(8,128)(2,1)S(1)} %get-tuple-element.85), channel_id=1, source_target_pairs={{0,1},{1,2},{2,3},{3,4},{4,5},{5,6},{6,7},{7,8},{8,9},{9,10},{10,1... | collective-permute-start | bytes 1572872 | tf_op jit(solution)/shard_map/ppermute | solution.py:21
  62.5 230.2 %copy-start.5 = (s32[24]{0:T(128)}, s32[24]{0:T(128)S(1)}, u32[]{:S(2)}) copy-start(s32[24]{0:T(128)S(1)} %fusion.53) | copy-start | bytes 292
  459.2 20.9 %copy-start = (bf16[64,8,16,128]{3,2,1,0:T(8,128)(2,1)S(1)}, bf16[64,8,16,128]{3,2,1,0:T(8,128)(2,1)}, u32[]{:S(2)}) copy-start(bf16[64,8,16,128]{3,2,1,0:T(8,128)(2,1)} %copy.154) | copy-start | bytes 6291460
  588.2 6.0 copy-start.6
  626.1 321.6 %all-to-all-start.1 = ((bf16[32,64,4096]{2,1,0:T(8,128)(2,1)}), bf16[32,64,4096]{2,1,0:T(8,128)(2,1)}, u32[]{:S(2)}, u32[]{:S(2)}) async-start(bf16[32,64,4096]{2,1,0:T(8,128)(2,1)} %scatter_fusion), calls=%async_computation.1 | async-start | bytes 33554432 | tf_op jit(solution)/shard_map/all_to_all | solution.py:138
  632.8 308.5 %all-reduce.6.cloned.1.call-start = ((), (), s32[]{:S(2)}) async-start(), calls=%async_computation.3 | async-start | bytes 2097152 | tf_op jit(solution)/shard_map/psum | solution.py:133
  745.0 110.9 %collective-permute-start.3 = (bf16[64,4096]{1,0:T(8,128)(2,1)S(1)}, bf16[64,4096]{1,0:T(8,128)(2,1)}, u32[]{:S(2)}, u32[]{:S(2)}) collective-permute-start(bf16[64,4096]{1,0:T(8,128)(2,1)S(1)} %fusion.30), channel_id=1, source_target_pairs={{1,0},{2,1},{3,2},{4,3},{5,4},{6,5},{7,6},{8,7},{9,8},{10,9},{11,1... | collective-permute-start | bytes 1572872 | tf_op jit(solution)/shard_map/ppermute | solution.py:24
  750.5 124.3 %collective-permute-start.2 = (bf16[64,4096]{1,0:T(8,128)(2,1)S(1)}, bf16[64,4096]{1,0:T(8,128)(2,1)}, u32[]{:S(2)}, u32[]{:S(2)}) collective-permute-start(bf16[64,4096]{1,0:T(8,128)(2,1)S(1)} %fusion.29), channel_id=1, source_target_pairs={{0,1},{1,2},{2,3},{3,4},{4,5},{5,6},{6,7},{7,8},{8,9},{9,10},{10,1... | collective-permute-start | bytes 1572872 | tf_op jit(solution)/shard_map/ppermute | solution.py:21
  781.3 11.0 %copy-start.2 = (bf16[8,16,128,64]{2,3,1,0:T(8,128)(2,1)S(1)}, bf16[8,16,128,64]{2,3,1,0:T(8,128)(2,1)}, u32[]{:S(2)}) copy-start(bf16[8,16,128,64]{2,3,1,0:T(8,128)(2,1)} %get-tuple-element.89) | copy-start | bytes 6291460
  890.1 57.5 %copy-start.4 = (pred[32]{0:T(512)(128)(4,1)S(1)}, pred[32]{0:T(512)(128)(4,1)}, u32[]{:S(2)}) copy-start(pred[32]{0:T(512)(128)(4,1)} %copy-done.3) | copy-start | bytes 100
  890.1 57.5 %copy-start.8 = (s32[32]{0:T(128)S(1)}, s32[32]{0:T(128)}, u32[]{:S(2)}) copy-start(s32[32]{0:T(128)} %copy-done.7) | copy-start | bytes 388
Sparse Core Ops, SparseCore 0:
  52.1 278.6 all-reduce.3
  798.5 142.6 all-reduce.5
where the time goes:
time: 999 us; the launch traced here: 989 us
  waiting for transfers between devices  360 us (36%)
  local copies, waits for them, and re-layouts  324 us (32%)
  other arithmetic  135 us (14%)
  matrix products  127 us (13%)
  starting transfers between devices  28.1 us (3%)
  between operations  14.9 us (1%)
    ppermute x2, waiting for transfers between devices, extended(): lax.ppermute(lax.slice_in_dim(block, 0, width, axis=dim), axis, backward)  276 us
    unnamed x32, local copies, waits for them, and re-layouts  80.4 us
    slice x2, local copies, waits for them, and re-layouts, body(): all_key = listed[..., :width].reshape(nbd, span, heads, HD)  45.1 us
    scatter x1, local copies, waits for them, and re-layouts, body(): jnp.zeros((ndev * cap, BS, both), jnp.bfloat16).at[mine_slot].set(rand_grad)  31.9 us
    scatter-add x2, local copies, waits for them, and re-layouts, body(): own = own.at[0].add(arrived[:BS]).at[nbd - 1].add(arrived[3 * BS:])  31.6 us
    psum x1, waiting for transfers between devices, from_root(): return lax.psum(kept, axis)  31.2 us
    dot_general x1, matrix products, body(): jnp.dot(onehot, back.reshape(ndev * cap, BS * both), preferred_element_ty...  29.2 us
    psum x1, waiting for transfers between devices, body(): lax.psum(glob_grad.astype(jnp.bfloat16), ('head', 'blk'))  28.4 us
  transfers between devices with their start and end apart: 8, of which 6 were waited for; matrix products, arithmetic and copies ran while one was open for 23% of the time, Pallas kernels for 0%

commit v1 on v0

v1 whole, which is shorter than its diff:
```python
import math

import jax
import jax.numpy as jnp
from jax import lax
from jax.experimental import pallas as pl
from jax.experimental.pallas import tpu as pltpu
from jax.sharding import PartitionSpec as P

HD = 128
BS = 64
R = 3


NEG = -1e30
INTERPRET = False


def extended(block, sides, width):
    for axis, dim in sides:
        count = lax.axis_size(axis)
        forward = [(i, i + 1) for i in range(count - 1)]
        backward = [(target, source) for source, target in forward]
        low = lax.ppermute(
            lax.slice_in_dim(block, block.shape[dim] - width, None, axis=dim), axis, forward
        )
        high = lax.ppermute(lax.slice_in_dim(block, 0, width, axis=dim), axis, backward)
        block = jnp.concatenate([low, block, high], axis=dim)
    return block


def from_root(value, axis, source):
    kept = jnp.where(lax.axis_index(axis) == source, value, 0).astype(value.dtype)
    return lax.psum(kept, axis)


def attention_kernel(
    slots_ref, q_ref, do_ref, mask_ref,
    kw0, kw1, kw2, vw0, vw1, vw2, kg, vg, kr0, kr1, kr2, vr0, vr1, vr2,
    out_ref, dq_ref, wk_ref, wv_ref, gk_ref, gv_ref, rk_ref, rv_ref,
):
    pf = jnp.float32
    scale = 1.0 / math.sqrt(HD)
    q = q_ref[...]
    do = do_ref[...]
    k = jnp.concatenate([kw0[...], kw1[...], kw2[...], kg[...], kr0[0], kr1[0], kr2[0]], axis=0)
    v = jnp.concatenate([vw0[...], vw1[...], vw2[...], vg[...], vr0[0], vr1[0], vr2[0]], axis=0)
    nt = (((1,), (1,)), ((), ()))
    s = lax.dot_general(q, k, nt, preferred_element_type=pf) * scale
    s = jnp.where(mask_ref[0] > 0, s, NEG)
    top = jnp.max(s, axis=1, keepdims=True)
    e = jnp.exp(s - top)
    p = e / jnp.sum(e, axis=1, keepdims=True)
    pb = p.astype(jnp.bfloat16)
    ob = jnp.dot(pb, v, preferred_element_type=pf).astype(jnp.bfloat16)
    out_ref[...] = ob
    delta = jnp.sum(do.astype(pf) * ob.astype(pf), axis=1, keepdims=True)
    dp = lax.dot_general(do, v, nt, preferred_element_type=pf)
    ds = p * (dp - delta)
    dsb = ds.astype(jnp.bfloat16)
    dq_ref[...] = (jnp.dot(dsb, k, preferred_element_type=pf) * scale).astype(jnp.bfloat16)
    kt = jnp.dot(ds.T.astype(jnp.bfloat16), q, preferred_element_type=pf) * scale
    vt = jnp.dot(p.T.astype(jnp.bfloat16), do, preferred_element_type=pf)
    w = 3 * BS
    g = 5 * BS
    wk_ref[0] = kt[:w]
    wv_ref[0] = vt[:w]
    gk_ref[0] = kt[w:g]
    gv_ref[0] = vt[w:g]
    rk_ref[0] = kt[g:].astype(jnp.bfloat16)
    rv_ref[0] = vt[g:].astype(jnp.bfloat16)


def attention(query, dout, mask, padded, glob, fetched, slots):
    rows, width = query.shape
    heads = width // HD
    nbd = rows // BS
    span = (5 + R) * BS

    def tile(j, col):
        return pl.BlockSpec((BS, HD), lambda n, h, s: (n + j, h + col))

    def rand_tile(j, col):
        return pl.BlockSpec((1, BS, HD), lambda n, h, s: (s[n * R + j], 0, h + col))

    row_spec = pl.BlockSpec((BS, HD), lambda n, h, s: (n, h))
    in_specs = (
        [row_spec, row_spec, pl.BlockSpec((1, 1, span), lambda n, h, s: (n, 0, 0))]
        + [tile(j, 0) for j in range(3)]
        + [tile(j, heads) for j in range(3)]
        + [
            pl.BlockSpec((2 * BS, HD), lambda n, h, s: (0, h)),
            pl.BlockSpec((2 * BS, HD), lambda n, h, s: (0, h + heads)),
        ]
        + [rand_tile(j, 0) for j in range(R)]
        + [rand_tile(j, heads) for j in range(R)]
    )

    def term_spec(size):
        return pl.BlockSpec((1, size, HD), lambda n, h, s: (n, 0, h))

    out_specs = [
        row_spec,
        row_spec,
        term_spec(3 * BS),
        term_spec(3 * BS),
        term_spec(2 * BS),
        term_spec(2 * BS),
        term_spec(R * BS),
        term_spec(R * BS),
    ]
    out_shape = [
        jax.ShapeDtypeStruct((rows, width), jnp.bfloat16),
        jax.ShapeDtypeStruct((rows, width), jnp.bfloat16),
        jax.ShapeDtypeStruct((nbd, 3 * BS, width), jnp.float32),
        jax.ShapeDtypeStruct((nbd, 3 * BS, width), jnp.float32),
        jax.ShapeDtypeStruct((nbd, 2 * BS, width), jnp.float32),
        jax.ShapeDtypeStruct((nbd, 2 * BS, width), jnp.float32),
        jax.ShapeDtypeStruct((nbd, R * BS, width), jnp.bfloat16),
        jax.ShapeDtypeStruct((nbd, R * BS, width), jnp.bfloat16),
    ]
    grid_spec = pltpu.PrefetchScalarGridSpec(
        num_scalar_prefetch=1,
        grid=(nbd, heads),
        in_specs=in_specs,
        out_specs=out_specs,
    )
    args = [query, dout, mask] + [padded] * 6 + [glob] * 2 + [fetched] * (2 * R)
    return pl.pallas_call(
        attention_kernel,
        grid_spec=grid_spec,
        out_shape=out_shape,
        interpret=INTERPRET,
    )(slots, *args)


def overlap(terms, nbd):
    width = terms.shape[-1]
    w4 = terms.reshape(nbd, 3, BS, width)
    return (
        jnp.pad(w4[:, 0], ((0, 2), (0, 0), (0, 0)))
        + jnp.pad(w4[:, 1], ((1, 1), (0, 0), (0, 0)))
        + jnp.pad(w4[:, 2], ((2, 0), (0, 0), (0, 0)))
    )


def body(query, key, value, dout, rand):
    rows, width = query.shape
    ndev = lax.axis_size(("head", "blk"))
    me = lax.axis_index(("head", "blk"))
    nbd = rows // BS
    total = nbd * ndev
    cap = (R * nbd + ndev - 1) // ndev
    pf = jnp.float32
    span = (5 + R) * BS
    pair = jnp.concatenate([key, value], axis=1)
    padded = extended(pair, ((("head", "blk"), 0),), BS)
    glob = from_root(pair[: 2 * BS], ("head", "blk"), 0)
    flat = rand.reshape(ndev, nbd * R)
    owner = flat // nbd
    local = flat - owner * nbd
    hit = owner == me
    order = jnp.cumsum(hit.astype(jnp.int32), axis=1) - 1
    slot_ids = jnp.arange(cap, dtype=jnp.int32)
    chosen = hit[:, None, :] & (order[:, None, :] == slot_ids[None, :, None])
    block_id = jnp.sum(jnp.where(chosen, local[:, None, :], 0), axis=2).reshape(-1)
    filled = jnp.any(chosen, axis=2).reshape(-1)
    tiles = pair.reshape(nbd, BS, 2 * width)
    outgoing = jnp.where(
        filled[:, None, None], jnp.take(tiles, block_id, axis=0), jnp.zeros((), pair.dtype)
    )
    fetched = lax.all_to_all(outgoing, ("head", "blk"), split_axis=0, concat_axis=0, tiled=True)
    mine = lax.dynamic_slice_in_dim(rand, me * nbd, nbd, 0).reshape(-1)
    mine_owner = mine // nbd
    count = mine.shape[0]
    earlier = jnp.arange(count)[:, None] > jnp.arange(count)[None, :]
    same = mine_owner[:, None] == mine_owner[None, :]
    mine_rank = jnp.sum(earlier & same, axis=1)
    mine_slot = (mine_owner * cap + mine_rank).astype(jnp.int32)
    first = me * nbd + jnp.arange(nbd, dtype=jnp.int32)
    always = first >= 0
    valid = jnp.concatenate(
        [
            jnp.stack([first > 0, always, first < total - 1, always, always], axis=1),
            jnp.ones((nbd, R), bool),
        ],
        axis=1,
    )
    mask = jnp.repeat(valid, BS, axis=1).astype(pf).reshape(nbd, 1, span)
    out, dq, wk, wv, gk, gv, rk, rv = attention(query, dout, mask, padded, glob, fetched, mine_slot)
    sk = overlap(wk, nbd)
    sv = overlap(wv, nbd)
    rims = jnp.concatenate(
        [
            jnp.concatenate([sk[0], sv[0]], axis=-1),
            jnp.concatenate([sk[nbd + 1], sv[nbd + 1]], axis=-1),
        ],
        axis=0,
    )
    arrived = extended(rims.astype(jnp.bfloat16), ((("head", "blk"), 0),), BS).astype(pf)
    own = jnp.concatenate([sk[1 : nbd + 1], sv[1 : nbd + 1]], axis=-1)
    own = own.at[0].add(arrived[:BS]).at[nbd - 1].add(arrived[3 * BS :])
    glob_grad = jnp.concatenate([jnp.sum(gk, axis=0), jnp.sum(gv, axis=0)], axis=-1).reshape(
        2, BS, 2 * width
    )
    glob_total = lax.psum(glob_grad.astype(jnp.bfloat16), ("head", "blk")).astype(pf)
    own = own.at[:2].add(jnp.where(me == 0, glob_total, 0.0))
    rand_grad = jnp.concatenate([rk, rv], axis=-1).reshape(nbd * R, BS, 2 * width)
    returning = jnp.zeros((ndev * cap, BS, 2 * width), jnp.bfloat16).at[mine_slot].set(rand_grad)
    back = lax.all_to_all(returning, ("head", "blk"), split_axis=0, concat_axis=0, tiled=True)
    onehot = (
        (block_id[None, :] == jnp.arange(nbd, dtype=jnp.int32)[:, None]) & filled[None, :]
    ).astype(jnp.bfloat16)
    own = own + jnp.dot(
        onehot, back.reshape(ndev * cap, BS * 2 * width), preferred_element_type=pf
    ).reshape(nbd, BS, 2 * width)
    dk = own[..., :width].astype(jnp.bfloat16).reshape(rows, width)
    dv = own[..., width:].astype(jnp.bfloat16).reshape(rows, width)
    return (out, dq, dk, dv)


def solution(mesh):
    placed = (
        P(("dp", "head", "blk"), None),
        P(("dp", "head", "blk"), None),
        P(("dp", "head", "blk"), None),
        P(("dp", "head", "blk"), None),
        P("dp", None),
    )
    return jax.shard_map(
        body,
        mesh=mesh,
        in_specs=placed,
        out_specs=(
            P(("dp", "head", "blk"), None),
            P(("dp", "head", "blk"), None),
            P(("dp", "head", "blk"), None),
            P(("dp", "head", "blk"), None),
        ),
        check_vma=False,
    )
```

time: 999 us -> 882 us (0.88)
  local copies, waits for them, and re-layouts: 324 us -> 118 us
  Pallas kernels: 0 us -> 150 us
  waiting for transfers between devices: 360 us -> 460 us
  matrix products: 127 us -> 29.1 us
  other arithmetic: 135 us -> 70.9 us
    pallas_call x0 -> x1, Pallas kernels: none -> 150 us  [attention(): pl.pallas_call(attention_kernel, grid_spec=grid_spec, out_shape=out_shape...]
    ppermute x2, waiting for transfers between devices: 276 us -> 392 us  [extended(): lax.ppermute(lax.slice_in_dim(block, 0, width, axis=dim), axis, backward)]
    slice x9 -> x3, local copies, waits for them, and re-layouts: 118 us -> 6.25 us  [the longest x2 4.98 us: body(): own = jnp.concatenate([sk[1:nbd + 1], sv[1:nbd + 1]], axis=-1)]
    dot_general x7 -> x1, matrix products: 127 us -> 29.1 us  [body(): jnp.dot(onehot, back.reshape(ndev * cap, BS * 2 * width), preferred_eleme...]
    unnamed x32 -> x12, local copies, waits for them, and re-layouts: 80.4 us -> 4.81 us
    concatenate x4 -> x5, other arithmetic: 39.5 us -> 16.4 us  [the longest x1 10.5 us: body(): jnp.concatenate([rk, rv], axis=-1).reshape(nbd * R, BS, 2 * width)]
    sub x1 -> x0, other arithmetic: 19.2 us -> none  [body(): expo = jnp.exp(scores - top)]
    squeeze x2 -> x4, local copies, waits for them, and re-layouts: 2.56 us -> 21.6 us  [the longest x2 19.5 us: overlap(): w4[:, 0]]
  transfers between devices with their start and end apart: 8 -> 8, of which waited for: 6 -> 6; matrix products, arithmetic and copies ran while one was open for 23% -> 12% of each run, Pallas kernels for 0% -> 0%
where the time goes in v1:
time: 882 us; the launch traced here: 871 us
  waiting for transfers between devices  460 us (52%)
  Pallas kernels  150 us (17%)
  local copies, waits for them, and re-layouts  118 us (13%)
  other arithmetic  70.9 us (8%)
  matrix products  29.1 us (3%)
  starting transfers between devices  27.9 us (3%)
  between operations  14.8 us (2%)
    ppermute x2, waiting for transfers between devices, extended(): lax.ppermute(lax.slice_in_dim(block, 0, width, axis=dim), axis, backward)  392 us
    pallas_call x1, Pallas kernels, attention(): pl.pallas_call(attention_kernel, grid_spec=grid_spec, out_shape=out_shape...  150 us
    psum x1, waiting for transfers between devices, from_root(): return lax.psum(kept, axis)  34.7 us
    scatter x1, local copies, waits for them, and re-layouts, body(): jnp.zeros((ndev * cap, BS, 2 * width), jnp.bfloat16).at[mine_slot]  31.7 us
    dot_general x1, matrix products, body(): jnp.dot(onehot, back.reshape(ndev * cap, BS * 2 * width), preferred_eleme...  29.1 us
    scatter-add x2, local copies, waits for them, and re-layouts, body(): own = own.at[0].add(arrived[:BS]).at[nbd - 1].add(arrived[3 * BS:])  28.3 us
    squeeze x2, local copies, waits for them, and re-layouts, overlap(): w4[:, 0]  19.5 us
    psum x1, waiting for transfers between devices, body(): lax.psum(glob_grad.astype(jnp.bfloat16), ('head', 'blk')).astype(pf)  19.1 us
  transfers between devices with their start and end apart: 8, of which 6 were waited for; matrix products, arithmetic and copies ran while one was open for 12% of the time, Pallas kernels for 0%

profile of v1, /device:TPU:14, one launch (start us, length us, event | category | flops | bytes accessed | tf_op | source)
XLA Modules:
  0.0 870.7 jit_solution(13936723225825148218)
XLA Ops:
  9.3 3.3 constant_dynamic-update-slice_fusion.1
  14.3 9.4 %gather_fusion = bf16[32,64,4096]{2,1,0:T(8,128)(2,1)} fusion(bf16[8,64,4096]{2,1,0:T(8,128)(2,1)} %bitcast.1, s32[1024]{0:T(1024)S(1)} %pad_clamp_fusion), kind=kCustom, calls=%fused_computation | custom fusion | bytes 33554560 | tf_op jit(solution)/shard_map/jit(_take)/gather | solution.py:170
  23.7 14.3 %select_select_fusion = bf16[32,64,4096]{2,1,0:T(8,128)(2,1)} fusion(bf16[32,64,4096]{2,1,0:T(8,128)(2,1)} %gather_fusion, pred[32]{0:T(512)(128)(4,1)S(1)} %compare_and_fusion, pred[32]{0:T(512)(128)(4,1)S(1)} %get-tuple-element.60), kind=kLoop, calls=%fused_computation.5 | loop fusion | flops 16777216 | bytes 33554496 | tf_op jit(solution)/shard_map/jit(_where)/select_n | solution.py:169
  38.0 8.6 all-to-all-start
  47.9 4.3 collective-permute-start.1
  58.5 221.5 %collective-permute-done.1 = bf16[64,4096]{1,0:T(8,128)(2,1)S(1)} collective-permute-done((bf16[64,4096]{1,0:T(8,128)(2,1)S(1)}, bf16[64,4096]{1,0:T(8,128)(2,1)S(1)}, u32[]{:S(2)}, u32[]{:S(2)}) %collective-permute-start.1) | collective-permute-done | bytes 524320 | tf_op jit(solution)/shard_map/ppermute | solution.py:27
  280.0 6.5 collective-permute-done
  286.5 5.7 pad_maximum_fusion.2.kw0.kw1.kw2.vw0.vw1.vw2
  292.2 34.7 %all-reduce.9.cloned.1.call-done.kg.vg = bf16[128,4096]{1,0:T(8,128)(2,1)} async-done(((bf16[128,4096]{1,0:T(8,128)(2,1)}), bf16[128,4096]{1,0:T(8,128)(2,1)}) %all-reduce.9.cloned.1.call-update) | async-done | bytes 1048592 | tf_op jit(solution)/shard_map/psum | solution.py:34
  326.8 149.7 %shard_map.84 = (bf16[512,2048]{1,0:T(8,128)(2,1)}, bf16[512,2048]{1,0:T(8,128)(2,1)}, f32[8,192,2048]{2,1,0:T(8,128)}, f32[8,192,2048]{2,1,0:T(8,128)}, f32[8,1...) custom-call(s32[24]{0:T(128)} %fusion.36.slots_ref, ...), custom_call_target="tpu_custom_call" | custom-call | tf_op jit(solution)/shard_map/pallas_call | solution.py:129
  476.6 10.5 %pad_maximum_fusion = bf16[8,192,4096]{2,1,0:T(8,128)(2,1)} fusion(bf16[8,192,2048]{2,1,0:T(8,128)(2,1)} %get-tuple-element.55, bf16[8,192,2048]{2,1,0:T(8,128)(2,1)} %get-tuple-element.54), kind=kLoop, calls=%fused_computation.6 | loop fusion | flops 25165824 | bytes 25165824 | tf_op jit(solution)/shard_map/concatenate | solution.py:208
  487.1 5.9 broadcast_in_dim.50
  493.1 31.7 %scatter_fusion = bf16[32,64,4096]{2,1,0:T(8,128)(2,1)} fusion(bf16[32,64,4096]{2,1,0:T(8,128)(2,1)} %broadcast_in_dim.50, s32[24]{0:T(128)S(1)} %fusion.29, bf16[24,64,4096]{2,1,0:T(8,128)(2,1)} %bitcast.74), kind=kCustom, calls=%fused_computation.1 | custom fusion | bytes 37748832 | tf_op jit(solution)/shard_map/scatter | solution.py:209
  524.8 6.6 all-to-all-start.1
  531.5 9.8 %slice_bitcast_fusion.2 = (f32[8,64,2048]{2,1,0:T(8,128)S(1)}, f32[8,64,2048]{2,1,0:T(8,128)}, f32[8,64,2048]{2,1,0:T(8,128)}) fusion(f32[8,3,64,2048]{3,2,1,0:T(8,128)} %bitcast.76), kind=kLoop, calls=%fused_computation.16 | loop fusion | bytes 25165824 | tf_op jit(solution)/shard_map/squeeze | solution.py:141
  541.2 6.7 fusion.31
  550.3 9.7 %slice_bitcast_fusion.5 = (f32[8,64,2048]{2,1,0:T(8,128)S(1)}, f32[8,64,2048]{2,1,0:T(8,128)}, f32[8,64,2048]{2,1,0:T(8,128)}) fusion(f32[8,3,64,2048]{3,2,1,0:T(8,128)} %bitcast.75), kind=kLoop, calls=%fused_computation.19 | loop fusion | bytes 25165824 | tf_op jit(solution)/shard_map/squeeze | solution.py:141
  560.0 6.6 fusion.30
  566.6 2.5 slice.163
  572.2 4.3 collective-permute-start.3
  579.4 4.2 reduce_sum.44
  583.6 4.2 reduce_sum.43
  590.0 4.1 pad_maximum_fusion.1
  594.2 170.6 %collective-permute-done.3 = bf16[64,4096]{1,0:T(8,128)(2,1)S(1)} collective-permute-done((bf16[64,4096]{1,0:T(8,128)(2,1)}, bf16[64,4096]{1,0:T(8,128)(2,1)S(1)}, u32[]{:S(2)}, u32[]{:S(2)}) %collective-permute-start.3) | collective-permute-done | bytes 524320 | tf_op jit(solution)/shard_map/ppermute | solution.py:27
  764.8 7.5 collective-permute-done.2
  773.6 8.1 copy.47
  783.4 20.2 %scatter-add.11 = f32[8,64,4096]{2,0,1:T(8,128)} dynamic-update-slice(f32[8,64,4096]{2,0,1:T(8,128)} %copy.47, f32[1,64,4096]{2,0,1:T(1,128)S(1)} %copy_add_fusion, s32[]{:T(128)} %constant.143.clone.1, s32[]{:T(128)} %constant.140.clone.1, s32[]{:T(128)} %constant.140.clone.1) | dynamic-update-slice | bytes 2097156 | tf_op jit(solution)/shard_map/scatter-add | solution.py:202
  803.6 19.1 %all-reduce.11.cloned.1.call-done = bf16[2,64,4096]{2,0,1:T(2,128)(2,1)} async-done(((bf16[2,64,4096]{2,0,1:T(2,128)(2,1)}), bf16[2,64,4096]{2,0,1:T(2,128)(2,1)}) %all-reduce.11.cloned.1.call-update) | async-done | bytes 1048592 | tf_op jit(solution)/shard_map/psum | solution.py:206
  822.7 6.4 fusion.5
  829.1 29.1 %add_convert_fusion = bf16[8,64,4096]{2,0,1:T(8,128)(2,1)S(1)} fusion(f32[8,64,4096]{2,0,1:T(8,128)} %fusion.5, s32[32]{0:T(128)S(1)} %copy-done.4, pred[32]{0:T(512)(128)(4,1)S(1)} %get-tuple-element.60, bf16[4,8,64,4096]{3,2,1,0:T(8,128)(2,1)} %bitcast.39), kind=kOutput, calls=%fused_computation.10 | convolution fusion | flops 138412544 | bytes 29360288 | tf_op jit(solution)/shard_map/dot_general | solution.py:214
  858.5 2.5 copy.51
  861.0 2.5 copy.52
  (58 shorter events, 25.0 us)
Async XLA Ops:
  7.2 5.5 copy-start.1
  8.8 0.5 copy-start.3
  38.0 288.8 %all-to-all-start = ((bf16[32,64,4096]{2,1,0:T(8,128)(2,1)}), bf16[32,64,4096]{2,1,0:T(8,128)(2,1)}, u32[]{:S(2)}, u32[]{:S(2)}) async-start(bf16[32,64,4096]{2,1,0:T(8,128)(2,1)} %select_select_fusion), calls=%async_computation | async-start | bytes 33554432 | tf_op jit(solution)/shard_map/all_to_all | solution.py:172
  46.6 9.9 %copy-start.2 = (s32[256,3]{0,1:T(4,128)S(1)}, s32[256,3]{0,1:T(4,128)}, u32[]{:S(2)}) copy-start(s32[256,3]{0,1:T(4,128)} %param.15) | copy-start | bytes 9220
  46.6 280.2 %all-reduce.9.cloned.1.call-start = ((), (), s32[]{:S(2)}) async-start(), calls=%async_computation.2 | async-start | bytes 2097152 | tf_op jit(solution)/shard_map/psum | solution.py:34
  47.9 232.1 %collective-permute-start.1 = (bf16[64,4096]{1,0:T(8,128)(2,1)S(1)}, bf16[64,4096]{1,0:T(8,128)(2,1)S(1)}, u32[]{:S(2)}, u32[]{:S(2)}) collective-permute-start(bf16[64,4096]{1,0:T(8,128)(2,1)S(1)} %get-tuple-element.71), channel_id=1, source_target_pairs={{1,0},{2,1},{3,2},{4,3},{5,4},{6,5},{7,6},{8,7},{9,8},{10,9},{11,1... | collective-permute-start | bytes 1572872 | tf_op jit(solution)/shard_map/ppermute | solution.py:27
  52.2 234.3 %collective-permute-start = (bf16[64,4096]{1,0:T(8,128)(2,1)S(1)}, bf16[64,4096]{1,0:T(8,128)(2,1)S(1)}, u32[]{:S(2)}, u32[]{:S(2)}) collective-permute-start(bf16[64,4096]{1,0:T(8,128)(2,1)S(1)} %get-tuple-element.70), channel_id=1, source_target_pairs={{0,1},{1,2},{2,3},{3,4},{4,5},{5,6},{6,7},{7,8},{8,9},{9,10},{10,1... | collective-permute-start | bytes 1572872 | tf_op jit(solution)/shard_map/ppermute | solution.py:24
  524.8 304.3 %all-to-all-start.1 = ((bf16[32,64,4096]{2,1,0:T(8,128)(2,1)}), bf16[32,64,4096]{2,1,0:T(8,128)(2,1)}, u32[]{:S(2)}, u32[]{:S(2)}) async-start(bf16[32,64,4096]{2,1,0:T(8,128)(2,1)} %scatter_fusion), calls=%async_computation.1 | async-start | bytes 33554432 | tf_op jit(solution)/shard_map/all_to_all | solution.py:210
  531.4 291.3 %all-reduce.11.cloned.1.call-start = ((), (), s32[]{:S(2)}) async-start(), calls=%async_computation.3 | async-start | bytes 2097152 | tf_op jit(solution)/shard_map/psum | solution.py:206
  572.2 192.6 %collective-permute-start.3 = (bf16[64,4096]{1,0:T(8,128)(2,1)}, bf16[64,4096]{1,0:T(8,128)(2,1)S(1)}, u32[]{:S(2)}, u32[]{:S(2)}) collective-permute-start(bf16[64,4096]{1,0:T(8,128)(2,1)} %pad_maximum_fusion.9), channel_id=1, source_target_pairs={{1,0},{2,1},{3,2},{4,3},{5,4},{6,5},{7,6},{8,7},{9,8},{10,9},{11,1... | collective-permute-start | bytes 1572872 | tf_op jit(solution)/shard_map/ppermute | solution.py:27
  577.3 195.0 %collective-permute-start.2 = (bf16[64,4096]{1,0:T(8,128)(2,1)}, bf16[64,4096]{1,0:T(8,128)(2,1)}, u32[]{:S(2)}, u32[]{:S(2)}) collective-permute-start(bf16[64,4096]{1,0:T(8,128)(2,1)} %pad_maximum_fusion.8), channel_id=1, source_target_pairs={{0,1},{1,2},{2,3},{3,4},{4,5},{5,6},{6,7},{7,8},{8,9},{9,10},{10,1... | collective-permute-start | bytes 1572872 | tf_op jit(solution)/shard_map/ppermute | solution.py:24
  590.0 182.3 %copy-start = (f32[8,64,2048]{2,1,0:T(8,128)S(1)}, f32[8,64,2048]{2,1,0:T(8,128)}, u32[]{:S(2)}) copy-start(f32[8,64,2048]{2,1,0:T(8,128)} %slice.167) | copy-start | bytes 12582916
  781.8 47.3 %copy-start.4 = (s32[32]{0:T(128)S(1)}, s32[32]{0:T(128)}, u32[]{:S(2)}) copy-start(s32[32]{0:T(128)} %copy-done.3) | copy-start | bytes 388
Sparse Core Ops, SparseCore 0:
  56.5 270.2 all-reduce.8
  590.1 232.4 all-reduce.10

commit v2 on v1

--- a/solution.py
+++ b/solution.py
@@ -34,10 +34,10 @@
     return lax.psum(kept, axis)
 
 
-def attention_kernel(
+def scores_kernel(
     slots_ref, q_ref, do_ref, mask_ref,
     kw0, kw1, kw2, vw0, vw1, vw2, kg, vg, kr0, kr1, kr2, vr0, vr1, vr2,
-    out_ref, dq_ref, wk_ref, wv_ref, gk_ref, gv_ref, rk_ref, rv_ref,
+    out_ref, dq_ref, rk_ref, rv_ref, pb_ref, dsb_ref,
 ):
     pf = jnp.float32
     scale = 1.0 / math.sqrt(HD)
@@ -46,6 +46,7 @@
     k = jnp.concatenate([kw0[...], kw1[...], kw2[...], kg[...], kr0[0], kr1[0], kr2[0]], axis=0)
     v = jnp.concatenate([vw0[...], vw1[...], vw2[...], vg[...], vr0[0], vr1[0], vr2[0]], axis=0)
     nt = (((1,), (1,)), ((), ()))
+    tn = (((0,), (0,)), ((), ()))
     s = lax.dot_general(q, k, nt, preferred_element_type=pf) * scale
     s = jnp.where(mask_ref[0] > 0, s, NEG)
     top = jnp.max(s, axis=1, keepdims=True)
@@ -59,16 +60,24 @@
     ds = p * (dp - delta)
     dsb = ds.astype(jnp.bfloat16)
     dq_ref[...] = (jnp.dot(dsb, k, preferred_element_type=pf) * scale).astype(jnp.bfloat16)
-    kt = jnp.dot(ds.T.astype(jnp.bfloat16), q, preferred_element_type=pf) * scale
-    vt = jnp.dot(p.T.astype(jnp.bfloat16), do, preferred_element_type=pf)
+    g = 5 * BS
+    rk_ref[0] = (lax.dot_general(dsb[:, g:], q, tn, preferred_element_type=pf) * scale).astype(jnp.bfloat16)
+    rv_ref[0] = lax.dot_general(pb[:, g:], do, tn, preferred_element_type=pf).astype(jnp.bfloat16)
+    pb_ref[0, 0] = pb[:, :g]
+    dsb_ref[0, 0] = dsb[:, :g]
+
+
+def terms_kernel(q_ref, do_ref, pb_ref, dsb_ref, wk_ref, wv_ref, gk_ref, gv_ref):
+    pf = jnp.float32
+    scale = 1.0 / math.sqrt(HD)
+    tn = (((0,), (0,)), ((), ()))
+    kt = lax.dot_general(dsb_ref[0, 0], q_ref[...], tn, preferred_element_type=pf) * scale
+    vt = lax.dot_general(pb_ref[0, 0], do_ref[...], tn, preferred_element_type=pf)
     w = 3 * BS
-    g = 5 * BS
     wk_ref[0] = kt[:w]
     wv_ref[0] = vt[:w]
-    gk_ref[0] = kt[w:g]
-    gv_ref[0] = vt[w:g]
-    rk_ref[0] = kt[g:].astype(jnp.bfloat16)
-    rv_ref[0] = vt[g:].astype(jnp.bfloat16)
+    gk_ref[0] = kt[w:]
+    gv_ref[0] = vt[w:]
 
 
 def attention(query, dout, mask, padded, glob, fetched, slots):
@@ -76,6 +85,7 @@
     heads = width // HD
     nbd = rows // BS
     span = (5 + R) * BS
+    g = 5 * BS
 
     def tile(j, col):
         return pl.BlockSpec((BS, HD), lambda n, h, s: (n + j, h + col))
@@ -95,29 +105,16 @@
         + [rand_tile(j, 0) for j in range(R)]
         + [rand_tile(j, heads) for j in range(R)]
     )
-
-    def term_spec(size):
-        return pl.BlockSpec((1, size, HD), lambda n, h, s: (n, 0, h))
-
-    out_specs = [
-        row_spec,
-        row_spec,
-        term_spec(3 * BS),
-        term_spec(3 * BS),
-        term_spec(2 * BS),
-        term_spec(2 * BS),
-        term_spec(R * BS),
-        term_spec(R * BS),
-    ]
+    rand_spec = pl.BlockSpec((1, R * BS, HD), lambda n, h, s: (n, 0, h))
+    prob_spec = pl.BlockSpec((1, 1, BS, g), lambda n, h, s: (n, h, 0, 0))
+    out_specs = [row_spec, row_spec, rand_spec, rand_spec, prob_spec, prob_spec]
     out_shape = [
         jax.ShapeDtypeStruct((rows, width), jnp.bfloat16),
         jax.ShapeDtypeStruct((rows, width), jnp.bfloat16),
-        jax.ShapeDtypeStruct((nbd, 3 * BS, width), jnp.float32),
-        jax.ShapeDtypeStruct((nbd, 3 * BS, width), jnp.float32),
-        jax.ShapeDtypeStruct((nbd, 2 * BS, width), jnp.float32),
-        jax.ShapeDtypeStruct((nbd, 2 * BS, width), jnp.float32),
         jax.ShapeDtypeStruct((nbd, R * BS, width), jnp.bfloat16),
         jax.ShapeDtypeStruct((nbd, R * BS, width), jnp.bfloat16),
+        jax.ShapeDtypeStruct((nbd, heads, BS, g), jnp.bfloat16),
+        jax.ShapeDtypeStruct((nbd, heads, BS, g), jnp.bfloat16),
     ]
     grid_spec = pltpu.PrefetchScalarGridSpec(
         num_scalar_prefetch=1,
@@ -126,12 +123,33 @@
         out_specs=out_specs,
     )
     args = [query, dout, mask] + [padded] * 6 + [glob] * 2 + [fetched] * (2 * R)
-    return pl.pallas_call(
-        attention_kernel,
+    out, dq, rk, rv, pb, dsb = pl.pallas_call(
+        scores_kernel,
         grid_spec=grid_spec,
         out_shape=out_shape,
         interpret=INTERPRET,
     )(slots, *args)
+
+    row2 = pl.BlockSpec((BS, HD), lambda n, h: (n, h))
+    prob2 = pl.BlockSpec((1, 1, BS, g), lambda n, h: (n, h, 0, 0))
+
+    def term_spec(size):
+        return pl.BlockSpec((1, size, HD), lambda n, h: (n, 0, h))
+
+    wk, wv, gk, gv = pl.pallas_call(
+        terms_kernel,
+        grid=(nbd, heads),
+        in_specs=[row2, row2, prob2, prob2],
+        out_specs=[term_spec(3 * BS), term_spec(3 * BS), term_spec(2 * BS), term_spec(2 * BS)],
+        out_shape=[
+            jax.ShapeDtypeStruct((nbd, 3 * BS, width), jnp.float32),
+            jax.ShapeDtypeStruct((nbd, 3 * BS, width), jnp.float32),
+            jax.ShapeDtypeStruct((nbd, 2 * BS, width), jnp.float32),
+            jax.ShapeDtypeStruct((nbd, 2 * BS, width), jnp.float32),
+        ],
+        interpret=INTERPRET,
+    )(query, dout, pb, dsb)
+    return out, dq, wk, wv, gk, gv, rk, rv
 
 
 def overlap(terms, nbd):
@@ -206,7 +224,13 @@
     glob_total = lax.psum(glob_grad.astype(jnp.bfloat16), ("head", "blk")).astype(pf)
     own = own.at[:2].add(jnp.where(me == 0, glob_total, 0.0))
     rand_grad = jnp.concatenate([rk, rv], axis=-1).reshape(nbd * R, BS, 2 * width)
-    returning = jnp.zeros((ndev * cap, BS, 2 * width), jnp.bfloat16).at[mine_slot].set(rand_grad)
+    match = mine_slot[None, :] == jnp.arange(ndev * cap, dtype=jnp.int32)[:, None]
+    source = jnp.argmax(match, axis=1)
+    returning = jnp.where(
+        jnp.any(match, axis=1)[:, None, None],
+        jnp.take(rand_grad, source, axis=0),
+        jnp.zeros((), jnp.bfloat16),
+    )
     back = lax.all_to_all(returning, ("head", "blk"), split_axis=0, concat_axis=0, tiled=True)
     onehot = (
         (block_id[None, :] == jnp.arange(nbd, dtype=jnp.int32)[:, None]) & filled[None, :]

time: 882 us -> 872 us (0.989)
  waiting for transfers between devices: 460 us -> 375 us
  Pallas kernels: 150 us -> 227 us
  local copies, waits for them, and re-layouts: 118 us -> 91.4 us
  other arithmetic: 70.9 us -> 88.4 us
    ppermute x2, waiting for transfers between devices: 392 us -> 0.01 us  [extended(): lax.ppermute(lax.slice_in_dim(block, 0, width, axis=dim), axis, backward)]
    ppermute x2, waiting for transfers between devices: 14 us -> 325 us  [extended(): lax.ppermute(lax.slice_in_dim(block, block.shape[dim] - width, None, axis...]
    pallas_call x1 -> x2, Pallas kernels: 150 us -> 227 us  [the longest x1 148 us: attention(): pl.pallas_call(scores_kernel, grid_spec=grid_spec, out_shape=out_shape, i...]
    scatter x1 -> x0, local copies, waits for them, and re-layouts: 31.7 us -> none  [body(): jnp.zeros((ndev * cap, BS, 2 * width), jnp.bfloat16).at[mine_slot]]
    select_n x1 -> x2, other arithmetic: 0.01 us -> 14.3 us  [the longest x1 14.3 us: body(): jnp.where(jnp.any(match, axis=1)[:, None, None], jnp.take(rand_grad, sour...]
    gather x0 -> x1, local copies, waits for them, and re-layouts: none -> 11.8 us  [body(): jnp.take(rand_grad, source, axis=0)]
  transfers between devices with their start and end apart: 8 -> 8, of which waited for: 6 -> 4; matrix products, arithmetic and copies ran while one was open for 12% -> 12% of each run, Pallas kernels for 0% -> 9%
where the time goes in v2:
time: 872 us; the launch traced here: 857 us
  waiting for transfers between devices  375 us (43%)
  Pallas kernels  227 us (26%)
  local copies, waits for them, and re-layouts  91.4 us (10%)
  other arithmetic  88.4 us (10%)
  starting transfers between devices  31.1 us (4%)
  matrix products  29.2 us (3%)
  between operations  14.9 us (2%)
    ppermute x2, waiting for transfers between devices, extended(): lax.ppermute(lax.slice_in_dim(block, block.shape[dim] - width, None, axis...  325 us
    pallas_call x1, Pallas kernels, attention(): pl.pallas_call(scores_kernel, grid_spec=grid_spec, out_shape=out_shape, i...  148 us
    pallas_call x1, Pallas kernels, attention(): pl.pallas_call(terms_kernel, grid=(nbd, heads), in_specs=[row2, row2, pro...  79.7 us
    psum x1, waiting for transfers between devices, from_root(): return lax.psum(kept, axis)  35.4 us
    dot_general x1, matrix products, body(): jnp.dot(onehot, back.reshape(ndev * cap, BS * 2 * width), preferred_eleme...  29.2 us
    scatter-add x2, local copies, waits for them, and re-layouts, body(): own = own.at[0].add(arrived[:BS]).at[nbd - 1].add(arrived[3 * BS:])  28.3 us
    squeeze x2, local copies, waits for them, and re-layouts, overlap(): w4[:, 0]  19.5 us
  transfers between devices with their start and end apart: 8, of which 4 were waited for; matrix products, arithmetic and copies ran while one was open for 12% of the time, Pallas kernels for 9%

profile of v2, /device:TPU:14, one launch (start us, length us, event | category | flops | bytes accessed | tf_op | source)
XLA Modules:
  0.0 857.3 jit_solution(5331515378730056985)
XLA Ops:
  11.1 3.2 constant_dynamic-update-slice_fusion.1
  15.8 9.3 %gather_fusion = bf16[32,64,4096]{2,1,0:T(8,128)(2,1)} fusion(bf16[8,64,4096]{2,1,0:T(8,128)(2,1)} %bitcast.1, s32[1024]{0:T(1024)S(1)} %pad_clamp_fusion.1), kind=kCustom, calls=%fused_computation | custom fusion | bytes 33554560 | tf_op jit(solution)/shard_map/jit(_take)/gather | solution.py:188
  25.1 14.3 %select_select_fusion.1 = bf16[32,64,4096]{2,1,0:T(8,128)(2,1)} fusion(bf16[32,64,4096]{2,1,0:T(8,128)(2,1)} %gather_fusion, pred[32]{0:T(512)(128)(4,1)S(1)} %get-tuple-element.85, pred[32]{0:T(512)(128)(4,1)S(1)} %get-tuple-element.66), kind=kLoop, calls=%fused_computation.6 | loop fusion | flops 16777216 | bytes 33554496 | tf_op jit(solution)/shard_map/jit(_where)/select_n | solution.py:187
  39.4 8.7 %all-to-all-start = ((bf16[32,64,4096]{2,1,0:T(8,128)(2,1)}), bf16[32,64,4096]{2,1,0:T(8,128)(2,1)}, u32[]{:S(2)}, u32[]{:S(2)}) async-start(bf16[32,64,4096]{2,1,0:T(8,128)(2,1)} %select_select_fusion.1), calls=%async_computation | async-start | bytes 33554432 | tf_op jit(solution)/shard_map/all_to_all | solution.py:190
  49.4 3.4 collective-permute-start
  52.8 4.3 collective-permute-start.1
  60.4 227.7 %collective-permute-done = bf16[64,4096]{1,0:T(8,128)(2,1)S(1)} collective-permute-done((bf16[64,4096]{1,0:T(8,128)(2,1)S(1)}, bf16[64,4096]{1,0:T(8,128)(2,1)S(1)}, u32[]{:S(2)}, u32[]{:S(2)}) %collective-permute-start) | collective-permute-done | bytes 524320 | tf_op jit(solution)/shard_map/ppermute | solution.py:24
  288.1 5.7 pad_maximum_fusion.2.kw0.kw1.kw2.vw0.vw1.vw2
  293.8 35.4 %all-reduce.9.cloned.1.call-done.kg.vg = bf16[128,4096]{1,0:T(8,128)(2,1)} async-done(((bf16[128,4096]{1,0:T(8,128)(2,1)}), bf16[128,4096]{1,0:T(8,128)(2,1)}) %all-reduce.9.cloned.1.call-update) | async-done | bytes 1048592 | tf_op jit(solution)/shard_map/psum | solution.py:34
  329.1 147.5 %shard_map.84 = (bf16[512,2048]{1,0:T(8,128)(2,1)}, bf16[512,2048]{1,0:T(8,128)(2,1)}, bf16[8,192,2048]{2,1,0:T(8,128)(2,1)}, bf16[8,192,2048]{2,1,0:T(8,128)(2,...) custom-call(s32[24]{0:T(128)} %copy-done.3, bf16[512,2048]{1,0:T(8,128)(2,1)} %q_ref.3, ...), custom_call_target="tpu_custom_call" | custom-call | tf_op jit(solution)/shard_map/pallas_call | solution.py:126
  476.7 10.6 %pad_maximum_fusion = bf16[8,192,4096]{2,1,0:T(8,128)(2,1)} fusion(bf16[8,192,2048]{2,1,0:T(8,128)(2,1)} %get-tuple-element.61, bf16[8,192,2048]{2,1,0:T(8,128)(2,1)} %get-tuple-element.60), kind=kLoop, calls=%fused_computation.7 | loop fusion | flops 25165824 | bytes 25165824 | tf_op jit(solution)/shard_map/concatenate | solution.py:226
  487.3 11.8 %gather_fusion.1 = bf16[32,64,4096]{2,1,0:T(8,128)(2,1)} fusion(bf16[24,64,4096]{2,1,0:T(8,128)(2,1)} %bitcast.68, s32[1024]{0:T(1024)S(1)} %pad_clamp_fusion), kind=kCustom, calls=%fused_computation.1 | custom fusion | bytes 33554560 | tf_op jit(solution)/shard_map/jit(_take)/gather | solution.py:231
  499.2 14.3 %select_select_fusion = bf16[32,64,4096]{2,1,0:T(8,128)(2,1)} fusion(bf16[32,64,4096]{2,1,0:T(8,128)(2,1)} %gather_fusion.1, pred[32]{0:T(512)(128)(4,1)S(1)} %get-tuple-element.84, pred[32]{0:T(512)(128)(4,1)S(1)} %fusion.19), kind=kLoop, calls=%fused_computation.5 | loop fusion | flops 16777216 | bytes 33554496 | tf_op jit(solution)/shard_map/jit(_where)/select_n | solution.py:229
  513.4 6.5 all-to-all-start.1
  520.1 79.7 %shard_map.85 = (f32[8,192,2048]{2,1,0:T(8,128)}, f32[8,192,2048]{2,1,0:T(8,128)}, f32[8,128,2048]{2,1,0:T(8,128)}, f32[8,128,2048]{2,1,0:T(8,128)}) custom-call(bf16[512,2048]{1,0:T(8,128)(2,1)} %q_ref.3, bf16[512,2048]{1,0:T(8,128)(2,1)} %do_ref.3, bf16[8,16,64,320]{3,2,1,0:T(8,128)(2,1)} %get-tuple-element.53.pb_ref, ...), custom_call_target="tpu_custom_call" | custom-call | tf_op jit(solution)/shard_map/pallas_call | solution.py:139
  599.9 4.2 reduce_sum.41
  604.1 4.2 reduce_sum.42
  610.5 9.8 %slice_bitcast_fusion.5 = (f32[8,64,2048]{2,1,0:T(8,128)S(1)}, f32[8,64,2048]{2,1,0:T(8,128)}, f32[8,64,2048]{2,1,0:T(8,128)}) fusion(f32[8,3,64,2048]{3,2,1,0:T(8,128)} %bitcast.74), kind=kLoop, calls=%fused_computation.20 | loop fusion | bytes 25165824 | tf_op jit(solution)/shard_map/squeeze | solution.py:159
  620.3 8.3 fusion.30
  628.6 9.8 %slice_bitcast_fusion.2 = (f32[8,64,2048]{2,1,0:T(8,128)S(1)}, f32[8,64,2048]{2,1,0:T(8,128)}, f32[8,64,2048]{2,1,0:T(8,128)}) fusion(f32[8,3,64,2048]{3,2,1,0:T(8,128)} %bitcast.73), kind=kLoop, calls=%fused_computation.17 | loop fusion | bytes 25165824 | tf_op jit(solution)/shard_map/squeeze | solution.py:159
  638.3 8.3 fusion.31
  649.6 3.5 collective-permute-start.2
  653.9 4.5 collective-permute-start.3
  662.0 3.0 pad_maximum_fusion.1
  665.0 97.7 %collective-permute-done.2 = bf16[64,4096]{1,0:T(8,128)(2,1)S(1)} collective-permute-done((bf16[64,4096]{1,0:T(8,128)(2,1)}, bf16[64,4096]{1,0:T(8,128)(2,1)S(1)}, u32[]{:S(2)}, u32[]{:S(2)}) %collective-permute-start.2) | collective-permute-done | bytes 524320 | tf_op jit(solution)/shard_map/ppermute | solution.py:24
  763.9 8.1 copy.45
  774.6 20.2 %scatter-add.11 = f32[8,64,4096]{2,0,1:T(8,128)} dynamic-update-slice(f32[8,64,4096]{2,0,1:T(8,128)} %copy.45, f32[1,64,4096]{2,0,1:T(1,128)S(1)} %copy_add_fusion, s32[]{:T(128)} %constant.156.clone.1, s32[]{:T(128)} %constant.153.clone.1, s32[]{:T(128)} %constant.153.clone.1) | dynamic-update-slice | bytes 2097156 | tf_op jit(solution)/shard_map/scatter-add | solution.py:220
  794.8 14.3 %all-reduce.11.cloned.1.call-done = bf16[2,64,4096]{2,0,1:T(2,128)(2,1)} async-done(((bf16[2,64,4096]{2,0,1:T(2,128)(2,1)}), bf16[2,64,4096]{2,0,1:T(2,128)(2,1)}) %all-reduce.11.cloned.1.call-update) | async-done | bytes 1048592 | tf_op jit(solution)/shard_map/psum | solution.py:224
  809.1 6.4 fusion.5
  815.5 29.2 %add_convert_fusion = bf16[8,64,4096]{2,0,1:T(8,128)(2,1)S(1)} fusion(f32[8,64,4096]{2,0,1:T(8,128)} %fusion.5, s32[32]{0:T(128)S(1)} %copy-done.2, pred[32]{0:T(512)(128)(4,1)S(1)} %get-tuple-element.66, bf16[4,8,64,4096]{3,2,1,0:T(8,128)(2,1)} %bitcast.37), kind=kOutput, calls=%fused_computation.11 | convolution fusion | flops 138412544 | bytes 29360288 | tf_op jit(solution)/shard_map/dot_general | solution.py:238
  845.1 2.5 copy.48
  847.5 2.5 copy.49
  (69 shorter events, 23.7 us)
Async XLA Ops:
  7.2 7.2 copy-start
  9.5 50.8 %copy-start.3 = (s32[24]{0:T(128)}, s32[24]{0:T(128)S(1)}, u32[]{:S(2)}) copy-start(s32[24]{0:T(128)S(1)} %fusion.36.slots_ref) | copy-start | bytes 292
  10.6 0.5 copy-start.1
  39.4 289.8 %all-to-all-start = ((bf16[32,64,4096]{2,1,0:T(8,128)(2,1)}), bf16[32,64,4096]{2,1,0:T(8,128)(2,1)}, u32[]{:S(2)}, u32[]{:S(2)}) async-start(bf16[32,64,4096]{2,1,0:T(8,128)(2,1)} %select_select_fusion.1), calls=%async_computation | async-start | bytes 33554432 | tf_op jit(solution)/shard_map/all_to_all | solution.py:190
  48.1 281.1 %all-reduce.9.cloned.1.call-start = ((), (), s32[]{:S(2)}) async-start(), calls=%async_computation.2 | async-start | bytes 2097152 | tf_op jit(solution)/shard_map/psum | solution.py:34
  49.4 238.7 %collective-permute-start = (bf16[64,4096]{1,0:T(8,128)(2,1)S(1)}, bf16[64,4096]{1,0:T(8,128)(2,1)S(1)}, u32[]{:S(2)}, u32[]{:S(2)}) collective-permute-start(bf16[64,4096]{1,0:T(8,128)(2,1)S(1)} %get-tuple-element.76), channel_id=1, source_target_pairs={{0,1},{1,2},{2,3},{3,4},{4,5},{5,6},{6,7},{7,8},{8,9},{9,10},{10,1... | collective-permute-start | bytes 1572872 | tf_op jit(solution)/shard_map/ppermute | solution.py:24
  52.8 235.3 %collective-permute-start.1 = (bf16[64,4096]{1,0:T(8,128)(2,1)S(1)}, bf16[64,4096]{1,0:T(8,128)(2,1)S(1)}, u32[]{:S(2)}, u32[]{:S(2)}) collective-permute-start(bf16[64,4096]{1,0:T(8,128)(2,1)S(1)} %get-tuple-element.77), channel_id=1, source_target_pairs={{1,0},{2,1},{3,2},{4,3},{5,4},{6,5},{7,6},{8,7},{9,8},{10,9},{11,1... | collective-permute-start | bytes 1572872 | tf_op jit(solution)/shard_map/ppermute | solution.py:27
  513.4 302.1 %all-to-all-start.1 = ((bf16[32,64,4096]{2,1,0:T(8,128)(2,1)}), bf16[32,64,4096]{2,1,0:T(8,128)(2,1)}, u32[]{:S(2)}, u32[]{:S(2)}) async-start(bf16[32,64,4096]{2,1,0:T(8,128)(2,1)} %select_select_fusion), calls=%async_computation.1 | async-start | bytes 33554432 | tf_op jit(solution)/shard_map/all_to_all | solution.py:234
  519.9 289.2 %all-reduce.11.cloned.1.call-start = ((), (), s32[]{:S(2)}) async-start(), calls=%async_computation.3 | async-start | bytes 2097152 | tf_op jit(solution)/shard_map/psum | solution.py:224
  638.3 20.1 %slice-start = ((s8[5242880]{0:T(1024)(128)(4,1)}), s8[4194304]{0:T(1024)(128)(4,1)S(1)}, s32[]{:S(2)}) async-start(s8[5242880]{0:T(1024)(128)(4,1)} %bitcast.69), calls=%async_computation.4 | async-start | bytes 8388608
  638.3 20.1 %slice-start.1 = ((s8[5242880]{0:T(1024)(128)(4,1)}), s8[1048576]{0:T(1024)(128)(4,1)S(1)}, s32[]{:S(2)}) async-start(s8[5242880]{0:T(1024)(128)(4,1)} %bitcast.69), calls=%async_computation.5 | async-start | bytes 2097152
  648.8 10.0 %slice-start.2 = ((s8[5242880]{0:T(1024)(128)(4,1)}), s8[4194304]{0:T(1024)(128)(4,1)S(1)}, s32[]{:S(2)}) async-start(s8[5242880]{0:T(1024)(128)(4,1)} %bitcast.71), calls=%async_computation.6 | async-start | bytes 8388608
  649.6 113.1 %collective-permute-start.2 = (bf16[64,4096]{1,0:T(8,128)(2,1)}, bf16[64,4096]{1,0:T(8,128)(2,1)S(1)}, u32[]{:S(2)}, u32[]{:S(2)}) collective-permute-start(bf16[64,4096]{1,0:T(8,128)(2,1)} %pad_maximum_fusion.8), channel_id=1, source_target_pairs={{0,1},{1,2},{2,3},{3,4},{4,5},{5,6},{6,7},{7,8},{8,9},{9,10},{10,1... | collective-permute-start | bytes 1572872 | tf_op jit(solution)/shard_map/ppermute | solution.py:24
  653.9 108.7 %collective-permute-start.3 = (bf16[64,4096]{1,0:T(8,128)(2,1)}, bf16[64,4096]{1,0:T(8,128)(2,1)}, u32[]{:S(2)}, u32[]{:S(2)}) collective-permute-start(bf16[64,4096]{1,0:T(8,128)(2,1)} %pad_maximum_fusion.9), channel_id=1, source_target_pairs={{1,0},{2,1},{3,2},{4,3},{5,4},{6,5},{7,6},{8,7},{9,8},{10,9},{11,1... | collective-permute-start | bytes 1572872 | tf_op jit(solution)/shard_map/ppermute | solution.py:27
  658.5 1.2 slice-start.3
  773.1 42.4 %copy-start.2 = (s32[32]{0:T(128)S(1)}, s32[32]{0:T(128)}, u32[]{:S(2)}) copy-start(s32[32]{0:T(128)} %copy-done.1) | copy-start | bytes 388
Sparse Core Ops, SparseCore 0:
  59.5 269.6 all-reduce.8
  610.6 198.4 all-reduce.10

commit v3 on v2

--- a/solution.py
+++ b/solution.py
@@ -14,6 +14,7 @@
 
 NEG = -1e30
 INTERPRET = False
+HG = 4
 
 
 def extended(block, sides, width):
@@ -41,72 +42,85 @@
 ):
     pf = jnp.float32
     scale = 1.0 / math.sqrt(HD)
-    q = q_ref[...]
-    do = do_ref[...]
-    k = jnp.concatenate([kw0[...], kw1[...], kw2[...], kg[...], kr0[0], kr1[0], kr2[0]], axis=0)
-    v = jnp.concatenate([vw0[...], vw1[...], vw2[...], vg[...], vr0[0], vr1[0], vr2[0]], axis=0)
     nt = (((1,), (1,)), ((), ()))
     tn = (((0,), (0,)), ((), ()))
-    s = lax.dot_general(q, k, nt, preferred_element_type=pf) * scale
-    s = jnp.where(mask_ref[0] > 0, s, NEG)
-    top = jnp.max(s, axis=1, keepdims=True)
-    e = jnp.exp(s - top)
-    p = e / jnp.sum(e, axis=1, keepdims=True)
-    pb = p.astype(jnp.bfloat16)
-    ob = jnp.dot(pb, v, preferred_element_type=pf).astype(jnp.bfloat16)
-    out_ref[...] = ob
-    delta = jnp.sum(do.astype(pf) * ob.astype(pf), axis=1, keepdims=True)
-    dp = lax.dot_general(do, v, nt, preferred_element_type=pf)
-    ds = p * (dp - delta)
-    dsb = ds.astype(jnp.bfloat16)
-    dq_ref[...] = (jnp.dot(dsb, k, preferred_element_type=pf) * scale).astype(jnp.bfloat16)
     g = 5 * BS
-    rk_ref[0] = (lax.dot_general(dsb[:, g:], q, tn, preferred_element_type=pf) * scale).astype(jnp.bfloat16)
-    rv_ref[0] = lax.dot_general(pb[:, g:], do, tn, preferred_element_type=pf).astype(jnp.bfloat16)
-    pb_ref[0, 0] = pb[:, :g]
-    dsb_ref[0, 0] = dsb[:, :g]
+    valid = mask_ref[0] > 0
+    for t in range(HG):
+        c = slice(t * HD, (t + 1) * HD)
+        q = q_ref[:, c]
+        do = do_ref[:, c]
+        k = jnp.concatenate(
+            [kw0[:, c], kw1[:, c], kw2[:, c], kg[:, c], kr0[0, :, c], kr1[0, :, c], kr2[0, :, c]], axis=0
+        )
+        v = jnp.concatenate(
+            [vw0[:, c], vw1[:, c], vw2[:, c], vg[:, c], vr0[0, :, c], vr1[0, :, c], vr2[0, :, c]], axis=0
+        )
+        s = lax.dot_general(q, k, nt, preferred_element_type=pf) * scale
+        s = jnp.where(valid, s, NEG)
+        top = jnp.max(s, axis=1, keepdims=True)
+        e = jnp.exp(s - top)
+        p = e / jnp.sum(e, axis=1, keepdims=True)
+        pb = p.astype(jnp.bfloat16)
+        ob = jnp.dot(pb, v, preferred_element_type=pf).astype(jnp.bfloat16)
+        out_ref[:, c] = ob
+        delta = jnp.sum(do.astype(pf) * ob.astype(pf), axis=1, keepdims=True)
+        dp = lax.dot_general(do, v, nt, preferred_element_type=pf)
+        ds = p * (dp - delta)
+        dsb = ds.astype(jnp.bfloat16)
+        dq_ref[:, c] = (jnp.dot(dsb, k, preferred_element_type=pf) * scale).astype(jnp.bfloat16)
+        rk_ref[0, :, c] = (
+            lax.dot_general(dsb[:, g:], q, tn, preferred_element_type=pf) * scale
+        ).astype(jnp.bfloat16)
+        rv_ref[0, :, c] = lax.dot_general(pb[:, g:], do, tn, preferred_element_type=pf).astype(jnp.bfloat16)
+        pb_ref[0, t] = pb[:, :g]
+        dsb_ref[0, t] = dsb[:, :g]
 
 
 def terms_kernel(q_ref, do_ref, pb_ref, dsb_ref, wk_ref, wv_ref, gk_ref, gv_ref):
     pf = jnp.float32
     scale = 1.0 / math.sqrt(HD)
     tn = (((0,), (0,)), ((), ()))
-    kt = lax.dot_general(dsb_ref[0, 0], q_ref[...], tn, preferred_element_type=pf) * scale
-    vt = lax.dot_general(pb_ref[0, 0], do_ref[...], tn, preferred_element_type=pf)
     w = 3 * BS
-    wk_ref[0] = kt[:w]
-    wv_ref[0] = vt[:w]
-    gk_ref[0] = kt[w:]
-    gv_ref[0] = vt[w:]
+    for t in range(HG):
+        c = slice(t * HD, (t + 1) * HD)
+        kt = lax.dot_general(dsb_ref[0, t], q_ref[:, c], tn, preferred_element_type=pf) * scale
+        vt = lax.dot_general(pb_ref[0, t], do_ref[:, c], tn, preferred_element_type=pf)
+        wk_ref[0, :, c] = kt[:w]
+        wv_ref[0, :, c] = vt[:w]
+        gk_ref[0, :, c] = kt[w:]
+        gv_ref[0, :, c] = vt[w:]
 
 
 def attention(query, dout, mask, padded, glob, fetched, slots):
     rows, width = query.shape
     heads = width // HD
+    groups = heads // HG
+    cw = HG * HD
     nbd = rows // BS
     span = (5 + R) * BS
     g = 5 * BS
 
     def tile(j, col):
-        return pl.BlockSpec((BS, HD), lambda n, h, s: (n + j, h + col))
+        return pl.BlockSpec((BS, cw), lambda n, h, s: (n + j, h + col))
 
     def rand_tile(j, col):
-        return pl.BlockSpec((1, BS, HD), lambda n, h, s: (s[n * R + j], 0, h + col))
-
-    row_spec = pl.BlockSpec((BS, HD), lambda n, h, s: (n, h))
+        return pl.BlockSpec((1, BS, cw), lambda n, h, s: (s[n * R + j], 0, h + col))
+
+    row_spec = pl.BlockSpec((BS, cw), lambda n, h, s: (n, h))
     in_specs = (
         [row_spec, row_spec, pl.BlockSpec((1, 1, span), lambda n, h, s: (n, 0, 0))]
         + [tile(j, 0) for j in range(3)]
-        + [tile(j, heads) for j in range(3)]
+        + [tile(j, groups) for j in range(3)]
         + [
-            pl.BlockSpec((2 * BS, HD), lambda n, h, s: (0, h)),
-            pl.BlockSpec((2 * BS, HD), lambda n, h, s: (0, h + heads)),
+            pl.BlockSpec((2 * BS, cw), lambda n, h, s: (0, h)),
+            pl.BlockSpec((2 * BS, cw), lambda n, h, s: (0, h + groups)),
         ]
         + [rand_tile(j, 0) for j in range(R)]
-        + [rand_tile(j, heads) for j in range(R)]
-    )
-    rand_spec = pl.BlockSpec((1, R * BS, HD), lambda n, h, s: (n, 0, h))
-    prob_spec = pl.BlockSpec((1, 1, BS, g), lambda n, h, s: (n, h, 0, 0))
+        + [rand_tile(j, groups) for j in range(R)]
+    )
+    rand_spec = pl.BlockSpec((1, R * BS, cw), lambda n, h, s: (n, 0, h))
+    prob_spec = pl.BlockSpec((1, HG, BS, g), lambda n, h, s: (n, h, 0, 0))
     out_specs = [row_spec, row_spec, rand_spec, rand_spec, prob_spec, prob_spec]
     out_shape = [
         jax.ShapeDtypeStruct((rows, width), jnp.bfloat16),
@@ -118,7 +132,7 @@
     ]
     grid_spec = pltpu.PrefetchScalarGridSpec(
         num_scalar_prefetch=1,
-        grid=(nbd, heads),
+        grid=(nbd, groups),
         in_specs=in_specs,
         out_specs=out_specs,
     )
@@ -130,15 +144,15 @@
         interpret=INTERPRET,
     )(slots, *args)
 
-    row2 = pl.BlockSpec((BS, HD), lambda n, h: (n, h))
-    prob2 = pl.BlockSpec((1, 1, BS, g), lambda n, h: (n, h, 0, 0))
+    row2 = pl.BlockSpec((BS, cw), lambda n, h: (n, h))
+    prob2 = pl.BlockSpec((1, HG, BS, g), lambda n, h: (n, h, 0, 0))
 
     def term_spec(size):
-        return pl.BlockSpec((1, size, HD), lambda n, h: (n, 0, h))
+        return pl.BlockSpec((1, size, cw), lambda n, h: (n, 0, h))
 
     wk, wv, gk, gv = pl.pallas_call(
         terms_kernel,
-        grid=(nbd, heads),
+        grid=(nbd, groups),
         in_specs=[row2, row2, prob2, prob2],
         out_specs=[term_spec(3 * BS), term_spec(3 * BS), term_spec(2 * BS), term_spec(2 * BS)],
         out_shape=[
@@ -217,12 +231,15 @@
     )
     arrived = extended(rims.astype(jnp.bfloat16), ((("head", "blk"), 0),), BS).astype(pf)
     own = jnp.concatenate([sk[1 : nbd + 1], sv[1 : nbd + 1]], axis=-1)
-    own = own.at[0].add(arrived[:BS]).at[nbd - 1].add(arrived[3 * BS :])
     glob_grad = jnp.concatenate([jnp.sum(gk, axis=0), jnp.sum(gv, axis=0)], axis=-1).reshape(
         2, BS, 2 * width
     )
     glob_total = lax.psum(glob_grad.astype(jnp.bfloat16), ("head", "blk")).astype(pf)
-    own = own.at[:2].add(jnp.where(me == 0, glob_total, 0.0))
+    edge = jnp.concatenate(
+        [arrived[None, :BS], jnp.zeros((nbd - 2, BS, 2 * width), pf), arrived[None, 3 * BS :]], axis=0
+    )
+    lead = jnp.pad(jnp.where(me == 0, glob_total, 0.0), ((0, nbd - 2), (0, 0), (0, 0)))
+    own = own + edge + lead
     rand_grad = jnp.concatenate([rk, rv], axis=-1).reshape(nbd * R, BS, 2 * width)
     match = mine_slot[None, :] == jnp.arange(ndev * cap, dtype=jnp.int32)[:, None]
     source = jnp.argmax(match, axis=1)

time: 872 us -> 830 us (0.952)
  Pallas kernels: 227 us -> 137 us
  waiting for transfers between devices: 375 us -> 447 us
  local copies, waits for them, and re-layouts: 91.4 us -> 67.5 us
    ppermute x2, waiting for transfers between devices: 0.01 us -> 353 us  [extended(): lax.ppermute(lax.slice_in_dim(block, 0, width, axis=dim), axis, backward)]
    ppermute x2, waiting for transfers between devices: 325 us -> 18.2 us  [extended(): lax.ppermute(lax.slice_in_dim(block, block.shape[dim] - width, None, axis...]
    pallas_call x1, Pallas kernels: 79.7 us -> 32.4 us  [attention(): pl.pallas_call(terms_kernel, grid=(nbd, groups), in_specs=[row2, row2, pr...]
    pallas_call x1, Pallas kernels: 148 us -> 104 us  [attention(): pl.pallas_call(scores_kernel, grid_spec=grid_spec, out_shape=out_shape, i...]
    scatter-add x2 -> x0, local copies, waits for them, and re-layouts: 28.3 us -> none  [body(): own = own.at[0].add(arrived[:BS]).at[nbd - 1].add(arrived[3 * BS:])]
    psum x1, waiting for transfers between devices: 14.3 us -> 41.4 us  [body(): lax.psum(glob_grad.astype(jnp.bfloat16), ('head', 'blk')).astype(pf)]
  transfers between devices with their start and end apart: 8 -> 8, of which waited for: 4 -> 6; matrix products, arithmetic and copies ran while one was open for 12% -> 10% of each run, Pallas kernels for 9% -> 4%
where the time goes in v3:
time: 830 us; the launch traced here: 816 us
  waiting for transfers between devices  447 us (54%)
  Pallas kernels  137 us (17%)
  other arithmetic  86 us (10%)
  local copies, waits for them, and re-layouts  67.5 us (8%)
  matrix products  36 us (4%)
  starting transfers between devices  27.7 us (3%)
  between operations  14.8 us (2%)
    ppermute x2, waiting for transfers between devices, extended(): lax.ppermute(lax.slice_in_dim(block, 0, width, axis=dim), axis, backward)  353 us
    pallas_call x1, Pallas kernels, attention(): pl.pallas_call(scores_kernel, grid_spec=grid_spec, out_shape=out_shape, i...  104 us
    psum x1, waiting for transfers between devices, body(): lax.psum(glob_grad.astype(jnp.bfloat16), ('head', 'blk')).astype(pf)  41.4 us
    dot_general x1, matrix products, body(): jnp.dot(onehot, back.reshape(ndev * cap, BS * 2 * width), preferred_eleme...  36 us
    psum x1, waiting for transfers between devices, from_root(): return lax.psum(kept, axis)  34.6 us
    pallas_call x1, Pallas kernels, attention(): pl.pallas_call(terms_kernel, grid=(nbd, groups), in_specs=[row2, row2, pr...  32.4 us
    squeeze x2, local copies, waits for them, and re-layouts, overlap(): w4[:, 0]  19.3 us
    ppermute x2, waiting for transfers between devices, extended(): lax.ppermute(lax.slice_in_dim(block, block.shape[dim] - width, None, axis...  18.2 us
  transfers between devices with their start and end apart: 8, of which 6 were waited for; matrix products, arithmetic and copies ran while one was open for 10% of the time, Pallas kernels for 4%

profile of v3, /device:TPU:14, one launch (start us, length us, event | category | flops | bytes accessed | tf_op | source)
XLA Modules:
  0.0 815.8 jit_solution(3992119718848743230)
XLA Ops:
  10.5 3.2 constant_dynamic-update-slice_fusion.1
  15.8 9.4 %gather_fusion = bf16[32,64,4096]{2,1,0:T(8,128)(2,1)} fusion(bf16[8,64,4096]{2,1,0:T(8,128)(2,1)} %bitcast.1, s32[1024]{0:T(1024)S(1)} %get-tuple-element.51), kind=kCustom, calls=%fused_computation | custom fusion | bytes 33554560 | tf_op jit(solution)/shard_map/jit(_take)/gather | solution.py:202
  25.2 14.3 %select_select_fusion.1 = bf16[32,64,4096]{2,1,0:T(8,128)(2,1)} fusion(bf16[32,64,4096]{2,1,0:T(8,128)(2,1)} %gather_fusion, pred[32]{0:T(512)(128)(4,1)S(1)} %compare_and_fusion.1, pred[32]{0:T(512)(128)(4,1)S(1)} %get-tuple-element.30), kind=kLoop, calls=%fused_computation.6 | loop fusion | flops 16777216 | bytes 33554496 | tf_op jit(solution)/shard_map/jit(_where)/select_n | solution.py:201
  39.4 8.5 %all-to-all-start = ((bf16[32,64,4096]{2,1,0:T(8,128)(2,1)}), bf16[32,64,4096]{2,1,0:T(8,128)(2,1)}, u32[]{:S(2)}, u32[]{:S(2)}) async-start(bf16[32,64,4096]{2,1,0:T(8,128)(2,1)} %select_select_fusion.1), calls=%async_computation | async-start | bytes 33554432 | tf_op jit(solution)/shard_map/all_to_all | solution.py:204
  49.3 4.3 collective-permute-start.1
  55.5 2.3 slice_select_fusion
  58.9 222.5 %collective-permute-done.1 = bf16[64,4096]{1,0:T(8,128)(2,1)S(1)} collective-permute-done((bf16[64,4096]{1,0:T(8,128)(2,1)S(1)}, bf16[64,4096]{1,0:T(8,128)(2,1)S(1)}, u32[]{:S(2)}, u32[]{:S(2)}) %collective-permute-start.1) | collective-permute-done | bytes 524320 | tf_op jit(solution)/shard_map/ppermute | solution.py:28
  281.4 6.6 collective-permute-done
  288.0 5.7 pad_maximum_fusion.2.kw0.kw1.kw2.vw0.vw1.vw2
  293.7 34.6 %all-reduce.10.cloned.1.call-done.kg.vg = bf16[128,4096]{1,0:T(8,128)(2,1)} async-done(((bf16[128,4096]{1,0:T(8,128)(2,1)}), bf16[128,4096]{1,0:T(8,128)(2,1)}) %all-reduce.10.cloned.1.call-update) | async-done | bytes 1048592 | tf_op jit(solution)/shard_map/psum | solution.py:35
  328.2 104.4 %shard_map.84 = (bf16[512,2048]{1,0:T(8,128)(2,1)}, bf16[512,2048]{1,0:T(8,128)(2,1)}, bf16[8,192,2048]{2,1,0:T(8,128)(2,1)}, bf16[8,192,2048]{2,1,0:T(8,128)(2,...) custom-call(s32[24]{0:T(128)} %copy-done.3, bf16[512,2048]{1,0:T(8,128)(2,1)} %q_ref.3, ...), custom_call_target="tpu_custom_call" | custom-call | tf_op jit(solution)/shard_map/pallas_call | solution.py:140
  432.7 10.6 %pad_maximum_fusion = bf16[8,192,4096]{2,1,0:T(8,128)(2,1)} fusion(bf16[8,192,2048]{2,1,0:T(8,128)(2,1)} %get-tuple-element.25, bf16[8,192,2048]{2,1,0:T(8,128)(2,1)} %get-tuple-element.24), kind=kLoop, calls=%fused_computation.7 | loop fusion | flops 25165824 | bytes 25165824 | tf_op jit(solution)/shard_map/concatenate | solution.py:243
  443.3 11.8 %gather_fusion.1 = bf16[32,64,4096]{2,1,0:T(8,128)(2,1)} fusion(bf16[24,64,4096]{2,1,0:T(8,128)(2,1)} %bitcast.66, s32[1024]{0:T(1024)S(1)} %get-tuple-element.50), kind=kCustom, calls=%fused_computation.1 | custom fusion | bytes 33554560 | tf_op jit(solution)/shard_map/jit(_take)/gather | solution.py:248
  455.1 14.3 %select_select_fusion = bf16[32,64,4096]{2,1,0:T(8,128)(2,1)} fusion(bf16[32,64,4096]{2,1,0:T(8,128)(2,1)} %gather_fusion.1, pred[32]{0:T(512)(128)(4,1)S(1)} %compare_and_fusion, pred[32]{0:T(512)(128)(4,1)S(1)} %fusion.18), kind=kLoop, calls=%fused_computation.5 | loop fusion | flops 16777216 | bytes 33554496 | tf_op jit(solution)/shard_map/jit(_where)/select_n | solution.py:246
  469.3 6.5 all-to-all-start.1
  476.2 32.4 %shard_map.85 = (f32[8,192,2048]{2,1,0:T(8,128)}, f32[8,192,2048]{2,1,0:T(8,128)}, f32[8,128,2048]{2,1,0:T(8,128)}, f32[8,128,2048]{2,1,0:T(8,128)}) custom-call(bf16[512,2048]{1,0:T(8,128)(2,1)} %q_ref.3, bf16[512,2048]{1,0:T(8,128)(2,1)} %do_ref.3, bf16[8,16,64,320]{3,2,1,0:T(8,128)(2,1)} %get-tuple-element.17.pb_ref, ...), custom_call_target="tpu_custom_call" | custom-call | tf_op jit(solution)/shard_map/pallas_call | solution.py:153
  508.6 9.6 %slice_bitcast_fusion.2 = (f32[8,64,2048]{2,1,0:T(8,128)}, f32[8,64,2048]{2,1,0:T(8,128)}, f32[8,64,2048]{2,1,0:T(8,128)}) fusion(f32[8,3,64,2048]{3,2,1,0:T(8,128)} %bitcast.68), kind=kLoop, calls=%fused_computation.18 | loop fusion | bytes 25165824 | tf_op jit(solution)/shard_map/squeeze | solution.py:173
  518.2 7.7 fusion.30
  525.9 9.6 %slice_bitcast_fusion.5 = (f32[8,64,2048]{2,1,0:T(8,128)}, f32[8,64,2048]{2,1,0:T(8,128)}, f32[8,64,2048]{2,1,0:T(8,128)}) fusion(f32[8,3,64,2048]{3,2,1,0:T(8,128)} %bitcast.67), kind=kLoop, calls=%fused_computation.21 | loop fusion | bytes 25165824 | tf_op jit(solution)/shard_map/squeeze | solution.py:173
  535.5 8.2 %fusion.29 = (bf16[10,64,2048]{2,1,0:T(8,128)(2,1)}, f32[10,64,2048]{2,1,0:T(8,128)S(1)}) fusion(f32[8,64,2048]{2,1,0:T(8,128)} %get-tuple-element.34, f32[8,64,2048]{2,1,0:T(8,128)} %get-tuple-element.33, f32[8,64,2048]{2,1,0:T(8,128)} %get-tuple-element.32), kind=kLoop, calls=%fused_computation.88 | loop fusion | flops 3932160 | bytes 20447232 | tf_op jit(solution)/shard_map/convert.11
  546.8 4.3 collective-permute-start.3
  556.0 2.4 slice.94
  558.4 4.2 reduce_sum.42
  562.7 4.2 reduce_sum.41
  569.1 7.7 pad_maximum_fusion.1
  576.7 130.3 %collective-permute-done.3 = bf16[64,4096]{1,0:T(8,128)(2,1)} collective-permute-done((bf16[64,4096]{1,0:T(8,128)(2,1)}, bf16[64,4096]{1,0:T(8,128)(2,1)}, u32[]{:S(2)}, u32[]{:S(2)}) %collective-permute-start.3) | collective-permute-done | bytes 524320 | tf_op jit(solution)/shard_map/ppermute | solution.py:28
  707.0 11.6 %collective-permute-done.2 = bf16[64,4096]{1,0:T(8,128)(2,1)} collective-permute-done((bf16[64,4096]{1,0:T(8,128)(2,1)}, bf16[64,4096]{1,0:T(8,128)(2,1)}, u32[]{:S(2)}, u32[]{:S(2)}) %collective-permute-start.2) | collective-permute-done | bytes 524320 | tf_op jit(solution)/shard_map/ppermute | solution.py:25
  723.3 41.4 %all-reduce.12.cloned.1.call-done = bf16[2,64,4096]{2,0,1:T(2,128)(2,1)} async-done(((bf16[2,64,4096]{2,0,1:T(2,128)(2,1)}), bf16[2,64,4096]{2,0,1:T(2,128)(2,1)}) %all-reduce.12.cloned.1.call-update) | async-done | bytes 1048592 | tf_op jit(solution)/shard_map/psum | solution.py:237
  764.7 2.3 convert_select_fusion
  767.0 36.0 %fusion.5 = bf16[8,64,4096]{2,0,1:T(8,128)(2,1)S(1)} fusion(f32[1,64,4096]{2,0,1:T(1,128)S(1)} %broadcast_in_dim.79, f32[1,64,4096]{2,0,1:T(1,128)} %copy.44, f32[8,64,4096]{2,1,0:T(8,128)} %pad_maximum_fusion.1, f32[2,64,4096]{2,0,1:T(2,128)S(1)} %convert_select_fusion, f32[8]{0:T(128)S(1)} %pad.37.clone, s32[32]{0:T(128)S(1)} %copy-done.2, ...), kind=kOutput, calls=%fused_computation.12 | convolution fusion | flops 146801152 | bytes 33554624 | tf_op jit(solution)/shard_map/dot_general | solution.py:255
  803.6 2.5 copy.48
  806.0 2.5 copy.49
  (58 shorter events, 25.2 us)
Async XLA Ops:
  7.2 7.1 copy-start
  8.8 0.5 copy-start.1
  10.5 48.3 %copy-start.3 = (s32[24]{0:T(128)}, s32[24]{0:T(128)S(1)}, u32[]{:S(2)}) copy-start(s32[24]{0:T(128)S(1)} %fusion.35.slots_ref) | copy-start | bytes 292
  39.4 288.8 %all-to-all-start = ((bf16[32,64,4096]{2,1,0:T(8,128)(2,1)}), bf16[32,64,4096]{2,1,0:T(8,128)(2,1)}, u32[]{:S(2)}, u32[]{:S(2)}) async-start(bf16[32,64,4096]{2,1,0:T(8,128)(2,1)} %select_select_fusion.1), calls=%async_computation | async-start | bytes 33554432 | tf_op jit(solution)/shard_map/all_to_all | solution.py:204
  48.0 280.2 %all-reduce.10.cloned.1.call-start = ((), (), s32[]{:S(2)}) async-start(), calls=%async_computation.2 | async-start | bytes 2097152 | tf_op jit(solution)/shard_map/psum | solution.py:35
  49.3 232.1 %collective-permute-start.1 = (bf16[64,4096]{1,0:T(8,128)(2,1)S(1)}, bf16[64,4096]{1,0:T(8,128)(2,1)S(1)}, u32[]{:S(2)}, u32[]{:S(2)}) collective-permute-start(bf16[64,4096]{1,0:T(8,128)(2,1)S(1)} %get-tuple-element.41), channel_id=1, source_target_pairs={{1,0},{2,1},{3,2},{4,3},{5,4},{6,5},{7,6},{8,7},{9,8},{10,9},{11,1... | collective-permute-start | bytes 1572872 | tf_op jit(solution)/shard_map/ppermute | solution.py:28
  53.6 234.4 %collective-permute-start = (bf16[64,4096]{1,0:T(8,128)(2,1)S(1)}, bf16[64,4096]{1,0:T(8,128)(2,1)S(1)}, u32[]{:S(2)}, u32[]{:S(2)}) collective-permute-start(bf16[64,4096]{1,0:T(8,128)(2,1)S(1)} %get-tuple-element.40), channel_id=1, source_target_pairs={{0,1},{1,2},{2,3},{3,4},{4,5},{5,6},{6,7},{7,8},{8,9},{9,10},{10,1... | collective-permute-start | bytes 1572872 | tf_op jit(solution)/shard_map/ppermute | solution.py:25
  469.3 297.6 %all-to-all-start.1 = ((bf16[32,64,4096]{2,1,0:T(8,128)(2,1)}), bf16[32,64,4096]{2,1,0:T(8,128)(2,1)}, u32[]{:S(2)}, u32[]{:S(2)}) async-start(bf16[32,64,4096]{2,1,0:T(8,128)(2,1)} %select_select_fusion), calls=%async_computation.1 | async-start | bytes 33554432 | tf_op jit(solution)/shard_map/all_to_all | solution.py:251
  475.9 288.8 %all-reduce.12.cloned.1.call-start = ((), (), s32[]{:S(2)}) async-start(), calls=%async_computation.3 | async-start | bytes 2097152 | tf_op jit(solution)/shard_map/psum | solution.py:237
  546.8 160.2 %collective-permute-start.3 = (bf16[64,4096]{1,0:T(8,128)(2,1)}, bf16[64,4096]{1,0:T(8,128)(2,1)}, u32[]{:S(2)}, u32[]{:S(2)}) collective-permute-start(bf16[64,4096]{1,0:T(8,128)(2,1)} %pad_maximum_fusion.9), channel_id=1, source_target_pairs={{1,0},{2,1},{3,2},{4,3},{5,4},{6,5},{7,6},{8,7},{9,8},{10,9},{11,1... | collective-permute-start | bytes 1572872 | tf_op jit(solution)/shard_map/ppermute | solution.py:28
  551.9 166.7 %collective-permute-start.2 = (bf16[64,4096]{1,0:T(8,128)(2,1)}, bf16[64,4096]{1,0:T(8,128)(2,1)}, u32[]{:S(2)}, u32[]{:S(2)}) collective-permute-start(bf16[64,4096]{1,0:T(8,128)(2,1)} %pad_maximum_fusion.8), channel_id=1, source_target_pairs={{0,1},{1,2},{2,3},{3,4},{4,5},{5,6},{6,7},{7,8},{8,9},{9,10},{10,1... | collective-permute-start | bytes 1572872 | tf_op jit(solution)/shard_map/ppermute | solution.py:25
  576.7 190.2 %copy-start.2 = (s32[32]{0:T(128)S(1)}, s32[32]{0:T(128)}, u32[]{:S(2)}) copy-start(s32[32]{0:T(128)} %copy-done.1) | copy-start | bytes 388
Sparse Core Ops, SparseCore 0:
  58.0 270.2 all-reduce.9
  569.2 195.4 all-reduce.11

commit v4 on v3

--- a/solution.py
+++ b/solution.py
@@ -15,6 +15,7 @@
 NEG = -1e30
 INTERPRET = False
 HG = 4
+CHUNKS = 2
 
 
 def extended(block, sides, width):
@@ -92,14 +93,18 @@
         gv_ref[0, :, c] = vt[w:]
 
 
-def attention(query, dout, mask, padded, glob, fetched, slots):
+def attention(query, dout, mask, padded, glob, fetched, slots, chunk, chunks):
     rows, width = query.shape
     heads = width // HD
     groups = heads // HG
+    per = groups // chunks
+    base = chunk * per
     cw = HG * HD
+    part = per * cw
     nbd = rows // BS
     span = (5 + R) * BS
     g = 5 * BS
+    hc = per * HG
 
     def tile(j, col):
         return pl.BlockSpec((BS, cw), lambda n, h, s: (n + j, h + col))
@@ -107,32 +112,33 @@
     def rand_tile(j, col):
         return pl.BlockSpec((1, BS, cw), lambda n, h, s: (s[n * R + j], 0, h + col))
 
-    row_spec = pl.BlockSpec((BS, cw), lambda n, h, s: (n, h))
+    row_spec = pl.BlockSpec((BS, cw), lambda n, h, s: (n, h + base))
     in_specs = (
         [row_spec, row_spec, pl.BlockSpec((1, 1, span), lambda n, h, s: (n, 0, 0))]
-        + [tile(j, 0) for j in range(3)]
-        + [tile(j, groups) for j in range(3)]
+        + [tile(j, base) for j in range(3)]
+        + [tile(j, groups + base) for j in range(3)]
         + [
-            pl.BlockSpec((2 * BS, cw), lambda n, h, s: (0, h)),
-            pl.BlockSpec((2 * BS, cw), lambda n, h, s: (0, h + groups)),
+            pl.BlockSpec((2 * BS, cw), lambda n, h, s: (0, h + base)),
+            pl.BlockSpec((2 * BS, cw), lambda n, h, s: (0, h + groups + base)),
         ]
         + [rand_tile(j, 0) for j in range(R)]
-        + [rand_tile(j, groups) for j in range(R)]
-    )
+        + [rand_tile(j, per) for j in range(R)]
+    )
+    own_row = pl.BlockSpec((BS, cw), lambda n, h, s: (n, h))
     rand_spec = pl.BlockSpec((1, R * BS, cw), lambda n, h, s: (n, 0, h))
     prob_spec = pl.BlockSpec((1, HG, BS, g), lambda n, h, s: (n, h, 0, 0))
-    out_specs = [row_spec, row_spec, rand_spec, rand_spec, prob_spec, prob_spec]
+    out_specs = [own_row, own_row, rand_spec, rand_spec, prob_spec, prob_spec]
     out_shape = [
-        jax.ShapeDtypeStruct((rows, width), jnp.bfloat16),
-        jax.ShapeDtypeStruct((rows, width), jnp.bfloat16),
-        jax.ShapeDtypeStruct((nbd, R * BS, width), jnp.bfloat16),
-        jax.ShapeDtypeStruct((nbd, R * BS, width), jnp.bfloat16),
-        jax.ShapeDtypeStruct((nbd, heads, BS, g), jnp.bfloat16),
-        jax.ShapeDtypeStruct((nbd, heads, BS, g), jnp.bfloat16),
+        jax.ShapeDtypeStruct((rows, part), jnp.bfloat16),
+        jax.ShapeDtypeStruct((rows, part), jnp.bfloat16),
+        jax.ShapeDtypeStruct((nbd, R * BS, part), jnp.bfloat16),
+        jax.ShapeDtypeStruct((nbd, R * BS, part), jnp.bfloat16),
+        jax.ShapeDtypeStruct((nbd, hc, BS, g), jnp.bfloat16),
+        jax.ShapeDtypeStruct((nbd, hc, BS, g), jnp.bfloat16),
     ]
     grid_spec = pltpu.PrefetchScalarGridSpec(
         num_scalar_prefetch=1,
-        grid=(nbd, groups),
+        grid=(nbd, per),
         in_specs=in_specs,
         out_specs=out_specs,
     )
@@ -144,7 +150,7 @@
         interpret=INTERPRET,
     )(slots, *args)
 
-    row2 = pl.BlockSpec((BS, cw), lambda n, h: (n, h))
+    row2 = pl.BlockSpec((BS, cw), lambda n, h: (n, h + base))
     prob2 = pl.BlockSpec((1, HG, BS, g), lambda n, h: (n, h, 0, 0))
 
     def term_spec(size):
@@ -152,14 +158,14 @@
 
     wk, wv, gk, gv = pl.pallas_call(
         terms_kernel,
-        grid=(nbd, groups),
+        grid=(nbd, per),
         in_specs=[row2, row2, prob2, prob2],
         out_specs=[term_spec(3 * BS), term_spec(3 * BS), term_spec(2 * BS), term_spec(2 * BS)],
         out_shape=[
-            jax.ShapeDtypeStruct((nbd, 3 * BS, width), jnp.float32),
-            jax.ShapeDtypeStruct((nbd, 3 * BS, width), jnp.float32),
-            jax.ShapeDtypeStruct((nbd, 2 * BS, width), jnp.float32),
-            jax.ShapeDtypeStruct((nbd, 2 * BS, width), jnp.float32),
+            jax.ShapeDtypeStruct((nbd, 3 * BS, part), jnp.float32),
+            jax.ShapeDtypeStruct((nbd, 3 * BS, part), jnp.float32),
+            jax.ShapeDtypeStruct((nbd, 2 * BS, part), jnp.float32),
+            jax.ShapeDtypeStruct((nbd, 2 * BS, part), jnp.float32),
         ],
         interpret=INTERPRET,
     )(query, dout, pb, dsb)
@@ -201,7 +207,6 @@
     outgoing = jnp.where(
         filled[:, None, None], jnp.take(tiles, block_id, axis=0), jnp.zeros((), pair.dtype)
     )
-    fetched = lax.all_to_all(outgoing, ("head", "blk"), split_axis=0, concat_axis=0, tiled=True)
     mine = lax.dynamic_slice_in_dim(rand, me * nbd, nbd, 0).reshape(-1)
     mine_owner = mine // nbd
     count = mine.shape[0]
@@ -219,45 +224,58 @@
         axis=1,
     )
     mask = jnp.repeat(valid, BS, axis=1).astype(pf).reshape(nbd, 1, span)
-    out, dq, wk, wv, gk, gv, rk, rv = attention(query, dout, mask, padded, glob, fetched, mine_slot)
-    sk = overlap(wk, nbd)
-    sv = overlap(wv, nbd)
-    rims = jnp.concatenate(
-        [
-            jnp.concatenate([sk[0], sv[0]], axis=-1),
-            jnp.concatenate([sk[nbd + 1], sv[nbd + 1]], axis=-1),
-        ],
-        axis=0,
-    )
-    arrived = extended(rims.astype(jnp.bfloat16), ((("head", "blk"), 0),), BS).astype(pf)
-    own = jnp.concatenate([sk[1 : nbd + 1], sv[1 : nbd + 1]], axis=-1)
-    glob_grad = jnp.concatenate([jnp.sum(gk, axis=0), jnp.sum(gv, axis=0)], axis=-1).reshape(
-        2, BS, 2 * width
-    )
-    glob_total = lax.psum(glob_grad.astype(jnp.bfloat16), ("head", "blk")).astype(pf)
-    edge = jnp.concatenate(
-        [arrived[None, :BS], jnp.zeros((nbd - 2, BS, 2 * width), pf), arrived[None, 3 * BS :]], axis=0
-    )
-    lead = jnp.pad(jnp.where(me == 0, glob_total, 0.0), ((0, nbd - 2), (0, 0), (0, 0)))
-    own = own + edge + lead
-    rand_grad = jnp.concatenate([rk, rv], axis=-1).reshape(nbd * R, BS, 2 * width)
     match = mine_slot[None, :] == jnp.arange(ndev * cap, dtype=jnp.int32)[:, None]
     source = jnp.argmax(match, axis=1)
-    returning = jnp.where(
-        jnp.any(match, axis=1)[:, None, None],
-        jnp.take(rand_grad, source, axis=0),
-        jnp.zeros((), jnp.bfloat16),
-    )
-    back = lax.all_to_all(returning, ("head", "blk"), split_axis=0, concat_axis=0, tiled=True)
+    present = jnp.any(match, axis=1)[:, None, None]
     onehot = (
         (block_id[None, :] == jnp.arange(nbd, dtype=jnp.int32)[:, None]) & filled[None, :]
     ).astype(jnp.bfloat16)
-    own = own + jnp.dot(
-        onehot, back.reshape(ndev * cap, BS * 2 * width), preferred_element_type=pf
-    ).reshape(nbd, BS, 2 * width)
-    dk = own[..., :width].astype(jnp.bfloat16).reshape(rows, width)
-    dv = own[..., width:].astype(jnp.bfloat16).reshape(rows, width)
-    return (out, dq, dk, dv)
+    chunks = CHUNKS
+    part = width // chunks
+    results = []
+    previous = None
+    for c in range(chunks):
+        cols = jnp.concatenate(
+            [outgoing[..., c * part : (c + 1) * part], outgoing[..., width + c * part : width + (c + 1) * part]],
+            axis=-1,
+        )
+        if previous is not None:
+            cols, _ = lax.optimization_barrier((cols, previous))
+        fetched = lax.all_to_all(cols, ("head", "blk"), split_axis=0, concat_axis=0, tiled=True)
+        previous = fetched
+        out, dq, wk, wv, gk, gv, rk, rv = attention(
+            query, dout, mask, padded, glob, fetched, mine_slot, c, chunks
+        )
+        sk = overlap(wk, nbd)
+        sv = overlap(wv, nbd)
+        rims = jnp.concatenate(
+            [
+                jnp.concatenate([sk[0], sv[0]], axis=-1),
+                jnp.concatenate([sk[nbd + 1], sv[nbd + 1]], axis=-1),
+            ],
+            axis=0,
+        )
+        arrived = extended(rims.astype(jnp.bfloat16), ((("head", "blk"), 0),), BS).astype(pf)
+        own = jnp.concatenate([sk[1 : nbd + 1], sv[1 : nbd + 1]], axis=-1)
+        glob_grad = jnp.concatenate([jnp.sum(gk, axis=0), jnp.sum(gv, axis=0)], axis=-1).reshape(
+            2, BS, 2 * part
+        )
+        glob_total = lax.psum(glob_grad.astype(jnp.bfloat16), ("head", "blk")).astype(pf)
+        edge = jnp.concatenate(
+            [arrived[None, :BS], jnp.zeros((nbd - 2, BS, 2 * part), pf), arrived[None, 3 * BS :]], axis=0
+        )
+        lead = jnp.pad(jnp.where(me == 0, glob_total, 0.0), ((0, nbd - 2), (0, 0), (0, 0)))
+        own = own + edge + lead
+        rand_grad = jnp.concatenate([rk, rv], axis=-1).reshape(nbd * R, BS, 2 * part)
+        returning = jnp.where(present, jnp.take(rand_grad, source, axis=0), jnp.zeros((), jnp.bfloat16))
+        back = lax.all_to_all(returning, ("head", "blk"), split_axis=0, concat_axis=0, tiled=True)
+        own = own + jnp.dot(
+            onehot, back.reshape(ndev * cap, BS * 2 * part), preferred_element_type=pf
+        ).reshape(nbd, BS, 2 * part)
+        dk = own[..., :part].astype(jnp.bfloat16).reshape(rows, part)
+        dv = own[..., part:].astype(jnp.bfloat16).reshape(rows, part)
+        results.append((out, dq, dk, dv))
+    return tuple(jnp.concatenate([r[i] for r in results], axis=1) for i in range(4))
 
 
 def solution(mesh):

time: 830 us -> 950 us (1.14)
  waiting for transfers between devices: 447 us -> 533 us
  starting transfers between devices: 27.7 us -> 43.5 us
  local copies, waits for them, and re-layouts: 67.5 us -> 82.4 us
    ppermute x2 -> x3, waiting for transfers between devices: 353 us -> 175 us  [extended(): lax.ppermute(lax.slice_in_dim(block, 0, width, axis=dim), axis, backward)]
    all_to_all x1 -> x2, waiting for transfers between devices: 0.01 us -> 103 us  [body(): lax.all_to_all(cols, ('head', 'blk'), split_axis=0, concat_axis=0, tiled=...]
    all_to_all x1 -> x2, waiting for transfers between devices: 0.01 us -> 84.3 us  [body(): lax.all_to_all(returning, ('head', 'blk'), split_axis=0, concat_axis=0, t...]
    psum x1, waiting for transfers between devices: 41.4 us -> 100 us  [body(): lax.psum(glob_grad.astype(jnp.bfloat16), ('head', 'blk')).astype(pf)]
    psum x1, waiting for transfers between devices: 34.6 us -> 65.5 us  [from_root(): return lax.psum(kept, axis)]
    concatenate x1 -> x8, other arithmetic: 10.6 us -> 35.4 us  [the longest x2 16.3 us: body(): jnp.concatenate([outgoing[..., c * part:(c + 1) * part], outgoing[..., wi...]
    squeeze x2, local copies, waits for them, and re-layouts: 19.3 us -> 4.55 us  [overlap(): w4[:, 0]]
    ppermute x2 -> x3, waiting for transfers between devices: 18.2 us -> 4.14 us  [extended(): lax.ppermute(lax.slice_in_dim(block, block.shape[dim] - width, None, axis...]
  transfers between devices with their start and end apart: 8 -> 12, of which waited for: 6 -> 8; matrix products, arithmetic and copies ran while one was open for 10% -> 13% of each run, Pallas kernels for 4% -> 9%
where the time goes in v4:
time: 950 us; the launch traced here: 942 us
  waiting for transfers between devices  533 us (56%)
  Pallas kernels  141 us (15%)
  other arithmetic  93.5 us (10%)
  local copies, waits for them, and re-layouts  82.4 us (9%)
  starting transfers between devices  43.5 us (5%)
  matrix products  34.4 us (4%)
  between operations  14.8 us (2%)
    ppermute x3, waiting for transfers between devices, extended(): lax.ppermute(lax.slice_in_dim(block, 0, width, axis=dim), axis, backward)  175 us
    pallas_call x2, Pallas kernels, attention(): pl.pallas_call(scores_kernel, grid_spec=grid_spec, out_shape=out_shape, i...  107 us
    all_to_all x2, waiting for transfers between devices, body(): lax.all_to_all(cols, ('head', 'blk'), split_axis=0, concat_axis=0, tiled=...  103 us
    psum x1, waiting for transfers between devices, body(): lax.psum(glob_grad.astype(jnp.bfloat16), ('head', 'blk')).astype(pf)  100 us
    all_to_all x2, waiting for transfers between devices, body(): lax.all_to_all(returning, ('head', 'blk'), split_axis=0, concat_axis=0, t...  84.3 us
    psum x1, waiting for transfers between devices, from_root(): return lax.psum(kept, axis)  65.5 us
    dot_general x2, matrix products, body(): jnp.dot(onehot, back.reshape(ndev * cap, BS * 2 * part), preferred_elemen...  34.4 us
    pallas_call x2, Pallas kernels, attention(): pl.pallas_call(terms_kernel, grid=(nbd, per), in_specs=[row2, row2, prob2...  33.8 us
  transfers between devices with their start and end apart: 12, of which 8 were waited for; matrix products, arithmetic and copies ran while one was open for 13% of the time, Pallas kernels for 9%

profile of v4, /device:TPU:14, one launch (start us, length us, event | category | flops | bytes accessed | tf_op | source)
XLA Modules:
  0.0 942.0 jit_solution(15677439905022095264)
XLA Ops:
  15.9 9.5 %gather_fusion = bf16[32,64,4096]{2,1,0:T(8,128)(2,1)} fusion(bf16[8,64,4096]{2,1,0:T(8,128)(2,1)} %bitcast.1, s32[1024]{0:T(1024)S(1)} %get-tuple-element.100), kind=kCustom, calls=%fused_computation.2 | custom fusion | bytes 33554560 | tf_op jit(solution)/shard_map/jit(_take)/gather | solution.py:208
  25.4 8.7 select_select_fusion
  34.1 6.1 fusion.48
  40.3 8.2 pad_maximum_fusion
  48.4 8.5 all-to-all-start
  57.0 8.2 pad_maximum_fusion.1
  65.1 103.5 %all-to-all-done.kr0.kr1.kr2.vr0.vr1.vr2 = bf16[32,64,2048]{2,1,0:T(8,128)(2,1)} async-done(((bf16[32,64,2048]{2,1,0:T(8,128)(2,1)}), bf16[32,64,2048]{2,1,0:T(8,128)(2,1)}, u32[]{:S(2)}, u32[]{:S(2)}) %all-to-all-start) | async-done | bytes 8388640 | tf_op jit(solution)/shard_map/all_to_all | solution.py:244
  168.6 4.8 all-to-all-start.1
  184.4 101.4 %collective-permute-done.1 = bf16[64,4096]{1,0:T(8,128)(2,1)S(1)} collective-permute-done((bf16[64,4096]{1,0:T(8,128)(2,1)S(1)}, bf16[64,4096]{1,0:T(8,128)(2,1)S(1)}, u32[]{:S(2)}, u32[]{:S(2)}) %collective-permute-start.1) | collective-permute-done | bytes 524320 | tf_op jit(solution)/shard_map/ppermute | solution.py:29
  288.0 5.6 pad_maximum_fusion.4.kw0.kw1.kw2.vw0.vw1.vw2
  293.6 65.5 %all-reduce.18.cloned.1.call-done.kg.vg = bf16[128,4096]{1,0:T(8,128)(2,1)} async-done(((bf16[128,4096]{1,0:T(8,128)(2,1)}), bf16[128,4096]{1,0:T(8,128)(2,1)}) %all-reduce.18.cloned.1.call-update) | async-done | bytes 1048592 | tf_op jit(solution)/shard_map/psum | solution.py:36
  359.1 53.5 %shard_map.84 = (bf16[512,1024]{1,0:T(8,128)(2,1)}, bf16[512,1024]{1,0:T(8,128)(2,1)}, bf16[8,192,1024]{2,1,0:T(8,128)(2,1)}, bf16[8,192,1024]{2,1,0:T(8,128)(2,...) custom-call(s32[24]{0:T(128)} %copy-done.11, bf16[512,2048]{1,0:T(8,128)(2,1)} %q_ref.7, ...), custom_call_target="tpu_custom_call" | custom-call | tf_op jit(solution)/shard_map/pallas_call | solution.py:146
  412.6 6.6 pad_maximum_fusion.2
  419.1 7.8 gather_fusion.1
  426.9 53.6 %shard_map.85 = (bf16[512,1024]{1,0:T(8,128)(2,1)}, bf16[512,1024]{1,0:T(8,128)(2,1)}, bf16[8,192,1024]{2,1,0:T(8,128)(2,1)}, bf16[8,192,1024]{2,1,0:T(8,128)(2,...) custom-call(s32[24]{0:T(128)} %copy-done.11, bf16[512,2048]{1,0:T(8,128)(2,1)} %q_ref.7, ...), custom_call_target="tpu_custom_call" | custom-call | tf_op jit(solution)/shard_map/pallas_call | solution.py:146
  480.6 6.5 pad_maximum_fusion.3
  487.1 7.8 gather_fusion.2
  494.9 11.8 %select_select_fusion.2 = (bf16[32,64,2048]{2,1,0:T(8,128)(2,1)}, bf16[32,64,2048]{2,1,0:T(8,128)(2,1)}) fusion(bf16[32,64,2048]{2,1,0:T(8,128)(2,1)} %gather_fusion.1, pred[32]{0:T(512)(128)(4,1)S(1)} %compare_and_fusion, pred[32]{0:T(512)(128)(4,1)S(1)} %fusion.28, bf16[32,64,2048]{2,1,0:T(8,128)(2,1)} %gather_fusion.2), kind=kLoop, calls=%fused_computation.13 | loop fusion | flops 16777216 | bytes 33554496 | tf_op jit(solution)/shard_map/jit(_where)/select_n | solution.py:270
  506.7 6.8 all-to-all-start.3
  513.5 16.9 %shard_map.86 = (f32[8,192,1024]{2,1,0:T(8,128)}, f32[8,192,1024]{2,1,0:T(8,128)}, f32[8,128,1024]{2,1,0:T(8,128)}, f32[8,128,1024]{2,1,0:T(8,128)}) custom-call(bf16[512,2048]{1,0:T(8,128)(2,1)} %q_ref.7, bf16[512,2048]{1,0:T(8,128)(2,1)} %do_ref.7, bf16[8,8,64,320]{3,2,1,0:T(8,128)(2,1)} %get-tuple-element.32.pb_ref, ...), custom_call_target="tpu_custom_call" | custom-call | tf_op jit(solution)/shard_map/pallas_call | solution.py:159
  530.4 3.4 fusion.50
  540.1 84.3 %all-to-all-done.3 = bf16[32,64,2048]{2,1,0:T(8,128)(2,1)} async-done(((bf16[32,64,2048]{2,1,0:T(8,128)(2,1)}), bf16[32,64,2048]{2,1,0:T(8,128)(2,1)}, u32[]{:S(2)}, u32[]{:S(2)}) %all-to-all-start.3) | async-done | bytes 8388640 | tf_op jit(solution)/shard_map/all_to_all | solution.py:271
  624.5 4.8 all-to-all-start.2
  629.5 3.4 fusion.49
  657.3 4.2 slice.192
  663.2 73.3 %collective-permute-done.3 = bf16[64,2048]{1,0:T(8,128)(2,1)S(1)} collective-permute-done((bf16[64,2048]{1,0:T(8,128)(2,1)S(1)}, bf16[64,2048]{1,0:T(8,128)(2,1)S(1)}, u32[]{:S(2)}, u32[]{:S(2)}) %collective-permute-start.3) | collective-permute-done | bytes 262176 | tf_op jit(solution)/shard_map/ppermute | solution.py:29
  741.1 16.9 %shard_map.87 = (f32[8,192,1024]{2,1,0:T(8,128)}, f32[8,192,1024]{2,1,0:T(8,128)}, f32[8,128,1024]{2,1,0:T(8,128)}, f32[8,128,1024]{2,1,0:T(8,128)}) custom-call(bf16[512,2048]{1,0:T(8,128)(2,1)} %q_ref.7, bf16[512,2048]{1,0:T(8,128)(2,1)} %do_ref.7, bf16[8,8,64,320]{3,2,1,0:T(8,128)(2,1)} %get-tuple-element.41.pb_ref, ...), custom_call_target="tpu_custom_call" | custom-call | tf_op jit(solution)/shard_map/pallas_call | solution.py:159
  766.3 3.9 collective-permute-start.5
  781.3 4.1 pad_maximum_fusion.5
  791.3 100.3 %all-reduce.20.cloned.1.call-done = (bf16[2,64,2048]{2,0,1:T(2,128)(2,1)}, bf16[2,64,2048]{2,0,1:T(2,128)(2,1)}) async-done(((bf16[2,64,2048]{2,0,1:T(2,128)(2,1)}, bf16[2,64,2048]{2,0,1:T(2,128)(2,1)}), (bf16[2,64,2048]{2,0,1:T(2,128)(2,1)}, bf16[2,64,2048]{2,0,1:T(2,128)(2,1)})) %all-reduce.20.cloned.1.call-update) | async-done | bytes 1048592 | tf_op jit(solution)/shard_map/psum | solution.py:263
  894.8 18.5 %fusion.11 = bf16[8,64,2048]{2,0,1:T(8,128)(2,1)S(1)} fusion(f32[1,64,2048]{2,0,1:T(1,128)S(1)} %broadcast_in_dim.96, f32[1,64,2048]{2,0,1:T(1,128)S(1)} %copy.158, f32[8,64,2048]{2,1,0:T(8,128)} %pad_maximum_fusion.5, f32[2,64,2048]{2,0,1:T(2,128)S(1)} %convert_select_fusion, f32[8]{0:T(128)S(1)} %pad.88.clone, s32[32]{0:T(128)S(1)} %copy-done.13, ...), kind=kOutput, calls=%fused_computation.25 | convolution fusion | flops 73400832 | bytes 16777408 | tf_op jit(solution)/shard_map/dot_general | solution.py:272
  914.1 15.9 %fusion.8 = bf16[8,64,2048]{2,0,1:T(8,128)(2,1)S(1)} fusion(f32[8,64,1024]{2,0,1:T(8,128)} %slice.192, f32[8,64,1024]{2,0,1:T(8,128)} %slice.188, f32[1,64,2048]{2,0,1:T(1,128)} %broadcast_in_dim.91, f32[1,64,2048]{2,0,1:T(1,128)} %copy.148, f32[2,64,2048]{2,0,1:T(2,128)S(1)} %convert_select_fusion.1, f32[8]{0:T(128)S(1)} %pad.88.clone, ...), kind=kOutput, calls=%fused_computation.20 | convolution fusion | flops 74449408 | bytes 16777408 | tf_op jit(solution)/shard_map/dot_general | solution.py:272
  (129 shorter events, 92.9 us)
Async XLA Ops:
  7.2 7.2 copy-start.4
  8.7 16.7 %copy-start.9 = (pred[32]{0:T(512)(128)(4,1)}, pred[32]{0:T(512)(128)(4,1)S(1)}, u32[]{:S(2)}) copy-start(pred[32]{0:T(512)(128)(4,1)S(1)} %get-tuple-element.59) | copy-start | bytes 100
  8.8 0.5 copy-start.12
  10.5 173.8 %copy-start.11 = (s32[24]{0:T(128)}, s32[24]{0:T(128)S(1)}, u32[]{:S(2)}) copy-start(s32[24]{0:T(128)S(1)} %fusion.56.slots_ref) | copy-start | bytes 292
  48.4 120.2 %all-to-all-start = ((bf16[32,64,2048]{2,1,0:T(8,128)(2,1)}), bf16[32,64,2048]{2,1,0:T(8,128)(2,1)}, u32[]{:S(2)}, u32[]{:S(2)}) async-start(bf16[32,64,2048]{2,1,0:T(8,128)(2,1)} %pad_maximum_fusion), calls=%async_computation | async-start | bytes 16777216 | tf_op jit(solution)/shard_map/all_to_all | solution.py:244
  168.6 258.4 %all-to-all-start.1 = ((bf16[32,64,2048]{2,1,0:T(8,128)(2,1)}), bf16[32,64,2048]{2,1,0:T(8,128)(2,1)}, u32[]{:S(2)}, u32[]{:S(2)}) async-start(bf16[32,64,2048]{2,1,0:T(8,128)(2,1)} %pad_maximum_fusion.1), calls=%async_computation.1 | async-start | bytes 16777216 | tf_op jit(solution)/shard_map/all_to_all | solution.py:244
  173.4 185.8 %all-reduce.18.cloned.1.call-start = ((), (), s32[]{:S(2)}) async-start(), calls=%async_computation.4 | async-start | bytes 2097152 | tf_op jit(solution)/shard_map/psum | solution.py:36
  174.7 111.1 %collective-permute-start.1 = (bf16[64,4096]{1,0:T(8,128)(2,1)S(1)}, bf16[64,4096]{1,0:T(8,128)(2,1)S(1)}, u32[]{:S(2)}, u32[]{:S(2)}) collective-permute-start(bf16[64,4096]{1,0:T(8,128)(2,1)S(1)} %get-tuple-element.78), channel_id=1, source_target_pairs={{1,0},{2,1},{3,2},{4,3},{5,4},{6,5},{7,6},{8,7},{9,8},{10,9},{11,1... | collective-permute-start | bytes 1572872 | tf_op jit(solution)/shard_map/ppermute | solution.py:29
  177.7 110.2 %collective-permute-start = (bf16[64,4096]{1,0:T(8,128)(2,1)S(1)}, bf16[64,4096]{1,0:T(8,128)(2,1)S(1)}, u32[]{:S(2)}, u32[]{:S(2)}) collective-permute-start(bf16[64,4096]{1,0:T(8,128)(2,1)S(1)} %get-tuple-element.77), channel_id=1, source_target_pairs={{0,1},{1,2},{2,3},{3,4},{4,5},{5,6},{6,7},{7,8},{8,9},{9,10},{10,1... | collective-permute-start | bytes 1572872 | tf_op jit(solution)/shard_map/ppermute | solution.py:26
  506.7 117.8 %all-to-all-start.3 = ((bf16[32,64,2048]{2,1,0:T(8,128)(2,1)}), bf16[32,64,2048]{2,1,0:T(8,128)(2,1)}, u32[]{:S(2)}, u32[]{:S(2)}) async-start(bf16[32,64,2048]{2,1,0:T(8,128)(2,1)} %get-tuple-element.96), calls=%async_computation.3 | async-start | bytes 16777216 | tf_op jit(solution)/shard_map/all_to_all | solution.py:271
  624.5 289.6 %all-to-all-start.2 = ((bf16[32,64,2048]{2,1,0:T(8,128)(2,1)}), bf16[32,64,2048]{2,1,0:T(8,128)(2,1)}, u32[]{:S(2)}, u32[]{:S(2)}) async-start(bf16[32,64,2048]{2,1,0:T(8,128)(2,1)} %get-tuple-element.95), calls=%async_computation.2 | async-start | bytes 16777216 | tf_op jit(solution)/shard_map/all_to_all | solution.py:271
  629.3 262.3 %all-reduce.20.cloned.1.call-start = ((), (), s32[]{:S(2)}) async-start(), calls=%async_computation.5 | async-start | bytes 2097152 | tf_op jit(solution)/shard_map/psum | solution.py:263
  634.2 2.5 copy-start.1
  634.2 2.5 copy-start.2
  644.3 92.2 %collective-permute-start.3 = (bf16[64,2048]{1,0:T(8,128)(2,1)S(1)}, bf16[64,2048]{1,0:T(8,128)(2,1)S(1)}, u32[]{:S(2)}, u32[]{:S(2)}) collective-permute-start(bf16[64,2048]{1,0:T(8,128)(2,1)S(1)} %pad_maximum_fusion.21), channel_id=1, source_target_pairs={{1,0},{2,1},{3,2},{4,3},{5,4},{6,5},{7,6},{8,7},{9,8},{10,9},{11,1... | collective-permute-start | bytes 786440 | tf_op jit(solution)/shard_map/ppermute | solution.py:29
  647.5 91.0 %collective-permute-start.2 = (bf16[64,2048]{1,0:T(8,128)(2,1)S(1)}, bf16[64,2048]{1,0:T(8,128)(2,1)S(1)}, u32[]{:S(2)}, u32[]{:S(2)}) collective-permute-start(bf16[64,2048]{1,0:T(8,128)(2,1)S(1)} %pad_maximum_fusion.20), channel_id=1, source_target_pairs={{0,1},{1,2},{2,3},{3,4},{4,5},{5,6},{6,7},{7,8},{8,9},{9,10},{10,1... | collective-permute-start | bytes 786440 | tf_op jit(solution)/shard_map/ppermute | solution.py:26
  655.9 5.6 copy-start
  761.5 2.8 copy-start.3
  766.3 22.9 %collective-permute-start.5 = (bf16[64,2048]{1,0:T(8,128)(2,1)S(1)}, bf16[64,2048]{1,0:T(8,128)(2,1)}, u32[]{:S(2)}, u32[]{:S(2)}) collective-permute-start(bf16[64,2048]{1,0:T(8,128)(2,1)S(1)} %pad_maximum_fusion.23), channel_id=1, source_target_pairs={{1,0},{2,1},{3,2},{4,3},{5,4},{6,5},{7,6},{8,7},{9,8},{10,9},{11,1... | collective-permute-start | bytes 786440 | tf_op jit(solution)/shard_map/ppermute | solution.py:29
  771.0 18.2 %collective-permute-start.4 = (bf16[64,2048]{1,0:T(8,128)(2,1)}, bf16[64,2048]{1,0:T(8,128)(2,1)}, u32[]{:S(2)}, u32[]{:S(2)}) collective-permute-start(bf16[64,2048]{1,0:T(8,128)(2,1)} %pad_maximum_fusion.22), channel_id=1, source_target_pairs={{0,1},{1,2},{2,3},{3,4},{4,5},{5,6},{6,7},{7,8},{8,9},{9,10},{10,1... | collective-permute-start | bytes 786440 | tf_op jit(solution)/shard_map/ppermute | solution.py:26
  781.3 4.1 copy-start.6
  781.3 4.1 copy-start.8
  785.4 1.5 copy-start.5
  785.4 2.3 copy-start.7
  789.2 105.6 %copy-start.10 = (pred[32]{0:T(512)(128)(4,1)S(1)}, pred[32]{0:T(512)(128)(4,1)}, u32[]{:S(2)}) copy-start(pred[32]{0:T(512)(128)(4,1)} %copy-done.9) | copy-start | bytes 100
  789.2 105.6 %copy-start.13 = (s32[32]{0:T(128)S(1)}, s32[32]{0:T(128)}, u32[]{:S(2)}) copy-start(s32[32]{0:T(128)} %copy-done.12) | copy-start | bytes 388
Sparse Core Ops, SparseCore 0:
  183.5 175.5 all-reduce.17
  781.4 110.0 all-reduce.19

commit v5 on v4

--- a/solution.py
+++ b/solution.py
@@ -239,7 +239,9 @@
             [outgoing[..., c * part : (c + 1) * part], outgoing[..., width + c * part : width + (c + 1) * part]],
             axis=-1,
         )
-        if previous is not None:
+        if previous is None:
+            cols, _, _ = lax.optimization_barrier((cols, padded, glob))
+        else:
             cols, _ = lax.optimization_barrier((cols, previous))
         fetched = lax.all_to_all(cols, ("head", "blk"), split_axis=0, concat_axis=0, tiled=True)
         previous = fetched

time: 950 us -> 883 us (0.929)
  waiting for transfers between devices: 533 us -> 472 us
    ppermute x3, waiting for transfers between devices: 175 us -> 73.1 us  [extended(): lax.ppermute(lax.slice_in_dim(block, 0, width, axis=dim), axis, backward)]
    all_to_all x2, waiting for transfers between devices: 103 us -> 145 us  [body(): lax.all_to_all(cols, ('head', 'blk'), split_axis=0, concat_axis=0, tiled=...]
  transfers between devices with their start and end apart: 12 -> 12, of which waited for: 8 -> 7; matrix products, arithmetic and copies ran while one was open for 13% -> 17% of each run, Pallas kernels for 9% -> 10%
where the time goes in v5:
time: 883 us; the launch traced here: 875 us
  waiting for transfers between devices  472 us (53%)
  Pallas kernels  141 us (16%)
  other arithmetic  93.7 us (11%)
  local copies, waits for them, and re-layouts  78.5 us (9%)
  starting transfers between devices  40.5 us (5%)
  matrix products  34.2 us (4%)
  between operations  15.1 us (2%)
    all_to_all x2, waiting for transfers between devices, body(): lax.all_to_all(cols, ('head', 'blk'), split_axis=0, concat_axis=0, tiled=...  145 us
    pallas_call x2, Pallas kernels, attention(): pl.pallas_call(scores_kernel, grid_spec=grid_spec, out_shape=out_shape, i...  107 us
    psum x1, waiting for transfers between devices, body(): lax.psum(glob_grad.astype(jnp.bfloat16), ('head', 'blk')).astype(pf)  100 us
    all_to_all x2, waiting for transfers between devices, body(): lax.all_to_all(returning, ('head', 'blk'), split_axis=0, concat_axis=0, t...  83.7 us
    ppermute x3, waiting for transfers between devices, extended(): lax.ppermute(lax.slice_in_dim(block, 0, width, axis=dim), axis, backward)  73.1 us
    psum x1, waiting for transfers between devices, from_root(): return lax.psum(kept, axis)  67.2 us
    dot_general x2, matrix products, body(): jnp.dot(onehot, back.reshape(ndev * cap, BS * 2 * part), preferred_elemen...  34.2 us
    pallas_call x2, Pallas kernels, attention(): pl.pallas_call(terms_kernel, grid=(nbd, per), in_specs=[row2, row2, prob2...  33.9 us
  transfers between devices with their start and end apart: 12, of which 7 were waited for; matrix products, arithmetic and copies ran while one was open for 17% of the time, Pallas kernels for 10%

profile of v5, /device:TPU:14, one launch (start us, length us, event | category | flops | bytes accessed | tf_op | source)
XLA Modules:
  0.0 874.5 jit_solution(5972951493413598000)
XLA Ops:
  11.6 5.3 collective-permute-start.1
  23.0 9.5 %gather_fusion = bf16[32,64,4096]{2,1,0:T(8,128)(2,1)} fusion(bf16[8,64,4096]{2,1,0:T(8,128)(2,1)} %bitcast.118, s32[1024]{0:T(1024)S(1)} %get-tuple-element.102), kind=kCustom, calls=%fused_computation.2 | custom fusion | bytes 33554560 | tf_op jit(solution)/shard_map/jit(_take)/gather | solution.py:208
  32.5 8.7 select_select_fusion
  41.2 6.1 fusion.48
  47.3 8.2 pad_maximum_fusion
  55.5 5.7 pad_maximum_fusion.4.kw0.kw1.kw2.vw0.vw1.vw2
  61.3 67.2 %all-reduce.18.cloned.1.call-done.kg.vg = bf16[128,4096]{1,0:T(8,128)(2,1)} async-done(((bf16[128,4096]{1,0:T(8,128)(2,1)}), bf16[128,4096]{1,0:T(8,128)(2,1)}) %all-reduce.18.cloned.1.call-update) | async-done | bytes 1048592 | tf_op jit(solution)/shard_map/psum | solution.py:36
  128.5 6.5 all-to-all-start
  135.0 8.2 pad_maximum_fusion.1
  143.1 103.5 %all-to-all-done.kr0.kr1.kr2.vr0.vr1.vr2 = bf16[32,64,2048]{2,1,0:T(8,128)(2,1)} async-done(((bf16[32,64,2048]{2,1,0:T(8,128)(2,1)}), bf16[32,64,2048]{2,1,0:T(8,128)(2,1)}, u32[]{:S(2)}, u32[]{:S(2)}) %all-to-all-start) | async-done | bytes 8388640 | tf_op jit(solution)/shard_map/all_to_all | solution.py:246
  246.6 5.0 all-to-all-start.1
  252.6 53.5 %shard_map.84 = (bf16[512,1024]{1,0:T(8,128)(2,1)}, bf16[512,1024]{1,0:T(8,128)(2,1)}, bf16[8,192,1024]{2,1,0:T(8,128)(2,1)}, bf16[8,192,1024]{2,1,0:T(8,128)(2,...) custom-call(s32[24]{0:T(128)} %copy-done.13, bf16[512,2048]{1,0:T(8,128)(2,1)} %q_ref.7, ...), custom_call_target="tpu_custom_call" | custom-call | tf_op jit(solution)/shard_map/pallas_call | solution.py:146
  306.1 6.6 pad_maximum_fusion.2
  312.7 7.8 gather_fusion.1
  320.4 42.0 %all-to-all-done.1.kr0.kr1.kr2.vr0.vr1.vr2 = bf16[32,64,2048]{2,1,0:T(8,128)(2,1)} async-done(((bf16[32,64,2048]{2,1,0:T(8,128)(2,1)}), bf16[32,64,2048]{2,1,0:T(8,128)(2,1)}, u32[]{:S(2)}, u32[]{:S(2)}) %all-to-all-start.1) | async-done | bytes 8388640 | tf_op jit(solution)/shard_map/all_to_all | solution.py:246
  362.4 53.6 %shard_map.85 = (bf16[512,1024]{1,0:T(8,128)(2,1)}, bf16[512,1024]{1,0:T(8,128)(2,1)}, bf16[8,192,1024]{2,1,0:T(8,128)(2,1)}, bf16[8,192,1024]{2,1,0:T(8,128)(2,...) custom-call(s32[24]{0:T(128)} %copy-done.13, bf16[512,2048]{1,0:T(8,128)(2,1)} %q_ref.7, ...), custom_call_target="tpu_custom_call" | custom-call | tf_op jit(solution)/shard_map/pallas_call | solution.py:146
  416.0 6.5 pad_maximum_fusion.3
  422.5 7.8 gather_fusion.2
  430.3 11.8 %select_select_fusion.2 = (bf16[32,64,2048]{2,1,0:T(8,128)(2,1)}, bf16[32,64,2048]{2,1,0:T(8,128)(2,1)}) fusion(bf16[32,64,2048]{2,1,0:T(8,128)(2,1)} %gather_fusion.1, pred[32]{0:T(512)(128)(4,1)S(1)} %compare_and_fusion, pred[32]{0:T(512)(128)(4,1)S(1)} %fusion.28, bf16[32,64,2048]{2,1,0:T(8,128)(2,1)} %gather_fusion.2), kind=kLoop, calls=%fused_computation.13 | loop fusion | flops 16777216 | bytes 33554496 | tf_op jit(solution)/shard_map/jit(_where)/select_n | solution.py:272
  442.1 4.7 all-to-all-start.3
  446.9 17.0 %shard_map.86 = (f32[8,192,1024]{2,1,0:T(8,128)}, f32[8,192,1024]{2,1,0:T(8,128)}, f32[8,128,1024]{2,1,0:T(8,128)}, f32[8,128,1024]{2,1,0:T(8,128)}) custom-call(bf16[512,2048]{1,0:T(8,128)(2,1)} %q_ref.7, bf16[512,2048]{1,0:T(8,128)(2,1)} %do_ref.7, bf16[8,8,64,320]{3,2,1,0:T(8,128)(2,1)} %get-tuple-element.34.pb_ref, ...), custom_call_target="tpu_custom_call" | custom-call | tf_op jit(solution)/shard_map/pallas_call | solution.py:159
  473.6 83.7 %all-to-all-done.3 = bf16[32,64,2048]{2,1,0:T(8,128)(2,1)} async-done(((bf16[32,64,2048]{2,1,0:T(8,128)(2,1)}), bf16[32,64,2048]{2,1,0:T(8,128)(2,1)}, u32[]{:S(2)}, u32[]{:S(2)}) %all-to-all-start.3) | async-done | bytes 8388640 | tf_op jit(solution)/shard_map/all_to_all | solution.py:273
  557.3 5.2 all-to-all-start.2
  562.5 3.4 fusion.49
  590.1 4.2 slice.192
  596.1 73.1 %collective-permute-done.3 = bf16[64,2048]{1,0:T(8,128)(2,1)S(1)} collective-permute-done((bf16[64,2048]{1,0:T(8,128)(2,1)S(1)}, bf16[64,2048]{1,0:T(8,128)(2,1)S(1)}, u32[]{:S(2)}, u32[]{:S(2)}) %collective-permute-start.3) | collective-permute-done | bytes 262176 | tf_op jit(solution)/shard_map/ppermute | solution.py:29
  673.9 16.9 %shard_map.87 = (f32[8,192,1024]{2,1,0:T(8,128)}, f32[8,192,1024]{2,1,0:T(8,128)}, f32[8,128,1024]{2,1,0:T(8,128)}, f32[8,128,1024]{2,1,0:T(8,128)}) custom-call(bf16[512,2048]{1,0:T(8,128)(2,1)} %q_ref.7, bf16[512,2048]{1,0:T(8,128)(2,1)} %do_ref.7, bf16[8,8,64,320]{3,2,1,0:T(8,128)(2,1)} %get-tuple-element.43.pb_ref, ...), custom_call_target="tpu_custom_call" | custom-call | tf_op jit(solution)/shard_map/pallas_call | solution.py:159
  699.1 3.8 collective-permute-start.5
  714.1 4.1 pad_maximum_fusion.5
  724.0 100.0 %all-reduce.20.cloned.1.call-done = (bf16[2,64,2048]{2,0,1:T(2,128)(2,1)}, bf16[2,64,2048]{2,0,1:T(2,128)(2,1)}) async-done(((bf16[2,64,2048]{2,0,1:T(2,128)(2,1)}, bf16[2,64,2048]{2,0,1:T(2,128)(2,1)}), (bf16[2,64,2048]{2,0,1:T(2,128)(2,1)}, bf16[2,64,2048]{2,0,1:T(2,128)(2,1)})) %all-reduce.20.cloned.1.call-update) | async-done | bytes 1048592 | tf_op jit(solution)/shard_map/psum | solution.py:265
  827.2 18.3 %fusion.11 = bf16[8,64,2048]{2,0,1:T(8,128)(2,1)S(1)} fusion(f32[1,64,2048]{2,0,1:T(1,128)S(1)} %broadcast_in_dim.96, f32[1,64,2048]{2,0,1:T(1,128)S(1)} %copy.158, f32[8,64,2048]{2,1,0:T(8,128)} %pad_maximum_fusion.5, f32[2,64,2048]{2,0,1:T(2,128)S(1)} %convert_select_fusion, f32[8]{0:T(128)S(1)} %pad.88.clone, s32[32]{0:T(128)S(1)} %copy-done.15, ...), kind=kOutput, calls=%fused_computation.25 | convolution fusion | flops 73400832 | bytes 16777408 | tf_op jit(solution)/shard_map/dot_general | solution.py:274
  846.3 16.0 %fusion.8 = bf16[8,64,2048]{2,0,1:T(8,128)(2,1)S(1)} fusion(f32[8,64,1024]{2,0,1:T(8,128)} %slice.192, f32[8,64,1024]{2,0,1:T(8,128)} %slice.188, f32[1,64,2048]{2,0,1:T(1,128)} %broadcast_in_dim.91, f32[1,64,2048]{2,0,1:T(1,128)} %copy.148, f32[2,64,2048]{2,0,1:T(2,128)S(1)} %convert_select_fusion.1, f32[8]{0:T(128)S(1)} %pad.88.clone, ...), kind=kOutput, calls=%fused_computation.20 | convolution fusion | flops 74449408 | bytes 16777408 | tf_op jit(solution)/shard_map/dot_general | solution.py:274
  (133 shorter events, 85.8 us)
Async XLA Ops:
  7.2 2.2 copy-start.5
  7.2 121.3 %all-reduce.18.cloned.1.call-start = ((), (), s32[]{:S(2)}) async-start(), calls=%async_computation.4 | async-start | bytes 2097152 | tf_op jit(solution)/shard_map/psum | solution.py:36
  9.4 11.7 %copy-start.10 = (s32[256,3]{0,1:T(4,128)S(1)}, s32[256,3]{0,1:T(4,128)}, u32[]{:S(2)}) copy-start(s32[256,3]{0,1:T(4,128)} %param.11) | copy-start | bytes 9220
  9.5 1.9 copy-start
  11.6 44.0 %collective-permute-start.1 = (bf16[64,4096]{1,0:T(8,128)(2,1)S(1)}, bf16[64,4096]{1,0:T(8,128)(2,1)S(1)}, u32[]{:S(2)}, u32[]{:S(2)}) collective-permute-start(bf16[64,4096]{1,0:T(8,128)(2,1)S(1)} %get-tuple-element.80), channel_id=1, source_target_pairs={{1,0},{2,1},{3,2},{4,3},{5,4},{6,5},{7,6},{8,7},{9,8},{10,9},{11,1... | collective-permute-start | bytes 1572872 | tf_op jit(solution)/shard_map/ppermute | solution.py:29
  16.8 38.7 %collective-permute-start = (bf16[64,4096]{1,0:T(8,128)(2,1)S(1)}, bf16[64,4096]{1,0:T(8,128)(2,1)S(1)}, u32[]{:S(2)}, u32[]{:S(2)}) collective-permute-start(bf16[64,4096]{1,0:T(8,128)(2,1)S(1)} %get-tuple-element.79), channel_id=1, source_target_pairs={{0,1},{1,2},{2,3},{3,4},{4,5},{5,6},{6,7},{7,8},{8,9},{9,10},{10,1... | collective-permute-start | bytes 1572872 | tf_op jit(solution)/shard_map/ppermute | solution.py:26
  21.8 10.8 %copy-start.11 = (pred[32]{0:T(512)(128)(4,1)}, pred[32]{0:T(512)(128)(4,1)S(1)}, u32[]{:S(2)}) copy-start(pred[32]{0:T(512)(128)(4,1)S(1)} %get-tuple-element.61) | copy-start | bytes 100
  21.9 10.6 %copy-start.14 = (s32[32]{0:T(128)}, s32[32]{0:T(128)S(1)}, u32[]{:S(2)}) copy-start(s32[32]{0:T(128)S(1)} %select_reduce_fusion) | copy-start | bytes 388
  22.4 230.1 %copy-start.13 = (s32[24]{0:T(128)}, s32[24]{0:T(128)S(1)}, u32[]{:S(2)}) copy-start(s32[24]{0:T(128)S(1)} %fusion.56.slots_ref) | copy-start | bytes 292
  128.5 118.1 %all-to-all-start = ((bf16[32,64,2048]{2,1,0:T(8,128)(2,1)}), bf16[32,64,2048]{2,1,0:T(8,128)(2,1)}, u32[]{:S(2)}, u32[]{:S(2)}) async-start(bf16[32,64,2048]{2,1,0:T(8,128)(2,1)} %pad_maximum_fusion), calls=%async_computation | async-start | bytes 16777216 | tf_op jit(solution)/shard_map/all_to_all | solution.py:246
  246.6 115.8 %all-to-all-start.1 = ((bf16[32,64,2048]{2,1,0:T(8,128)(2,1)}), bf16[32,64,2048]{2,1,0:T(8,128)(2,1)}, u32[]{:S(2)}, u32[]{:S(2)}) async-start(bf16[32,64,2048]{2,1,0:T(8,128)(2,1)} %pad_maximum_fusion.1), calls=%async_computation.1 | async-start | bytes 16777216 | tf_op jit(solution)/shard_map/all_to_all | solution.py:246
  442.1 115.1 %all-to-all-start.3 = ((bf16[32,64,2048]{2,1,0:T(8,128)(2,1)}), bf16[32,64,2048]{2,1,0:T(8,128)(2,1)}, u32[]{:S(2)}, u32[]{:S(2)}) async-start(bf16[32,64,2048]{2,1,0:T(8,128)(2,1)} %get-tuple-element.98), calls=%async_computation.3 | async-start | bytes 16777216 | tf_op jit(solution)/shard_map/all_to_all | solution.py:273
  557.3 289.0 %all-to-all-start.2 = ((bf16[32,64,2048]{2,1,0:T(8,128)(2,1)}), bf16[32,64,2048]{2,1,0:T(8,128)(2,1)}, u32[]{:S(2)}, u32[]{:S(2)}) async-start(bf16[32,64,2048]{2,1,0:T(8,128)(2,1)} %get-tuple-element.97), calls=%async_computation.2 | async-start | bytes 16777216 | tf_op jit(solution)/shard_map/all_to_all | solution.py:273
  562.4 261.6 %all-reduce.20.cloned.1.call-start = ((), (), s32[]{:S(2)}) async-start(), calls=%async_computation.5 | async-start | bytes 2097152 | tf_op jit(solution)/shard_map/psum | solution.py:265
  567.1 2.5 copy-start.2
  567.1 2.5 copy-start.3
  577.2 92.0 %collective-permute-start.3 = (bf16[64,2048]{1,0:T(8,128)(2,1)S(1)}, bf16[64,2048]{1,0:T(8,128)(2,1)S(1)}, u32[]{:S(2)}, u32[]{:S(2)}) collective-permute-start(bf16[64,2048]{1,0:T(8,128)(2,1)S(1)} %pad_maximum_fusion.21), channel_id=1, source_target_pairs={{1,0},{2,1},{3,2},{4,3},{5,4},{6,5},{7,6},{8,7},{9,8},{10,9},{11,1... | collective-permute-start | bytes 786440 | tf_op jit(solution)/shard_map/ppermute | solution.py:29
  580.0 91.3 %collective-permute-start.2 = (bf16[64,2048]{1,0:T(8,128)(2,1)S(1)}, bf16[64,2048]{1,0:T(8,128)(2,1)S(1)}, u32[]{:S(2)}, u32[]{:S(2)}) collective-permute-start(bf16[64,2048]{1,0:T(8,128)(2,1)S(1)} %pad_maximum_fusion.20), channel_id=1, source_target_pairs={{0,1},{1,2},{2,3},{3,4},{4,5},{5,6},{6,7},{7,8},{8,9},{9,10},{10,1... | collective-permute-start | bytes 786440 | tf_op jit(solution)/shard_map/ppermute | solution.py:26
  588.7 5.6 copy-start.1
  694.3 2.8 copy-start.4
  699.1 22.8 %collective-permute-start.5 = (bf16[64,2048]{1,0:T(8,128)(2,1)S(1)}, bf16[64,2048]{1,0:T(8,128)(2,1)}, u32[]{:S(2)}, u32[]{:S(2)}) collective-permute-start(bf16[64,2048]{1,0:T(8,128)(2,1)S(1)} %pad_maximum_fusion.23), channel_id=1, source_target_pairs={{1,0},{2,1},{3,2},{4,3},{5,4},{6,5},{7,6},{8,7},{9,8},{10,9},{11,1... | collective-permute-start | bytes 786440 | tf_op jit(solution)/shard_map/ppermute | solution.py:29
  703.6 18.3 %collective-permute-start.4 = (bf16[64,2048]{1,0:T(8,128)(2,1)}, bf16[64,2048]{1,0:T(8,128)(2,1)}, u32[]{:S(2)}, u32[]{:S(2)}) collective-permute-start(bf16[64,2048]{1,0:T(8,128)(2,1)} %pad_maximum_fusion.22), channel_id=1, source_target_pairs={{0,1},{1,2},{2,3},{3,4},{4,5},{5,6},{6,7},{7,8},{8,9},{9,10},{10,1... | collective-permute-start | bytes 786440 | tf_op jit(solution)/shard_map/ppermute | solution.py:26
  714.0 4.1 copy-start.7
  714.1 4.1 copy-start.9
  718.1 1.5 copy-start.6
  718.1 2.3 copy-start.8
  721.9 105.3 %copy-start.12 = (pred[32]{0:T(512)(128)(4,1)S(1)}, pred[32]{0:T(512)(128)(4,1)}, u32[]{:S(2)}) copy-start(pred[32]{0:T(512)(128)(4,1)} %copy-done.11) | copy-start | bytes 100
  721.9 105.3 %copy-start.15 = (s32[32]{0:T(128)S(1)}, s32[32]{0:T(128)}, u32[]{:S(2)}) copy-start(s32[32]{0:T(128)} %copy-done.14) | copy-start | bytes 388
Sparse Core Ops, SparseCore 0:
  21.2 107.2 all-reduce.17
  714.2 109.7 all-reduce.19

commit v6 on v3

--- a/solution.py
+++ b/solution.py
@@ -30,9 +30,22 @@
     return block
 
 
-def from_root(value, axis, source):
-    kept = jnp.where(lax.axis_index(axis) == source, value, 0).astype(value.dtype)
-    return lax.psum(kept, axis)
+def spread(pieces, axis):
+    return lax.all_to_all(pieces, axis, split_axis=0, concat_axis=0, tiled=True)
+
+
+def from_root(value, axis):
+    n = lax.axis_size(axis)
+    pieces = value.reshape(n, -1)
+    mine = spread(pieces, axis)[0]
+    return spread(jnp.broadcast_to(mine[None], pieces.shape), axis).reshape(value.shape)
+
+
+def sum_all(value, axis):
+    n = lax.axis_size(axis)
+    pieces = value.reshape(n, -1)
+    mine = jnp.sum(spread(pieces, axis).astype(jnp.float32), axis=0).astype(value.dtype)
+    return spread(jnp.broadcast_to(mine[None], pieces.shape), axis).reshape(value.shape)
 
 
 def scores_kernel(
@@ -187,7 +200,7 @@
     span = (5 + R) * BS
     pair = jnp.concatenate([key, value], axis=1)
     padded = extended(pair, ((("head", "blk"), 0),), BS)
-    glob = from_root(pair[: 2 * BS], ("head", "blk"), 0)
+    glob = from_root(pair[: 2 * BS], ("head", "blk"))
     flat = rand.reshape(ndev, nbd * R)
     owner = flat // nbd
     local = flat - owner * nbd
@@ -234,7 +247,7 @@
     glob_grad = jnp.concatenate([jnp.sum(gk, axis=0), jnp.sum(gv, axis=0)], axis=-1).reshape(
         2, BS, 2 * width
     )
-    glob_total = lax.psum(glob_grad.astype(jnp.bfloat16), ("head", "blk")).astype(pf)
+    glob_total = sum_all(glob_grad.astype(jnp.bfloat16), ("head", "blk")).astype(pf)
     edge = jnp.concatenate(
         [arrived[None, :BS], jnp.zeros((nbd - 2, BS, 2 * width), pf), arrived[None, 3 * BS :]], axis=0
     )

time: 830 us -> 870 us (1.048)
  other arithmetic: 86 us -> 123 us
  waiting for transfers between devices: 447 us -> 420 us
  starting transfers between devices: 27.7 us -> 52.6 us
  local copies, waits for them, and re-layouts: 67.5 us -> 91 us
  between operations: 14.8 us -> 1.27 us
    psum x2 -> x0, waiting for transfers between devices: 76 us -> none  [the longest x1 41.4 us: body(): lax.psum(glob_grad.astype(jnp.bfloat16), ('head', 'blk')).astype(pf)]
    ppermute x2, waiting for transfers between devices: 353 us -> 384 us  [extended(): lax.ppermute(lax.slice_in_dim(block, 0, width, axis=dim), axis, backward)]
    all_to_all x0 -> x4, starting transfers between devices: none -> 26.8 us  [spread(): return lax.all_to_all(pieces, axis, split_axis=0, concat_axis=0, tiled=True)]
    broadcast_in_dim x0 -> x2, other arithmetic: none -> 14.1 us  [the longest x1 7.05 us: from_root(): jnp.broadcast_to(mine[None], pieces.shape)]
    all_to_all x0 -> x2, other arithmetic: none -> 13.5 us  [spread(): return lax.all_to_all(pieces, axis, split_axis=0, concat_axis=0, tiled=True)]
    unnamed x10 -> x28, local copies, waits for them, and re-layouts: 4.61 us -> 15.9 us
    ppermute x2, waiting for transfers between devices: 18.2 us -> 29.4 us  [extended(): lax.ppermute(lax.slice_in_dim(block, block.shape[dim] - width, None, axis...]
  transfers between devices with their start and end apart: 8 -> 10, of which waited for: 6 -> 7; matrix products, arithmetic and copies ran while one was open for 10% -> 17% of each run, Pallas kernels for 4% -> 0%
where the time goes in v6:
time: 870 us; the launch traced here: 862 us
  waiting for transfers between devices  420 us (48%)
  Pallas kernels  137 us (16%)
  other arithmetic  123 us (14%)
  local copies, waits for them, and re-layouts  91 us (10%)
  starting transfers between devices  52.6 us (6%)
  matrix products  36.3 us (4%)
    ppermute x2, waiting for transfers between devices, extended(): lax.ppermute(lax.slice_in_dim(block, 0, width, axis=dim), axis, backward)  384 us
    pallas_call x1, Pallas kernels, attention(): pl.pallas_call(scores_kernel, grid_spec=grid_spec, out_shape=out_shape, i...  104 us
    dot_general x1, matrix products, body(): jnp.dot(onehot, back.reshape(ndev * cap, BS * 2 * width), preferred_eleme...  36.3 us
    pallas_call x1, Pallas kernels, attention(): pl.pallas_call(terms_kernel, grid=(nbd, groups), in_specs=[row2, row2, pr...  32.1 us
    ppermute x2, waiting for transfers between devices, extended(): lax.ppermute(lax.slice_in_dim(block, block.shape[dim] - width, None, axis...  29.4 us
    all_to_all x4, starting transfers between devices, spread(): return lax.all_to_all(pieces, axis, split_axis=0, concat_axis=0, tiled=True)  26.8 us
    squeeze x2, local copies, waits for them, and re-layouts, overlap(): w4[:, 0]  19.2 us
  transfers between devices with their start and end apart: 10, of which 7 were waited for; matrix products, arithmetic and copies ran while one was open for 17% of the time, Pallas kernels for 0%

profile of v6, /device:TPU:14, one launch (start us, length us, event | category | flops | bytes accessed | tf_op | source)
XLA Modules:
  0.0 861.6 jit_solution(323516072907869943)
XLA Ops:
  7.6 7.0 reduce.28
  16.2 9.0 %all-to-all-start = ((bf16[32,2,8192]{2,1,0:T(2,128)(2,1)}), bf16[32,2,8192]{2,1,0:T(2,128)(2,1)S(1)}, u32[]{:S(2)}, u32[]{:S(2)}) async-start(bf16[32,2,8192]{2,1,0:T(2,128)(2,1)} %reshape.372), calls=%async_computation | async-start | bytes 2097152 | tf_op jit(solution)/shard_map/all_to_all | solution.py:34
  27.1 9.4 %gather_fusion = bf16[32,64,4096]{2,1,0:T(8,128)(2,1)} fusion(bf16[8,64,4096]{2,1,0:T(8,128)(2,1)} %bitcast.65, s32[1024]{0:T(1024)S(1)} %get-tuple-element.51), kind=kCustom, calls=%fused_computation | custom fusion | bytes 33554560 | tf_op jit(solution)/shard_map/jit(_take)/gather | solution.py:215
  43.8 7.0 reduce.29
  52.5 5.2 all-to-all-start.1
  57.7 14.3 %select_select_fusion.1 = bf16[32,64,4096]{2,1,0:T(8,128)(2,1)} fusion(bf16[32,64,4096]{2,1,0:T(8,128)(2,1)} %gather_fusion, pred[32]{0:T(512)(128)(4,1)S(1)} %compare_and_fusion.1, pred[32]{0:T(512)(128)(4,1)S(1)} %get-tuple-element.30), kind=kLoop, calls=%fused_computation.6 | loop fusion | flops 16777216 | bytes 33554496 | tf_op jit(solution)/shard_map/jit(_where)/select_n | solution.py:214
  73.5 6.4 all-to-all-start.2
  81.1 4.3 collective-permute-start.1
  88.8 216.0 %collective-permute-done.1 = bf16[64,4096]{1,0:T(8,128)(2,1)S(1)} collective-permute-done((bf16[64,4096]{1,0:T(8,128)(2,1)S(1)}, bf16[64,4096]{1,0:T(8,128)(2,1)S(1)}, u32[]{:S(2)}, u32[]{:S(2)}) %collective-permute-start.1) | collective-permute-done | bytes 524320 | tf_op jit(solution)/shard_map/ppermute | solution.py:28
  304.8 14.7 %collective-permute-done = bf16[64,4096]{1,0:T(8,128)(2,1)S(1)} collective-permute-done((bf16[64,4096]{1,0:T(8,128)(2,1)S(1)}, bf16[64,4096]{1,0:T(8,128)(2,1)S(1)}, u32[]{:S(2)}, u32[]{:S(2)}) %collective-permute-start) | collective-permute-done | bytes 524320 | tf_op jit(solution)/shard_map/ppermute | solution.py:25
  319.5 5.7 pad_maximum_fusion.2.kw0.kw1.kw2.vw0.vw1.vw2
  326.2 6.4 reduce.23
  334.3 104.4 %shard_map.84 = (bf16[512,2048]{1,0:T(8,128)(2,1)}, bf16[512,2048]{1,0:T(8,128)(2,1)}, bf16[8,192,2048]{2,1,0:T(8,128)(2,1)}, bf16[8,192,2048]{2,1,0:T(8,128)(2,...) custom-call(s32[24]{0:T(128)} %copy-done.7, bf16[512,2048]{1,0:T(8,128)(2,1)} %q_ref.3, ...), custom_call_target="tpu_custom_call" | custom-call | tf_op jit(solution)/shard_map/pallas_call | solution.py:153
  438.7 32.1 %shard_map.85 = (f32[8,192,2048]{2,1,0:T(8,128)}, f32[8,192,2048]{2,1,0:T(8,128)}, f32[8,128,2048]{2,1,0:T(8,128)}, f32[8,128,2048]{2,1,0:T(8,128)}) custom-call(bf16[512,2048]{1,0:T(8,128)(2,1)} %q_ref.3, bf16[512,2048]{1,0:T(8,128)(2,1)} %do_ref.3, bf16[8,16,64,320]{3,2,1,0:T(8,128)(2,1)} %get-tuple-element.17.pb_ref, ...), custom_call_target="tpu_custom_call" | custom-call | tf_op jit(solution)/shard_map/pallas_call | solution.py:166
  481.4 7.0 reduce.30
  490.0 5.0 all-to-all-start.3
  495.1 10.6 %pad_maximum_fusion = bf16[8,192,4096]{2,1,0:T(8,128)(2,1)} fusion(bf16[8,192,2048]{2,1,0:T(8,128)(2,1)} %get-tuple-element.25, bf16[8,192,2048]{2,1,0:T(8,128)(2,1)} %get-tuple-element.24), kind=kLoop, calls=%fused_computation.7 | loop fusion | flops 25165824 | bytes 25165824 | tf_op jit(solution)/shard_map/concatenate | solution.py:256
  505.7 11.8 %gather_fusion.1 = bf16[32,64,4096]{2,1,0:T(8,128)(2,1)} fusion(bf16[24,64,4096]{2,1,0:T(8,128)(2,1)} %bitcast.66, s32[1024]{0:T(1024)S(1)} %get-tuple-element.50), kind=kCustom, calls=%fused_computation.1 | custom fusion | bytes 33554560 | tf_op jit(solution)/shard_map/jit(_take)/gather | solution.py:261
  522.5 7.0 reduce.31
  531.1 7.7 all-to-all-start.4
  538.8 14.3 %select_select_fusion = bf16[32,64,4096]{2,1,0:T(8,128)(2,1)} fusion(bf16[32,64,4096]{2,1,0:T(8,128)(2,1)} %gather_fusion.1, pred[32]{0:T(512)(128)(4,1)S(1)} %compare_and_fusion, pred[32]{0:T(512)(128)(4,1)S(1)} %fusion.19), kind=kLoop, calls=%fused_computation.5 | loop fusion | flops 16777216 | bytes 33554496 | tf_op jit(solution)/shard_map/jit(_where)/select_n | solution.py:259
  554.4 6.4 all-to-all-start.5
  560.9 9.6 %slice_bitcast_fusion.2 = (f32[8,64,2048]{2,1,0:T(8,128)}, f32[8,64,2048]{2,1,0:T(8,128)}, f32[8,64,2048]{2,1,0:T(8,128)}) fusion(f32[8,3,64,2048]{3,2,1,0:T(8,128)} %bitcast.68), kind=kLoop, calls=%fused_computation.18 | loop fusion | bytes 25165824 | tf_op jit(solution)/shard_map/squeeze | solution.py:186
  570.5 7.7 fusion.31
  578.2 9.6 %slice_bitcast_fusion.5 = (f32[8,64,2048]{2,1,0:T(8,128)}, f32[8,64,2048]{2,1,0:T(8,128)}, f32[8,64,2048]{2,1,0:T(8,128)}) fusion(f32[8,3,64,2048]{3,2,1,0:T(8,128)} %bitcast.67), kind=kLoop, calls=%fused_computation.21 | loop fusion | bytes 25165824 | tf_op jit(solution)/shard_map/squeeze | solution.py:186
  587.8 8.2 fusion.30
  598.3 4.3 collective-permute-start.3
  611.3 6.4 pad_maximum_fusion.1
  617.7 168.0 %collective-permute-done.3 = bf16[64,4096]{1,0:T(8,128)(2,1)} collective-permute-done((bf16[64,4096]{1,0:T(8,128)(2,1)S(1)}, bf16[64,4096]{1,0:T(8,128)(2,1)}, u32[]{:S(2)}, u32[]{:S(2)}) %collective-permute-start.3) | collective-permute-done | bytes 524320 | tf_op jit(solution)/shard_map/ppermute | solution.py:28
  785.8 14.8 %collective-permute-done.2 = bf16[64,4096]{1,0:T(8,128)(2,1)} collective-permute-done((bf16[64,4096]{1,0:T(8,128)(2,1)}, bf16[64,4096]{1,0:T(8,128)(2,1)}, u32[]{:S(2)}, u32[]{:S(2)}) %collective-permute-start.2) | collective-permute-done | bytes 524320 | tf_op jit(solution)/shard_map/ppermute | solution.py:25
  807.2 7.4 fusion.8
  819.5 36.3 %fusion.5 = bf16[8,64,4096]{2,0,1:T(8,128)(2,1)S(1)} fusion(f32[1,64,4096]{2,0,1:T(1,128)S(1)} %copy-done.3, f32[1,64,4096]{2,0,1:T(1,128)} %copy.78, f32[8,64,4096]{2,1,0:T(8,128)} %pad_maximum_fusion.1, f32[2,64,4096]{2,0,1:T(2,128)} %copy.81, f32[8]{0:T(128)S(1)} %pad.37.clone, s32[32]{0:T(128)S(1)} %copy-done.6, ...), kind=kOutput, calls=%fused_computation.12 | convolution fusion | flops 146801152 | bytes 33554624 | tf_op jit(solution)/shard_map/dot_general | solution.py:268
  (92 shorter events, 76.1 us)
Async XLA Ops:
  0.6 2.2 copy-start.2
  3.1 2.0 copy-start
  5.2 20.0 %copy-start.4 = (s32[256,3]{0,1:T(4,128)S(1)}, s32[256,3]{0,1:T(4,128)}, u32[]{:S(2)}) copy-start(s32[256,3]{0,1:T(4,128)} %param.9) | copy-start | bytes 9220
  16.2 24.5 %all-to-all-start = ((bf16[32,2,8192]{2,1,0:T(2,128)(2,1)}), bf16[32,2,8192]{2,1,0:T(2,128)(2,1)S(1)}, u32[]{:S(2)}, u32[]{:S(2)}) async-start(bf16[32,2,8192]{2,1,0:T(2,128)(2,1)} %reshape.372), calls=%async_computation | async-start | bytes 2097152 | tf_op jit(solution)/shard_map/all_to_all | solution.py:34
  26.0 10.5 %copy-start.7 = (s32[24]{0:T(128)}, s32[24]{0:T(128)S(1)}, u32[]{:S(2)}) copy-start(s32[24]{0:T(128)S(1)} %fusion.36.slots_ref) | copy-start | bytes 292
  26.5 10.1 %copy-start.5 = (s32[32]{0:T(128)}, s32[32]{0:T(128)S(1)}, u32[]{:S(2)}) copy-start(s32[32]{0:T(128)S(1)} %select_reduce_fusion) | copy-start | bytes 388
  52.5 21.0 %all-to-all-start.1 = ((bf16[32,2,8192]{2,1,0:T(2,128)(2,1)}), bf16[32,2,8192]{2,1,0:T(2,128)(2,1)S(1)}, u32[]{:S(2)}, u32[]{:S(2)}) async-start(bf16[32,2,8192]{2,1,0:T(2,128)(2,1)} %reshape.374), calls=%async_computation.1 | async-start | bytes 2097152 | tf_op jit(solution)/shard_map/all_to_all | solution.py:34
  73.5 260.8 %all-to-all-start.2 = ((bf16[32,64,4096]{2,1,0:T(8,128)(2,1)}), bf16[32,64,4096]{2,1,0:T(8,128)(2,1)}, u32[]{:S(2)}, u32[]{:S(2)}) async-start(bf16[32,64,4096]{2,1,0:T(8,128)(2,1)} %select_select_fusion.1), calls=%async_computation.2 | async-start | bytes 33554432 | tf_op jit(solution)/shard_map/all_to_all | solution.py:217
  81.1 223.7 %collective-permute-start.1 = (bf16[64,4096]{1,0:T(8,128)(2,1)S(1)}, bf16[64,4096]{1,0:T(8,128)(2,1)S(1)}, u32[]{:S(2)}, u32[]{:S(2)}) collective-permute-start(bf16[64,4096]{1,0:T(8,128)(2,1)S(1)} %get-tuple-element.41), channel_id=1, source_target_pairs={{1,0},{2,1},{3,2},{4,3},{5,4},{6,5},{7,6},{8,7},{9,8},{10,9},{11,1... | collective-permute-start | bytes 1572872 | tf_op jit(solution)/shard_map/ppermute | solution.py:28
  85.4 234.1 %collective-permute-start = (bf16[64,4096]{1,0:T(8,128)(2,1)S(1)}, bf16[64,4096]{1,0:T(8,128)(2,1)S(1)}, u32[]{:S(2)}, u32[]{:S(2)}) collective-permute-start(bf16[64,4096]{1,0:T(8,128)(2,1)S(1)} %get-tuple-element.40), channel_id=1, source_target_pairs={{0,1},{1,2},{2,3},{3,4},{4,5},{5,6},{6,7},{7,8},{8,9},{9,10},{10,1... | collective-permute-start | bytes 1572872 | tf_op jit(solution)/shard_map/ppermute | solution.py:25
  479.4 15.6 %copy-start.8 = (s32[24]{0:T(128)S(1)}, s32[24]{0:T(128)}, u32[]{:S(2)}) copy-start(s32[24]{0:T(128)} %copy-done.7) | copy-start | bytes 292
  490.0 27.5 %all-to-all-start.3 = ((bf16[32,2,8192]{2,1,0:T(2,128)(2,1)}), bf16[32,2,8192]{2,1,0:T(2,128)(2,1)S(1)}, u32[]{:S(2)}, u32[]{:S(2)}) async-start(bf16[32,2,8192]{2,1,0:T(2,128)(2,1)} %reshape.376), calls=%async_computation.3 | async-start | bytes 2097152 | tf_op jit(solution)/shard_map/all_to_all | solution.py:34
  531.1 23.3 %all-to-all-start.4 = ((bf16[32,2,8192]{2,1,0:T(2,128)(2,1)}), bf16[32,2,8192]{2,1,0:T(2,128)(2,1)S(1)}, u32[]{:S(2)}, u32[]{:S(2)}) async-start(bf16[32,2,8192]{2,1,0:T(2,128)(2,1)} %reshape.378), calls=%async_computation.4 | async-start | bytes 2097152 | tf_op jit(solution)/shard_map/all_to_all | solution.py:34
  554.4 265.1 %all-to-all-start.5 = ((bf16[32,64,4096]{2,1,0:T(8,128)(2,1)}), bf16[32,64,4096]{2,1,0:T(8,128)(2,1)}, u32[]{:S(2)}, u32[]{:S(2)}) async-start(bf16[32,64,4096]{2,1,0:T(8,128)(2,1)} %select_select_fusion), calls=%async_computation.5 | async-start | bytes 33554432 | tf_op jit(solution)/shard_map/all_to_all | solution.py:264
  598.3 187.5 %collective-permute-start.3 = (bf16[64,4096]{1,0:T(8,128)(2,1)S(1)}, bf16[64,4096]{1,0:T(8,128)(2,1)}, u32[]{:S(2)}, u32[]{:S(2)}) collective-permute-start(bf16[64,4096]{1,0:T(8,128)(2,1)S(1)} %pad_maximum_fusion.9), channel_id=1, source_target_pairs={{1,0},{2,1},{3,2},{4,3},{5,4},{6,5},{7,6},{8,7},{9,8},{10,9},{11,1... | collective-permute-start | bytes 1572872 | tf_op jit(solution)/shard_map/ppermute | solution.py:28
  603.4 197.1 %collective-permute-start.2 = (bf16[64,4096]{1,0:T(8,128)(2,1)}, bf16[64,4096]{1,0:T(8,128)(2,1)}, u32[]{:S(2)}, u32[]{:S(2)}) collective-permute-start(bf16[64,4096]{1,0:T(8,128)(2,1)} %pad_maximum_fusion.8), channel_id=1, source_target_pairs={{0,1},{1,2},{2,3},{3,4},{4,5},{5,6},{6,7},{7,8},{8,9},{9,10},{10,1... | collective-permute-start | bytes 1572872 | tf_op jit(solution)/shard_map/ppermute | solution.py:25
  607.6 3.7 copy-start.1
  814.6 4.9 copy-start.3
  814.6 4.9 copy-start.6

commit v7 on v6

--- a/solution.py
+++ b/solution.py
@@ -157,13 +157,23 @@
         interpret=INTERPRET,
     )(slots, *args)
 
+    return out, dq, rk, rv, pb, dsb
+
+
+def window_terms(query, dout, pb, dsb):
+    rows, width = query.shape
+    heads = width // HD
+    groups = heads // HG
+    cw = HG * HD
+    nbd = rows // BS
+    g = 5 * BS
     row2 = pl.BlockSpec((BS, cw), lambda n, h: (n, h))
     prob2 = pl.BlockSpec((1, HG, BS, g), lambda n, h: (n, h, 0, 0))
 
     def term_spec(size):
         return pl.BlockSpec((1, size, cw), lambda n, h: (n, 0, h))
 
-    wk, wv, gk, gv = pl.pallas_call(
+    return pl.pallas_call(
         terms_kernel,
         grid=(nbd, groups),
         in_specs=[row2, row2, prob2, prob2],
@@ -176,7 +186,6 @@
         ],
         interpret=INTERPRET,
     )(query, dout, pb, dsb)
-    return out, dq, wk, wv, gk, gv, rk, rv
 
 
 def overlap(terms, nbd):
@@ -232,7 +241,18 @@
         axis=1,
     )
     mask = jnp.repeat(valid, BS, axis=1).astype(pf).reshape(nbd, 1, span)
-    out, dq, wk, wv, gk, gv, rk, rv = attention(query, dout, mask, padded, glob, fetched, mine_slot)
+    out, dq, rk, rv, pb, dsb = attention(query, dout, mask, padded, glob, fetched, mine_slot)
+    rand_grad = jnp.concatenate([rk, rv], axis=-1).reshape(nbd * R, BS, 2 * width)
+    match = mine_slot[None, :] == jnp.arange(ndev * cap, dtype=jnp.int32)[:, None]
+    source = jnp.argmax(match, axis=1)
+    returning = jnp.where(
+        jnp.any(match, axis=1)[:, None, None],
+        jnp.take(rand_grad, source, axis=0),
+        jnp.zeros((), jnp.bfloat16),
+    )
+    back = lax.all_to_all(returning, ("head", "blk"), split_axis=0, concat_axis=0, tiled=True)
+    pb, dsb, _ = lax.optimization_barrier((pb, dsb, returning))
+    wk, wv, gk, gv = window_terms(query, dout, pb, dsb)
     sk = overlap(wk, nbd)
     sv = overlap(wv, nbd)
     rims = jnp.concatenate(
@@ -247,21 +267,13 @@
     glob_grad = jnp.concatenate([jnp.sum(gk, axis=0), jnp.sum(gv, axis=0)], axis=-1).reshape(
         2, BS, 2 * width
     )
+    glob_grad, _ = lax.optimization_barrier((glob_grad, back))
     glob_total = sum_all(glob_grad.astype(jnp.bfloat16), ("head", "blk")).astype(pf)
     edge = jnp.concatenate(
         [arrived[None, :BS], jnp.zeros((nbd - 2, BS, 2 * width), pf), arrived[None, 3 * BS :]], axis=0
     )
     lead = jnp.pad(jnp.where(me == 0, glob_total, 0.0), ((0, nbd - 2), (0, 0), (0, 0)))
     own = own + edge + lead
-    rand_grad = jnp.concatenate([rk, rv], axis=-1).reshape(nbd * R, BS, 2 * width)
-    match = mine_slot[None, :] == jnp.arange(ndev * cap, dtype=jnp.int32)[:, None]
-    source = jnp.argmax(match, axis=1)
-    returning = jnp.where(
-        jnp.any(match, axis=1)[:, None, None],
-        jnp.take(rand_grad, source, axis=0),
-        jnp.zeros((), jnp.bfloat16),
-    )
-    back = lax.all_to_all(returning, ("head", "blk"), split_axis=0, concat_axis=0, tiled=True)
     onehot = (
         (block_id[None, :] == jnp.arange(nbd, dtype=jnp.int32)[:, None]) & filled[None, :]
     ).astype(jnp.bfloat16)

time: 870 us -> 849 us (0.976)
  waiting for transfers between devices: 420 us -> 383 us
  starting transfers between devices: 52.6 us -> 64.4 us
    ppermute x2, waiting for transfers between devices: 384 us -> 0.01 us  [extended(): lax.ppermute(lax.slice_in_dim(block, 0, width, axis=dim), axis, backward)]
    ppermute x2, waiting for transfers between devices: 29.4 us -> 229 us  [extended(): lax.ppermute(lax.slice_in_dim(block, block.shape[dim] - width, None, axis...]
    all_to_all x1, waiting for transfers between devices: 0.01 us -> 146 us  [body(): lax.all_to_all(returning, ('head', 'blk'), split_axis=0, concat_axis=0, t...]
    all_to_all x4, starting transfers between devices: 26.8 us -> 37.1 us  [spread(): return lax.all_to_all(pieces, axis, split_axis=0, concat_axis=0, tiled=True)]
    all_to_all x2 -> x3, other arithmetic: 13.5 us -> 20.5 us  [spread(): return lax.all_to_all(pieces, axis, split_axis=0, concat_axis=0, tiled=True)]
  transfers between devices with their start and end apart: 10 -> 10, of which waited for: 7 -> 5; matrix products, arithmetic and copies ran while one was open for 17% -> 15% of each run, Pallas kernels for 0% -> 4%
where the time goes in v7:
time: 849 us; the launch traced here: 840 us
  waiting for transfers between devices  383 us (45%)
  Pallas kernels  137 us (16%)
  other arithmetic  126 us (15%)
  local copies, waits for them, and re-layouts  92.5 us (11%)
  starting transfers between devices  64.4 us (8%)
  matrix products  36.1 us (4%)
    ppermute x2, waiting for transfers between devices, extended(): lax.ppermute(lax.slice_in_dim(block, block.shape[dim] - width, None, axis...  229 us
    all_to_all x1, waiting for transfers between devices, body(): lax.all_to_all(returning, ('head', 'blk'), split_axis=0, concat_axis=0, t...  146 us
    pallas_call x1, Pallas kernels, attention(): pl.pallas_call(scores_kernel, grid_spec=grid_spec, out_shape=out_shape, i...  104 us
    all_to_all x4, starting transfers between devices, spread(): return lax.all_to_all(pieces, axis, split_axis=0, concat_axis=0, tiled=True)  37.1 us
    dot_general x1, matrix products, body(): jnp.dot(onehot, back.reshape(ndev * cap, BS * 2 * width), preferred_eleme...  36.1 us
    pallas_call x1, Pallas kernels, window_terms(): pl.pallas_call(terms_kernel, grid=(nbd, groups), in_specs=[row2, row2, pr...  32.1 us
    all_to_all x3, other arithmetic, spread(): return lax.all_to_all(pieces, axis, split_axis=0, concat_axis=0, tiled=True)  20.5 us
    squeeze x2, local copies, waits for them, and re-layouts, overlap(): w4[:, 0]  19.4 us
  transfers between devices with their start and end apart: 10, of which 5 were waited for; matrix products, arithmetic and copies ran while one was open for 15% of the time, Pallas kernels for 4%

profile of v7, /device:TPU:14, one launch (start us, length us, event | category | flops | bytes accessed | tf_op | source)
XLA Modules:
  0.0 839.7 jit_solution(8218890600961035291)
XLA Ops:
  7.6 7.0 reduce.28
  16.2 8.9 %all-to-all-start = ((bf16[32,2,8192]{2,1,0:T(2,128)(2,1)}), bf16[32,2,8192]{2,1,0:T(2,128)(2,1)S(1)}, u32[]{:S(2)}, u32[]{:S(2)}) async-start(bf16[32,2,8192]{2,1,0:T(2,128)(2,1)} %reshape.364), calls=%async_computation | async-start | bytes 2097152 | tf_op jit(solution)/shard_map/all_to_all | solution.py:34
  27.0 9.4 %gather_fusion = bf16[32,64,4096]{2,1,0:T(8,128)(2,1)} fusion(bf16[8,64,4096]{2,1,0:T(8,128)(2,1)} %bitcast.66, s32[1024]{0:T(1024)S(1)} %get-tuple-element.57), kind=kCustom, calls=%fused_computation | custom fusion | bytes 33554560 | tf_op jit(solution)/shard_map/jit(_take)/gather | solution.py:224
  36.4 4.3 all-to-all-done
  43.8 7.0 reduce.29
  52.4 5.2 all-to-all-start.1
  57.6 14.3 %select_select_fusion.1 = bf16[32,64,4096]{2,1,0:T(8,128)(2,1)} fusion(bf16[32,64,4096]{2,1,0:T(8,128)(2,1)} %gather_fusion, pred[32]{0:T(512)(128)(4,1)S(1)} %compare_and_fusion.1, pred[32]{0:T(512)(128)(4,1)S(1)} %get-tuple-element.36), kind=kLoop, calls=%fused_computation.6 | loop fusion | flops 16777216 | bytes 33554496 | tf_op jit(solution)/shard_map/jit(_where)/select_n | solution.py:223
  73.4 6.4 all-to-all-start.2
  84.4 4.7 collective-permute-start.1
  90.2 229.3 %collective-permute-done = bf16[64,4096]{1,0:T(8,128)(2,1)S(1)} collective-permute-done((bf16[64,4096]{1,0:T(8,128)(2,1)S(1)}, bf16[64,4096]{1,0:T(8,128)(2,1)S(1)}, u32[]{:S(2)}, u32[]{:S(2)}) %collective-permute-start) | collective-permute-done | bytes 524320 | tf_op jit(solution)/shard_map/ppermute | solution.py:25
  319.4 5.7 pad_maximum_fusion.2.kw0.kw1.kw2.vw0.vw1.vw2
  326.1 6.4 reduce.23
  334.2 104.4 %shard_map.84 = (bf16[512,2048]{1,0:T(8,128)(2,1)}, bf16[512,2048]{1,0:T(8,128)(2,1)}, bf16[8,192,2048]{2,1,0:T(8,128)(2,1)}, bf16[8,192,2048]{2,1,0:T(8,128)(2,...) custom-call(s32[24]{0:T(128)} %copy-done.12, bf16[512,2048]{1,0:T(8,128)(2,1)} %q_ref.3, ...), custom_call_target="tpu_custom_call" | custom-call | tf_op jit(solution)/shard_map/pallas_call | solution.py:153
  438.6 10.6 %pad_maximum_fusion = bf16[8,192,4096]{2,1,0:T(8,128)(2,1)} fusion(bf16[8,192,2048]{2,1,0:T(8,128)(2,1)} %get-tuple-element.24, bf16[8,192,2048]{2,1,0:T(8,128)(2,1)} %get-tuple-element.23), kind=kLoop, calls=%fused_computation.7 | loop fusion | flops 25165824 | bytes 25165824 | tf_op jit(solution)/shard_map/concatenate | solution.py:245
  449.2 11.8 %gather_fusion.1 = bf16[32,64,4096]{2,1,0:T(8,128)(2,1)} fusion(bf16[24,64,4096]{2,1,0:T(8,128)(2,1)} %bitcast.67, s32[1024]{0:T(1024)S(1)} %get-tuple-element.56), kind=kCustom, calls=%fused_computation.1 | custom fusion | bytes 33554560 | tf_op jit(solution)/shard_map/jit(_take)/gather | solution.py:250
  461.1 14.3 %select_select_fusion = bf16[32,64,4096]{2,1,0:T(8,128)(2,1)} fusion(bf16[32,64,4096]{2,1,0:T(8,128)(2,1)} %gather_fusion.1, pred[32]{0:T(512)(128)(4,1)S(1)} %compare_and_fusion, pred[32]{0:T(512)(128)(4,1)S(1)} %fusion.19), kind=kLoop, calls=%fused_computation.5 | loop fusion | flops 16777216 | bytes 33554496 | tf_op jit(solution)/shard_map/jit(_where)/select_n | solution.py:248
  475.3 5.1 all-to-all-start.3
  480.6 32.1 %shard_map.85 = (f32[8,192,2048]{2,1,0:T(8,128)}, f32[8,192,2048]{2,1,0:T(8,128)}, f32[8,128,2048]{2,1,0:T(8,128)}, f32[8,128,2048]{2,1,0:T(8,128)}) custom-call(bf16[512,2048]{1,0:T(8,128)(2,1)} %q_ref.3, bf16[512,2048]{1,0:T(8,128)(2,1)} %do_ref.3, bf16[8,16,64,320]{3,2,1,0:T(8,128)(2,1)} %get-tuple-element.25.pb_ref, ...), custom_call_target="tpu_custom_call" | custom-call | tf_op jit(solution)/shard_map/pallas_call | solution.py:176
  521.2 9.7 %slice_bitcast_fusion.5 = (f32[8,64,2048]{2,1,0:T(8,128)S(1)}, f32[8,64,2048]{2,1,0:T(8,128)}, f32[8,64,2048]{2,1,0:T(8,128)}) fusion(f32[8,3,64,2048]{3,2,1,0:T(8,128)} %bitcast.71), kind=kLoop, calls=%fused_computation.21 | loop fusion | bytes 25165824 | tf_op jit(solution)/shard_map/squeeze | solution.py:195
  530.8 8.2 fusion.30
  539.1 9.7 %slice_bitcast_fusion.2 = (f32[8,64,2048]{2,1,0:T(8,128)S(1)}, f32[8,64,2048]{2,1,0:T(8,128)}, f32[8,64,2048]{2,1,0:T(8,128)}) fusion(f32[8,3,64,2048]{3,2,1,0:T(8,128)} %bitcast.70), kind=kLoop, calls=%fused_computation.18 | loop fusion | bytes 25165824 | tf_op jit(solution)/shard_map/squeeze | solution.py:195
  548.8 8.2 fusion.31
  558.8 145.6 %all-to-all-done.3 = bf16[32,64,4096]{2,1,0:T(8,128)(2,1)} async-done(((bf16[32,64,4096]{2,1,0:T(8,128)(2,1)}), bf16[32,64,4096]{2,1,0:T(8,128)(2,1)}, u32[]{:S(2)}, u32[]{:S(2)}) %all-to-all-start.3) | async-done | bytes 16777248 | tf_op jit(solution)/shard_map/all_to_all | solution.py:253
  706.4 7.0 reduce.30
  715.0 17.2 %all-to-all-start.4 = ((bf16[32,2,8192]{2,1,0:T(2,128)(2,1)}), bf16[32,2,8192]{2,1,0:T(2,128)(2,1)S(1)}, u32[]{:S(2)}, u32[]{:S(2)}) async-start(bf16[32,2,8192]{2,1,0:T(2,128)(2,1)} %reshape.368), calls=%async_computation.4 | async-start | bytes 2097152 | tf_op jit(solution)/shard_map/all_to_all | solution.py:34
  733.5 5.0 slice.103
  745.8 4.3 collective-permute-start.3
  755.5 7.0 reduce.31
  764.2 5.8 all-to-all-start.5
  770.0 7.7 pad_maximum_fusion.1
  786.6 7.4 fusion.8
  797.6 36.1 %fusion.5 = bf16[8,64,4096]{2,0,1:T(8,128)(2,1)S(1)} fusion(f32[1,64,4096]{2,0,1:T(1,128)S(1)} %copy-done.8, f32[1,64,4096]{2,0,1:T(1,128)} %copy.78, f32[8,64,4096]{2,1,0:T(8,128)} %pad_maximum_fusion.1, f32[2,64,4096]{2,0,1:T(2,128)S(1)} %copy.81, f32[8]{0:T(128)S(1)} %pad.35.clone, s32[32]{0:T(128)S(1)} %copy-done.11, ...), kind=kOutput, calls=%fused_computation.12 | convolution fusion | flops 146801152 | bytes 33554624 | tf_op jit(solution)/shard_map/dot_general | solution.py:280
  (105 shorter events, 72.1 us)
Async XLA Ops:
  0.6 2.2 copy-start.7
  3.1 2.0 copy-start
  5.2 19.9 %copy-start.9 = (s32[256,3]{0,1:T(4,128)S(1)}, s32[256,3]{0,1:T(4,128)}, u32[]{:S(2)}) copy-start(s32[256,3]{0,1:T(4,128)} %param.9) | copy-start | bytes 9220
  16.2 24.5 %all-to-all-start = ((bf16[32,2,8192]{2,1,0:T(2,128)(2,1)}), bf16[32,2,8192]{2,1,0:T(2,128)(2,1)S(1)}, u32[]{:S(2)}, u32[]{:S(2)}) async-start(bf16[32,2,8192]{2,1,0:T(2,128)(2,1)} %reshape.364), calls=%async_computation | async-start | bytes 2097152 | tf_op jit(solution)/shard_map/all_to_all | solution.py:34
  25.9 64.2 %copy-start.12 = (s32[24]{0:T(128)}, s32[24]{0:T(128)S(1)}, u32[]{:S(2)}) copy-start(s32[24]{0:T(128)S(1)} %fusion.36.slots_ref) | copy-start | bytes 292
  26.4 10.0 %copy-start.10 = (s32[32]{0:T(128)}, s32[32]{0:T(128)S(1)}, u32[]{:S(2)}) copy-start(s32[32]{0:T(128)S(1)} %select_reduce_fusion) | copy-start | bytes 388
  52.4 21.0 %all-to-all-start.1 = ((bf16[32,2,8192]{2,1,0:T(2,128)(2,1)}), bf16[32,2,8192]{2,1,0:T(2,128)(2,1)S(1)}, u32[]{:S(2)}, u32[]{:S(2)}) async-start(bf16[32,2,8192]{2,1,0:T(2,128)(2,1)} %reshape.366), calls=%async_computation.1 | async-start | bytes 2097152 | tf_op jit(solution)/shard_map/all_to_all | solution.py:34
  73.4 260.8 %all-to-all-start.2 = ((bf16[32,64,4096]{2,1,0:T(8,128)(2,1)}), bf16[32,64,4096]{2,1,0:T(8,128)(2,1)}, u32[]{:S(2)}, u32[]{:S(2)}) async-start(bf16[32,64,4096]{2,1,0:T(8,128)(2,1)} %select_select_fusion.1), calls=%async_computation.2 | async-start | bytes 33554432 | tf_op jit(solution)/shard_map/all_to_all | solution.py:226
  81.0 238.4 %collective-permute-start = (bf16[64,4096]{1,0:T(8,128)(2,1)S(1)}, bf16[64,4096]{1,0:T(8,128)(2,1)S(1)}, u32[]{:S(2)}, u32[]{:S(2)}) collective-permute-start(bf16[64,4096]{1,0:T(8,128)(2,1)S(1)} %get-tuple-element.46), channel_id=1, source_target_pairs={{0,1},{1,2},{2,3},{3,4},{4,5},{5,6},{6,7},{7,8},{8,9},{9,10},{10,1... | collective-permute-start | bytes 1572872 | tf_op jit(solution)/shard_map/ppermute | solution.py:25
  84.4 235.0 %collective-permute-start.1 = (bf16[64,4096]{1,0:T(8,128)(2,1)S(1)}, bf16[64,4096]{1,0:T(8,128)(2,1)S(1)}, u32[]{:S(2)}, u32[]{:S(2)}) collective-permute-start(bf16[64,4096]{1,0:T(8,128)(2,1)S(1)} %get-tuple-element.47), channel_id=1, source_target_pairs={{1,0},{2,1},{3,2},{4,3},{5,4},{6,5},{7,6},{8,7},{9,8},{10,9},{11,1... | collective-permute-start | bytes 1572872 | tf_op jit(solution)/shard_map/ppermute | solution.py:28
  475.3 229.1 %all-to-all-start.3 = ((bf16[32,64,4096]{2,1,0:T(8,128)(2,1)}), bf16[32,64,4096]{2,1,0:T(8,128)(2,1)}, u32[]{:S(2)}, u32[]{:S(2)}) async-start(bf16[32,64,4096]{2,1,0:T(8,128)(2,1)} %select_select_fusion), calls=%async_computation.3 | async-start | bytes 33554432 | tf_op jit(solution)/shard_map/all_to_all | solution.py:253
  715.0 35.1 %all-to-all-start.4 = ((bf16[32,2,8192]{2,1,0:T(2,128)(2,1)}), bf16[32,2,8192]{2,1,0:T(2,128)(2,1)S(1)}, u32[]{:S(2)}, u32[]{:S(2)}) async-start(bf16[32,2,8192]{2,1,0:T(2,128)(2,1)} %reshape.368), calls=%async_computation.4 | async-start | bytes 2097152 | tf_op jit(solution)/shard_map/all_to_all | solution.py:34
  732.2 6.3 slice-start
  733.5 7.3 copy-start.3
  733.5 11.5 %copy-start.5 = (bf16[64,2048]{1,0:T(8,128)(2,1)}, bf16[64,2048]{1,0:T(8,128)(2,1)S(1)}, u32[]{:S(2)}) copy-start(bf16[64,2048]{1,0:T(8,128)(2,1)S(1)} %get-tuple-element.51) | copy-start | bytes 786436
  733.5 5.0 slice-start.1
  738.5 6.5 copy-start.1
  741.6 36.2 %collective-permute-start.2 = (bf16[64,4096]{1,0:T(8,128)(2,1)}, bf16[64,4096]{1,0:T(8,128)(2,1)}, u32[]{:S(2)}, u32[]{:S(2)}) collective-permute-start(bf16[64,4096]{1,0:T(8,128)(2,1)} %pad_maximum_fusion.8), channel_id=1, source_target_pairs={{0,1},{1,2},{2,3},{3,4},{4,5},{5,6},{6,7},{7,8},{8,9},{9,10},{10,1... | collective-permute-start | bytes 1572872 | tf_op jit(solution)/shard_map/ppermute | solution.py:25
  745.8 31.9 %collective-permute-start.3 = (bf16[64,4096]{1,0:T(8,128)(2,1)}, bf16[64,4096]{1,0:T(8,128)(2,1)}, u32[]{:S(2)}, u32[]{:S(2)}) collective-permute-start(bf16[64,4096]{1,0:T(8,128)(2,1)} %pad_maximum_fusion.9), channel_id=1, source_target_pairs={{1,0},{2,1},{3,2},{4,3},{5,4},{6,5},{7,6},{8,7},{9,8},{10,9},{11,1... | collective-permute-start | bytes 1572872 | tf_op jit(solution)/shard_map/ppermute | solution.py:28
  764.2 21.4 %all-to-all-start.5 = ((bf16[32,2,8192]{2,1,0:T(2,128)(2,1)}), bf16[32,2,8192]{2,1,0:T(2,128)(2,1)S(1)}, u32[]{:S(2)}, u32[]{:S(2)}) async-start(bf16[32,2,8192]{2,1,0:T(2,128)(2,1)} %reshape.370), calls=%async_computation.5 | async-start | bytes 2097152 | tf_op jit(solution)/shard_map/all_to_all | solution.py:34
  770.0 7.8 copy-start.2
  770.0 7.8 copy-start.4
  770.0 7.8 copy-start.6
  794.0 3.6 copy-start.8
  794.0 3.6 copy-start.11

commit v8 on v6

--- a/solution.py
+++ b/solution.py
@@ -38,13 +38,6 @@
     n = lax.axis_size(axis)
     pieces = value.reshape(n, -1)
     mine = spread(pieces, axis)[0]
-    return spread(jnp.broadcast_to(mine[None], pieces.shape), axis).reshape(value.shape)
-
-
-def sum_all(value, axis):
-    n = lax.axis_size(axis)
-    pieces = value.reshape(n, -1)
-    mine = jnp.sum(spread(pieces, axis).astype(jnp.float32), axis=0).astype(value.dtype)
     return spread(jnp.broadcast_to(mine[None], pieces.shape), axis).reshape(value.shape)
 
 
@@ -211,8 +204,8 @@
     block_id = jnp.sum(jnp.where(chosen, local[:, None, :], 0), axis=2).reshape(-1)
     filled = jnp.any(chosen, axis=2).reshape(-1)
     tiles = pair.reshape(nbd, BS, 2 * width)
-    outgoing = jnp.where(
-        filled[:, None, None], jnp.take(tiles, block_id, axis=0), jnp.zeros((), pair.dtype)
+    outgoing = jnp.take(
+        tiles, jnp.where(filled, block_id, nbd), axis=0, mode="fill", fill_value=0
     )
     fetched = lax.all_to_all(outgoing, ("head", "blk"), split_axis=0, concat_axis=0, tiled=True)
     mine = lax.dynamic_slice_in_dim(rand, me * nbd, nbd, 0).reshape(-1)
@@ -247,7 +240,7 @@
     glob_grad = jnp.concatenate([jnp.sum(gk, axis=0), jnp.sum(gv, axis=0)], axis=-1).reshape(
         2, BS, 2 * width
     )
-    glob_total = sum_all(glob_grad.astype(jnp.bfloat16), ("head", "blk")).astype(pf)
+    glob_total = lax.psum(glob_grad.astype(jnp.bfloat16), ("head", "blk")).astype(pf)
     edge = jnp.concatenate(
         [arrived[None, :BS], jnp.zeros((nbd - 2, BS, 2 * width), pf), arrived[None, 3 * BS :]], axis=0
     )
@@ -256,10 +249,12 @@
     rand_grad = jnp.concatenate([rk, rv], axis=-1).reshape(nbd * R, BS, 2 * width)
     match = mine_slot[None, :] == jnp.arange(ndev * cap, dtype=jnp.int32)[:, None]
     source = jnp.argmax(match, axis=1)
-    returning = jnp.where(
-        jnp.any(match, axis=1)[:, None, None],
-        jnp.take(rand_grad, source, axis=0),
-        jnp.zeros((), jnp.bfloat16),
+    returning = jnp.take(
+        rand_grad,
+        jnp.where(jnp.any(match, axis=1), source, nbd * R),
+        axis=0,
+        mode="fill",
+        fill_value=0,
     )
     back = lax.all_to_all(returning, ("head", "blk"), split_axis=0, concat_axis=0, tiled=True)
     onehot = (

time: 870 us -> 836 us (0.961)
  other arithmetic: 123 us -> 104 us
  starting transfers between devices: 52.6 us -> 38.1 us
  local copies, waits for them, and re-layouts: 91 us -> 76.6 us
  between operations: 1.27 us -> 14.9 us
    psum x0 -> x1, waiting for transfers between devices: none -> 41.2 us  [body(): lax.psum(glob_grad.astype(jnp.bfloat16), ('head', 'blk')).astype(pf)]
    ppermute x2, waiting for transfers between devices: 384 us -> 347 us  [extended(): lax.ppermute(lax.slice_in_dim(block, 0, width, axis=dim), axis, backward)]
    all_to_all x4 -> x2, starting transfers between devices: 26.8 us -> 14.1 us  [spread(): return lax.all_to_all(pieces, axis, split_axis=0, concat_axis=0, tiled=True)]
    select_n x4 -> x3, other arithmetic: 28.6 us -> 28 us  [the longest x2 14 us: body(): jnp.take(tiles, jnp.where(filled, block_id, nbd), axis=0, mode='fill', fi...]
  transfers between devices with their start and end apart: 10 -> 9, of which waited for: 7 -> 7; matrix products, arithmetic and copies ran while one was open for 17% -> 13% of each run, Pallas kernels for 0% -> 4%
where the time goes in v8:
time: 836 us; the launch traced here: 826 us
  waiting for transfers between devices  420 us (50%)
  Pallas kernels  137 us (16%)
  other arithmetic  104 us (12%)
  local copies, waits for them, and re-layouts  76.6 us (9%)
  starting transfers between devices  38.1 us (5%)
  matrix products  36 us (4%)
  between operations  14.9 us (2%)
    ppermute x2, waiting for transfers between devices, extended(): lax.ppermute(lax.slice_in_dim(block, 0, width, axis=dim), axis, backward)  347 us
    pallas_call x1, Pallas kernels, attention(): pl.pallas_call(scores_kernel, grid_spec=grid_spec, out_shape=out_shape, i...  104 us
    psum x1, waiting for transfers between devices, body(): lax.psum(glob_grad.astype(jnp.bfloat16), ('head', 'blk')).astype(pf)  41.2 us
    dot_general x1, matrix products, body(): jnp.dot(onehot, back.reshape(ndev * cap, BS * 2 * width), preferred_eleme...  36 us
    pallas_call x1, Pallas kernels, attention(): pl.pallas_call(terms_kernel, grid=(nbd, groups), in_specs=[row2, row2, pr...  32.4 us
    ppermute x2, waiting for transfers between devices, extended(): lax.ppermute(lax.slice_in_dim(block, block.shape[dim] - width, None, axis...  26.1 us
    squeeze x2, local copies, waits for them, and re-layouts, overlap(): w4[:, 0]  19.3 us
  transfers between devices with their start and end apart: 9, of which 7 were waited for; matrix products, arithmetic and copies ran while one was open for 13% of the time, Pallas kernels for 4%

profile of v8, /device:TPU:14, one launch (start us, length us, event | category | flops | bytes accessed | tf_op | source)
XLA Modules:
  0.0 826.0 jit_solution(995189508062132716)
XLA Ops:
  14.0 7.1 reduce.24
  22.7 8.9 %all-to-all-start = ((bf16[32,2,8192]{2,1,0:T(2,128)(2,1)}), bf16[32,2,8192]{2,1,0:T(2,128)(2,1)S(1)}, u32[]{:S(2)}, u32[]{:S(2)}) async-start(bf16[32,2,8192]{2,1,0:T(2,128)(2,1)} %reshape.353), calls=%async_computation | async-start | bytes 2097152 | tf_op jit(solution)/shard_map/all_to_all | solution.py:34
  33.6 9.5 %gather_fusion = bf16[32,64,4096]{2,1,0:T(8,128)(2,1)} fusion(bf16[8,64,4096]{2,1,0:T(8,128)(2,1)} %bitcast.66, s32[1024]{0:T(1024)S(1)} %get-tuple-element.53), kind=kCustom, calls=%fused_computation | custom fusion | bytes 33554560 | tf_op jit(solution)/shard_map/jit(_take)/gather | solution.py:207
  43.1 4.1 all-to-all-done
  50.2 7.1 reduce.25
  58.9 5.2 all-to-all-start.1
  64.1 14.0 %broadcast_select_fusion.1 = bf16[32,64,4096]{2,1,0:T(8,128)(2,1)} fusion(bf16[32,64,4096]{2,1,0:T(8,128)(2,1)} %gather_fusion, pred[32]{0:T(512)(128)(4,1)S(1)} %compare_and_fusion.1), kind=kLoop, calls=%fused_computation.6 | loop fusion | flops 8388608 | bytes 33554464 | tf_op jit(solution)/shard_map/jit(_take)/select_n | solution.py:207
  79.9 6.4 all-to-all-start.2
  87.5 4.3 collective-permute-start.1
  95.1 216.2 %collective-permute-done.1 = bf16[64,4096]{1,0:T(8,128)(2,1)S(1)} collective-permute-done((bf16[64,4096]{1,0:T(8,128)(2,1)S(1)}, bf16[64,4096]{1,0:T(8,128)(2,1)S(1)}, u32[]{:S(2)}, u32[]{:S(2)}) %collective-permute-start.1) | collective-permute-done | bytes 524320 | tf_op jit(solution)/shard_map/ppermute | solution.py:28
  311.3 14.7 %collective-permute-done = bf16[64,4096]{1,0:T(8,128)(2,1)S(1)} collective-permute-done((bf16[64,4096]{1,0:T(8,128)(2,1)S(1)}, bf16[64,4096]{1,0:T(8,128)(2,1)S(1)}, u32[]{:S(2)}, u32[]{:S(2)}) %collective-permute-start) | collective-permute-done | bytes 524320 | tf_op jit(solution)/shard_map/ppermute | solution.py:25
  325.9 5.7 pad_maximum_fusion.2.kw0.kw1.kw2.vw0.vw1.vw2
  332.6 6.4 reduce.21
  340.7 104.4 %shard_map.84 = (bf16[512,2048]{1,0:T(8,128)(2,1)}, bf16[512,2048]{1,0:T(8,128)(2,1)}, bf16[8,192,2048]{2,1,0:T(8,128)(2,1)}, bf16[8,192,2048]{2,1,0:T(8,128)(2,...) custom-call(s32[24]{0:T(128)} %copy-done.7, bf16[512,2048]{1,0:T(8,128)(2,1)} %q_ref.3, ...), custom_call_target="tpu_custom_call" | custom-call | tf_op jit(solution)/shard_map/pallas_call | solution.py:146
  445.1 10.6 %pad_maximum_fusion = bf16[8,192,4096]{2,1,0:T(8,128)(2,1)} fusion(bf16[8,192,2048]{2,1,0:T(8,128)(2,1)} %get-tuple-element.25, bf16[8,192,2048]{2,1,0:T(8,128)(2,1)} %get-tuple-element.24), kind=kLoop, calls=%fused_computation.7 | loop fusion | flops 25165824 | bytes 25165824 | tf_op jit(solution)/shard_map/concatenate | solution.py:249
  455.7 11.8 %gather_fusion.1 = bf16[32,64,4096]{2,1,0:T(8,128)(2,1)} fusion(bf16[24,64,4096]{2,1,0:T(8,128)(2,1)} %bitcast.67, s32[1024]{0:T(1024)S(1)} %get-tuple-element.52), kind=kCustom, calls=%fused_computation.1 | custom fusion | bytes 33554560 | tf_op jit(solution)/shard_map/jit(_take)/gather | solution.py:252
  467.5 14.0 %broadcast_select_fusion = bf16[32,64,4096]{2,1,0:T(8,128)(2,1)} fusion(bf16[32,64,4096]{2,1,0:T(8,128)(2,1)} %gather_fusion.1, pred[32]{0:T(512)(128)(4,1)S(1)} %get-tuple-element.26), kind=kLoop, calls=%fused_computation.5 | loop fusion | flops 8388608 | bytes 33554464 | tf_op jit(solution)/shard_map/jit(_take)/select_n | solution.py:252
  481.5 5.0 all-to-all-start.3
  486.8 32.4 %shard_map.85 = (f32[8,192,2048]{2,1,0:T(8,128)}, f32[8,192,2048]{2,1,0:T(8,128)}, f32[8,128,2048]{2,1,0:T(8,128)}, f32[8,128,2048]{2,1,0:T(8,128)}) custom-call(bf16[512,2048]{1,0:T(8,128)(2,1)} %q_ref.3, bf16[512,2048]{1,0:T(8,128)(2,1)} %do_ref.3, bf16[8,16,64,320]{3,2,1,0:T(8,128)(2,1)} %get-tuple-element.17.pb_ref, ...), custom_call_target="tpu_custom_call" | custom-call | tf_op jit(solution)/shard_map/pallas_call | solution.py:159
  519.2 9.6 %slice_bitcast_fusion.2 = (f32[8,64,2048]{2,1,0:T(8,128)}, f32[8,64,2048]{2,1,0:T(8,128)}, f32[8,64,2048]{2,1,0:T(8,128)}) fusion(f32[8,3,64,2048]{3,2,1,0:T(8,128)} %bitcast.69), kind=kLoop, calls=%fused_computation.18 | loop fusion | bytes 25165824 | tf_op jit(solution)/shard_map/squeeze | solution.py:179
  528.8 7.7 fusion.30
  536.6 9.6 %slice_bitcast_fusion.5 = (f32[8,64,2048]{2,1,0:T(8,128)}, f32[8,64,2048]{2,1,0:T(8,128)}, f32[8,64,2048]{2,1,0:T(8,128)}) fusion(f32[8,3,64,2048]{3,2,1,0:T(8,128)} %bitcast.68), kind=kLoop, calls=%fused_computation.21 | loop fusion | bytes 25165824 | tf_op jit(solution)/shard_map/squeeze | solution.py:179
  546.2 8.2 fusion.29
  557.4 3.8 collective-permute-start.3
  568.7 4.2 reduce_sum.39
  573.0 4.2 reduce_sum.38
  579.3 7.7 pad_maximum_fusion.1
  587.0 130.6 %collective-permute-done.3 = bf16[64,4096]{1,0:T(8,128)(2,1)} collective-permute-done((bf16[64,4096]{1,0:T(8,128)(2,1)}, bf16[64,4096]{1,0:T(8,128)(2,1)}, u32[]{:S(2)}, u32[]{:S(2)}) %collective-permute-start.3) | collective-permute-done | bytes 524320 | tf_op jit(solution)/shard_map/ppermute | solution.py:28
  717.6 11.4 %collective-permute-done.2 = bf16[64,4096]{1,0:T(8,128)(2,1)} collective-permute-done((bf16[64,4096]{1,0:T(8,128)(2,1)}, bf16[64,4096]{1,0:T(8,128)(2,1)}, u32[]{:S(2)}, u32[]{:S(2)}) %collective-permute-start.2) | collective-permute-done | bytes 524320 | tf_op jit(solution)/shard_map/ppermute | solution.py:25
  733.6 41.2 %all-reduce.9.cloned.1.call-done = bf16[2,64,4096]{2,0,1:T(2,128)(2,1)} async-done(((bf16[2,64,4096]{2,0,1:T(2,128)(2,1)}), bf16[2,64,4096]{2,0,1:T(2,128)(2,1)}) %all-reduce.9.cloned.1.call-update) | async-done | bytes 1048592 | tf_op jit(solution)/shard_map/psum | solution.py:243
  777.1 36.0 %fusion.5 = bf16[8,64,4096]{2,0,1:T(8,128)(2,1)S(1)} fusion(f32[1,64,4096]{2,0,1:T(1,128)S(1)} %broadcast_in_dim.70, f32[1,64,4096]{2,0,1:T(1,128)} %copy.77, f32[8,64,4096]{2,1,0:T(8,128)} %pad_maximum_fusion.1, f32[2,64,4096]{2,0,1:T(2,128)S(1)} %convert_select_fusion, f32[8]{0:T(128)S(1)} %pad.37.clone, s32[32]{0:T(128)S(1)} %copy-done.4, ...), kind=kOutput, calls=%fused_computation.12 | convolution fusion | flops 146801152 | bytes 33554624 | tf_op jit(solution)/shard_map/dot_general | solution.py:263
  813.7 2.5 copy.81
  (78 shorter events, 46.9 us)
Async XLA Ops:
  7.2 2.2 copy-start.1
  9.6 2.0 copy-start
  11.7 19.9 %copy-start.2 = (s32[256,3]{0,1:T(4,128)S(1)}, s32[256,3]{0,1:T(4,128)}, u32[]{:S(2)}) copy-start(s32[256,3]{0,1:T(4,128)} %param.9) | copy-start | bytes 9220
  22.7 24.5 %all-to-all-start = ((bf16[32,2,8192]{2,1,0:T(2,128)(2,1)}), bf16[32,2,8192]{2,1,0:T(2,128)(2,1)S(1)}, u32[]{:S(2)}, u32[]{:S(2)}) async-start(bf16[32,2,8192]{2,1,0:T(2,128)(2,1)} %reshape.353), calls=%async_computation | async-start | bytes 2097152 | tf_op jit(solution)/shard_map/all_to_all | solution.py:34
  32.4 10.6 %copy-start.7 = (s32[24]{0:T(128)}, s32[24]{0:T(128)S(1)}, u32[]{:S(2)}) copy-start(s32[24]{0:T(128)S(1)} %fusion.34.slots_ref) | copy-start | bytes 292
  32.7 10.3 %copy-start.3 = (s32[32]{0:T(128)}, s32[32]{0:T(128)S(1)}, u32[]{:S(2)}) copy-start(s32[32]{0:T(128)S(1)} %get-tuple-element.32) | copy-start | bytes 388
  32.9 10.1 %copy-start.5 = (pred[32]{0:T(512)(128)(4,1)}, pred[32]{0:T(512)(128)(4,1)S(1)}, u32[]{:S(2)}) copy-start(pred[32]{0:T(512)(128)(4,1)S(1)} %reduce_or.18) | copy-start | bytes 100
  58.9 21.0 %all-to-all-start.1 = ((bf16[32,2,8192]{2,1,0:T(2,128)(2,1)}), bf16[32,2,8192]{2,1,0:T(2,128)(2,1)S(1)}, u32[]{:S(2)}, u32[]{:S(2)}) async-start(bf16[32,2,8192]{2,1,0:T(2,128)(2,1)} %reshape.355), calls=%async_computation.1 | async-start | bytes 2097152 | tf_op jit(solution)/shard_map/all_to_all | solution.py:34
  79.9 260.8 %all-to-all-start.2 = ((bf16[32,64,4096]{2,1,0:T(8,128)(2,1)}), bf16[32,64,4096]{2,1,0:T(8,128)(2,1)}, u32[]{:S(2)}, u32[]{:S(2)}) async-start(bf16[32,64,4096]{2,1,0:T(8,128)(2,1)} %broadcast_select_fusion.1), calls=%async_computation.2 | async-start | bytes 33554432 | tf_op jit(solution)/shard_map/all_to_all | solution.py:210
  87.5 223.7 %collective-permute-start.1 = (bf16[64,4096]{1,0:T(8,128)(2,1)S(1)}, bf16[64,4096]{1,0:T(8,128)(2,1)S(1)}, u32[]{:S(2)}, u32[]{:S(2)}) collective-permute-start(bf16[64,4096]{1,0:T(8,128)(2,1)S(1)} %get-tuple-element.43), channel_id=1, source_target_pairs={{1,0},{2,1},{3,2},{4,3},{5,4},{6,5},{7,6},{8,7},{9,8},{10,9},{11,1... | collective-permute-start | bytes 1572872 | tf_op jit(solution)/shard_map/ppermute | solution.py:28
  91.8 234.1 %collective-permute-start = (bf16[64,4096]{1,0:T(8,128)(2,1)S(1)}, bf16[64,4096]{1,0:T(8,128)(2,1)S(1)}, u32[]{:S(2)}, u32[]{:S(2)}) collective-permute-start(bf16[64,4096]{1,0:T(8,128)(2,1)S(1)} %get-tuple-element.42), channel_id=1, source_target_pairs={{0,1},{1,2},{2,3},{3,4},{4,5},{5,6},{6,7},{7,8},{8,9},{9,10},{10,1... | collective-permute-start | bytes 1572872 | tf_op jit(solution)/shard_map/ppermute | solution.py:25
  481.5 295.6 %all-to-all-start.3 = ((bf16[32,64,4096]{2,1,0:T(8,128)(2,1)}), bf16[32,64,4096]{2,1,0:T(8,128)(2,1)}, u32[]{:S(2)}, u32[]{:S(2)}) async-start(bf16[32,64,4096]{2,1,0:T(8,128)(2,1)} %broadcast_select_fusion), calls=%async_computation.3 | async-start | bytes 33554432 | tf_op jit(solution)/shard_map/all_to_all | solution.py:259
  486.5 288.3 %all-reduce.9.cloned.1.call-start = ((), (), s32[]{:S(2)}) async-start(), calls=%async_computation.4 | async-start | bytes 2097152 | tf_op jit(solution)/shard_map/psum | solution.py:243
  557.4 160.2 %collective-permute-start.3 = (bf16[64,4096]{1,0:T(8,128)(2,1)}, bf16[64,4096]{1,0:T(8,128)(2,1)}, u32[]{:S(2)}, u32[]{:S(2)}) collective-permute-start(bf16[64,4096]{1,0:T(8,128)(2,1)} %pad_maximum_fusion.9), channel_id=1, source_target_pairs={{1,0},{2,1},{3,2},{4,3},{5,4},{6,5},{7,6},{8,7},{9,8},{10,9},{11,1... | collective-permute-start | bytes 1572872 | tf_op jit(solution)/shard_map/ppermute | solution.py:28
  562.0 167.0 %collective-permute-start.2 = (bf16[64,4096]{1,0:T(8,128)(2,1)}, bf16[64,4096]{1,0:T(8,128)(2,1)}, u32[]{:S(2)}, u32[]{:S(2)}) collective-permute-start(bf16[64,4096]{1,0:T(8,128)(2,1)} %pad_maximum_fusion.8), channel_id=1, source_target_pairs={{0,1},{1,2},{2,3},{3,4},{4,5},{5,6},{6,7},{7,8},{8,9},{9,10},{10,1... | collective-permute-start | bytes 1572872 | tf_op jit(solution)/shard_map/ppermute | solution.py:25
  587.0 190.1 %copy-start.4 = (s32[32]{0:T(128)S(1)}, s32[32]{0:T(128)}, u32[]{:S(2)}) copy-start(s32[32]{0:T(128)} %copy-done.3) | copy-start | bytes 388
  587.0 190.1 %copy-start.6 = (pred[32]{0:T(512)(128)(4,1)S(1)}, pred[32]{0:T(512)(128)(4,1)}, u32[]{:S(2)}) copy-start(pred[32]{0:T(512)(128)(4,1)} %copy-done.5) | copy-start | bytes 100
Sparse Core Ops, SparseCore 0:
  579.5 195.3 all-reduce.8

commit v9 on v3

--- a/solution.py
+++ b/solution.py
@@ -14,7 +14,7 @@
 
 NEG = -1e30
 INTERPRET = False
-HG = 4
+HG = 8
 
 
 def extended(block, sides, width):

time: 830 us -> 824 us (level); the launches traced: 816 us -> 820 us
  Pallas kernels: 137 us -> 121 us
  matrix products: 36 us -> 47.1 us
  waiting for transfers between devices: 447 us -> 456 us
    dot_general x1, matrix products: 36 us -> 47.1 us  [body(): jnp.dot(onehot, back.reshape(ndev * cap, BS * 2 * width), preferred_eleme...]
    ppermute x2, waiting for transfers between devices: 353 us -> 362 us  [extended(): lax.ppermute(lax.slice_in_dim(block, 0, width, axis=dim), axis, backward)]
    pallas_call x1, Pallas kernels: 32.4 us -> 23.6 us  [attention(): pl.pallas_call(terms_kernel, grid=(nbd, groups), in_specs=[row2, row2, pr...]
  transfers between devices with their start and end apart: 8 -> 8, of which waited for: 6 -> 6; matrix products, arithmetic and copies ran while one was open for 10% -> 10% of each run, Pallas kernels for 4% -> 3%
where the time goes in v9:
time: 824 us; the launch traced here: 820 us
  waiting for transfers between devices  456 us (55%)
  Pallas kernels  121 us (15%)
  other arithmetic  86 us (10%)
  local copies, waits for them, and re-layouts  67.5 us (8%)
  matrix products  47.1 us (6%)
  starting transfers between devices  27.9 us (3%)
  between operations  14.5 us (2%)
    ppermute x2, waiting for transfers between devices, extended(): lax.ppermute(lax.slice_in_dim(block, 0, width, axis=dim), axis, backward)  362 us
    pallas_call x1, Pallas kernels, attention(): pl.pallas_call(scores_kernel, grid_spec=grid_spec, out_shape=out_shape, i...  97.7 us
    dot_general x1, matrix products, body(): jnp.dot(onehot, back.reshape(ndev * cap, BS * 2 * width), preferred_eleme...  47.1 us
    psum x1, waiting for transfers between devices, body(): lax.psum(glob_grad.astype(jnp.bfloat16), ('head', 'blk')).astype(pf)  41.8 us
    psum x1, waiting for transfers between devices, from_root(): return lax.psum(kept, axis)  34.4 us
    pallas_call x1, Pallas kernels, attention(): pl.pallas_call(terms_kernel, grid=(nbd, groups), in_specs=[row2, row2, pr...  23.6 us
    squeeze x2, local copies, waits for them, and re-layouts, overlap(): w4[:, 0]  19.3 us
    ppermute x2, waiting for transfers between devices, extended(): lax.ppermute(lax.slice_in_dim(block, block.shape[dim] - width, None, axis...  17.9 us
  transfers between devices with their start and end apart: 8, of which 6 were waited for; matrix products, arithmetic and copies ran while one was open for 10% of the time, Pallas kernels for 3%

profile of v9, /device:TPU:14, one launch (start us, length us, event | category | flops | bytes accessed | tf_op | source)
XLA Modules:
  0.0 820.4 jit_solution(2982879969407185811)
XLA Ops:
  10.5 3.2 constant_dynamic-update-slice_fusion.1
  15.8 9.4 %gather_fusion = bf16[32,64,4096]{2,1,0:T(8,128)(2,1)} fusion(bf16[8,64,4096]{2,1,0:T(8,128)(2,1)} %bitcast.1, s32[1024]{0:T(1024)S(1)} %get-tuple-element.51), kind=kCustom, calls=%fused_computation | custom fusion | bytes 33554560 | tf_op jit(solution)/shard_map/jit(_take)/gather | solution.py:202
  25.2 14.3 %select_select_fusion.1 = bf16[32,64,4096]{2,1,0:T(8,128)(2,1)} fusion(bf16[32,64,4096]{2,1,0:T(8,128)(2,1)} %gather_fusion, pred[32]{0:T(512)(128)(4,1)S(1)} %compare_and_fusion.1, pred[32]{0:T(512)(128)(4,1)S(1)} %get-tuple-element.30), kind=kLoop, calls=%fused_computation.6 | loop fusion | flops 16777216 | bytes 33554496 | tf_op jit(solution)/shard_map/jit(_where)/select_n | solution.py:201
  39.4 8.6 %all-to-all-start = ((bf16[32,64,4096]{2,1,0:T(8,128)(2,1)}), bf16[32,64,4096]{2,1,0:T(8,128)(2,1)}, u32[]{:S(2)}, u32[]{:S(2)}) async-start(bf16[32,64,4096]{2,1,0:T(8,128)(2,1)} %select_select_fusion.1), calls=%async_computation | async-start | bytes 33554432 | tf_op jit(solution)/shard_map/all_to_all | solution.py:204
  49.4 4.3 collective-permute-start.1
  55.6 2.3 slice_select_fusion
  59.0 222.5 %collective-permute-done.1 = bf16[64,4096]{1,0:T(8,128)(2,1)S(1)} collective-permute-done((bf16[64,4096]{1,0:T(8,128)(2,1)S(1)}, bf16[64,4096]{1,0:T(8,128)(2,1)S(1)}, u32[]{:S(2)}, u32[]{:S(2)}) %collective-permute-start.1) | collective-permute-done | bytes 524320 | tf_op jit(solution)/shard_map/ppermute | solution.py:28
  281.4 6.7 collective-permute-done
  288.1 5.7 pad_maximum_fusion.2.kw0.kw1.kw2.vw0.vw1.vw2
  293.8 34.4 %all-reduce.10.cloned.1.call-done.kg.vg = bf16[128,4096]{1,0:T(8,128)(2,1)} async-done(((bf16[128,4096]{1,0:T(8,128)(2,1)}), bf16[128,4096]{1,0:T(8,128)(2,1)}) %all-reduce.10.cloned.1.call-update) | async-done | bytes 1048592 | tf_op jit(solution)/shard_map/psum | solution.py:35
  328.2 97.7 %shard_map.84 = (bf16[512,2048]{1,0:T(8,128)(2,1)}, bf16[512,2048]{1,0:T(8,128)(2,1)}, bf16[8,192,2048]{2,1,0:T(8,128)(2,1)}, bf16[8,192,2048]{2,1,0:T(8,128)(2,...) custom-call(s32[24]{0:T(128)} %copy-done.3, bf16[512,2048]{1,0:T(8,128)(2,1)} %q_ref.3, ...), custom_call_target="tpu_custom_call" | custom-call | tf_op jit(solution)/shard_map/pallas_call | solution.py:140
  425.9 10.6 %pad_maximum_fusion = bf16[8,192,4096]{2,1,0:T(8,128)(2,1)} fusion(bf16[8,192,2048]{2,1,0:T(8,128)(2,1)} %get-tuple-element.25, bf16[8,192,2048]{2,1,0:T(8,128)(2,1)} %get-tuple-element.24), kind=kLoop, calls=%fused_computation.7 | loop fusion | flops 25165824 | bytes 25165824 | tf_op jit(solution)/shard_map/concatenate | solution.py:243
  436.5 11.8 %gather_fusion.1 = bf16[32,64,4096]{2,1,0:T(8,128)(2,1)} fusion(bf16[24,64,4096]{2,1,0:T(8,128)(2,1)} %bitcast.66, s32[1024]{0:T(1024)S(1)} %get-tuple-element.50), kind=kCustom, calls=%fused_computation.1 | custom fusion | bytes 33554560 | tf_op jit(solution)/shard_map/jit(_take)/gather | solution.py:248
  448.3 14.3 %select_select_fusion = bf16[32,64,4096]{2,1,0:T(8,128)(2,1)} fusion(bf16[32,64,4096]{2,1,0:T(8,128)(2,1)} %gather_fusion.1, pred[32]{0:T(512)(128)(4,1)S(1)} %compare_and_fusion, pred[32]{0:T(512)(128)(4,1)S(1)} %fusion.18), kind=kLoop, calls=%fused_computation.5 | loop fusion | flops 16777216 | bytes 33554496 | tf_op jit(solution)/shard_map/jit(_where)/select_n | solution.py:246
  462.6 6.5 all-to-all-start.1
  469.5 23.6 %shard_map.85 = (f32[8,192,2048]{2,1,0:T(8,128)}, f32[8,192,2048]{2,1,0:T(8,128)}, f32[8,128,2048]{2,1,0:T(8,128)}, f32[8,128,2048]{2,1,0:T(8,128)}) custom-call(bf16[512,2048]{1,0:T(8,128)(2,1)} %q_ref.3, bf16[512,2048]{1,0:T(8,128)(2,1)} %do_ref.3, bf16[8,16,64,320]{3,2,1,0:T(8,128)(2,1)} %get-tuple-element.17.pb_ref, ...), custom_call_target="tpu_custom_call" | custom-call | tf_op jit(solution)/shard_map/pallas_call | solution.py:153
  493.1 9.6 %slice_bitcast_fusion.2 = (f32[8,64,2048]{2,1,0:T(8,128)}, f32[8,64,2048]{2,1,0:T(8,128)}, f32[8,64,2048]{2,1,0:T(8,128)}) fusion(f32[8,3,64,2048]{3,2,1,0:T(8,128)} %bitcast.68), kind=kLoop, calls=%fused_computation.18 | loop fusion | bytes 25165824 | tf_op jit(solution)/shard_map/squeeze | solution.py:173
  502.7 7.7 fusion.30
  510.4 9.6 %slice_bitcast_fusion.5 = (f32[8,64,2048]{2,1,0:T(8,128)}, f32[8,64,2048]{2,1,0:T(8,128)}, f32[8,64,2048]{2,1,0:T(8,128)}) fusion(f32[8,3,64,2048]{3,2,1,0:T(8,128)} %bitcast.67), kind=kLoop, calls=%fused_computation.21 | loop fusion | bytes 25165824 | tf_op jit(solution)/shard_map/squeeze | solution.py:173
  520.0 8.2 %fusion.29 = (bf16[10,64,2048]{2,1,0:T(8,128)(2,1)}, f32[10,64,2048]{2,1,0:T(8,128)S(1)}) fusion(f32[8,64,2048]{2,1,0:T(8,128)} %get-tuple-element.34, f32[8,64,2048]{2,1,0:T(8,128)} %get-tuple-element.33, f32[8,64,2048]{2,1,0:T(8,128)} %get-tuple-element.32), kind=kLoop, calls=%fused_computation.88 | loop fusion | flops 3932160 | bytes 20447232 | tf_op jit(solution)/shard_map/convert.11
  531.3 4.3 collective-permute-start.3
  540.5 2.4 slice.94
  542.9 4.2 reduce_sum.42
  547.2 4.2 reduce_sum.41
  553.6 7.7 pad_maximum_fusion.1
  561.2 139.5 %collective-permute-done.3 = bf16[64,4096]{1,0:T(8,128)(2,1)} collective-permute-done((bf16[64,4096]{1,0:T(8,128)(2,1)}, bf16[64,4096]{1,0:T(8,128)(2,1)}, u32[]{:S(2)}, u32[]{:S(2)}) %collective-permute-start.3) | collective-permute-done | bytes 524320 | tf_op jit(solution)/shard_map/ppermute | solution.py:28
  700.7 11.2 %collective-permute-done.2 = bf16[64,4096]{1,0:T(8,128)(2,1)} collective-permute-done((bf16[64,4096]{1,0:T(8,128)(2,1)}, bf16[64,4096]{1,0:T(8,128)(2,1)}, u32[]{:S(2)}, u32[]{:S(2)}) %collective-permute-start.2) | collective-permute-done | bytes 524320 | tf_op jit(solution)/shard_map/ppermute | solution.py:25
  716.6 41.8 %all-reduce.12.cloned.1.call-done = bf16[2,64,4096]{2,0,1:T(2,128)(2,1)} async-done(((bf16[2,64,4096]{2,0,1:T(2,128)(2,1)}), bf16[2,64,4096]{2,0,1:T(2,128)(2,1)}) %all-reduce.12.cloned.1.call-update) | async-done | bytes 1048592 | tf_op jit(solution)/shard_map/psum | solution.py:237
  758.3 2.3 convert_select_fusion
  760.6 47.1 %fusion.5 = bf16[8,64,4096]{2,0,1:T(8,128)(2,1)S(1)} fusion(f32[1,64,4096]{2,0,1:T(1,128)S(1)} %broadcast_in_dim.79, f32[1,64,4096]{2,0,1:T(1,128)} %copy.44, f32[8,64,4096]{2,1,0:T(8,128)} %pad_maximum_fusion.1, f32[2,64,4096]{2,0,1:T(2,128)S(1)} %convert_select_fusion, f32[8]{0:T(128)S(1)} %pad.37.clone, s32[32]{0:T(128)S(1)} %copy-done.2, ...), kind=kOutput, calls=%fused_computation.12 | convolution fusion | flops 146801152 | bytes 33554624 | tf_op jit(solution)/shard_map/dot_general | solution.py:255
  808.4 2.5 copy.48
  810.8 2.5 copy.49
  (58 shorter events, 25.2 us)
Async XLA Ops:
  7.2 7.1 copy-start
  8.8 0.5 copy-start.1
  10.5 48.4 %copy-start.3 = (s32[24]{0:T(128)}, s32[24]{0:T(128)S(1)}, u32[]{:S(2)}) copy-start(s32[24]{0:T(128)S(1)} %fusion.35.slots_ref) | copy-start | bytes 292
  39.4 288.7 %all-to-all-start = ((bf16[32,64,4096]{2,1,0:T(8,128)(2,1)}), bf16[32,64,4096]{2,1,0:T(8,128)(2,1)}, u32[]{:S(2)}, u32[]{:S(2)}) async-start(bf16[32,64,4096]{2,1,0:T(8,128)(2,1)} %select_select_fusion.1), calls=%async_computation | async-start | bytes 33554432 | tf_op jit(solution)/shard_map/all_to_all | solution.py:204
  48.1 280.1 %all-reduce.10.cloned.1.call-start = ((), (), s32[]{:S(2)}) async-start(), calls=%async_computation.2 | async-start | bytes 2097152 | tf_op jit(solution)/shard_map/psum | solution.py:35
  49.4 232.0 %collective-permute-start.1 = (bf16[64,4096]{1,0:T(8,128)(2,1)S(1)}, bf16[64,4096]{1,0:T(8,128)(2,1)S(1)}, u32[]{:S(2)}, u32[]{:S(2)}) collective-permute-start(bf16[64,4096]{1,0:T(8,128)(2,1)S(1)} %get-tuple-element.41), channel_id=1, source_target_pairs={{1,0},{2,1},{3,2},{4,3},{5,4},{6,5},{7,6},{8,7},{9,8},{10,9},{11,1... | collective-permute-start | bytes 1572872 | tf_op jit(solution)/shard_map/ppermute | solution.py:28
  53.7 234.4 %collective-permute-start = (bf16[64,4096]{1,0:T(8,128)(2,1)S(1)}, bf16[64,4096]{1,0:T(8,128)(2,1)S(1)}, u32[]{:S(2)}, u32[]{:S(2)}) collective-permute-start(bf16[64,4096]{1,0:T(8,128)(2,1)S(1)} %get-tuple-element.40), channel_id=1, source_target_pairs={{0,1},{1,2},{2,3},{3,4},{4,5},{5,6},{6,7},{7,8},{8,9},{9,10},{10,1... | collective-permute-start | bytes 1572872 | tf_op jit(solution)/shard_map/ppermute | solution.py:25
  462.6 298.0 %all-to-all-start.1 = ((bf16[32,64,4096]{2,1,0:T(8,128)(2,1)}), bf16[32,64,4096]{2,1,0:T(8,128)(2,1)}, u32[]{:S(2)}, u32[]{:S(2)}) async-start(bf16[32,64,4096]{2,1,0:T(8,128)(2,1)} %select_select_fusion), calls=%async_computation.1 | async-start | bytes 33554432 | tf_op jit(solution)/shard_map/all_to_all | solution.py:251
  469.1 289.2 %all-reduce.12.cloned.1.call-start = ((), (), s32[]{:S(2)}) async-start(), calls=%async_computation.3 | async-start | bytes 2097152 | tf_op jit(solution)/shard_map/psum | solution.py:237
  531.3 169.4 %collective-permute-start.3 = (bf16[64,4096]{1,0:T(8,128)(2,1)}, bf16[64,4096]{1,0:T(8,128)(2,1)}, u32[]{:S(2)}, u32[]{:S(2)}) collective-permute-start(bf16[64,4096]{1,0:T(8,128)(2,1)} %pad_maximum_fusion.9), channel_id=1, source_target_pairs={{1,0},{2,1},{3,2},{4,3},{5,4},{6,5},{7,6},{8,7},{9,8},{10,9},{11,1... | collective-permute-start | bytes 1572872 | tf_op jit(solution)/shard_map/ppermute | solution.py:28
  536.4 175.5 %collective-permute-start.2 = (bf16[64,4096]{1,0:T(8,128)(2,1)}, bf16[64,4096]{1,0:T(8,128)(2,1)}, u32[]{:S(2)}, u32[]{:S(2)}) collective-permute-start(bf16[64,4096]{1,0:T(8,128)(2,1)} %pad_maximum_fusion.8), channel_id=1, source_target_pairs={{0,1},{1,2},{2,3},{3,4},{4,5},{5,6},{6,7},{7,8},{8,9},{9,10},{10,1... | collective-permute-start | bytes 1572872 | tf_op jit(solution)/shard_map/ppermute | solution.py:25
  561.2 199.4 %copy-start.2 = (s32[32]{0:T(128)S(1)}, s32[32]{0:T(128)}, u32[]{:S(2)}) copy-start(s32[32]{0:T(128)} %copy-done.1) | copy-start | bytes 388
Sparse Core Ops, SparseCore 0:
  58.1 270.0 all-reduce.9
  553.7 204.5 all-reduce.11

commit v10 on v9

--- a/solution.py
+++ b/solution.py
@@ -14,7 +14,7 @@
 
 NEG = -1e30
 INTERPRET = False
-HG = 8
+HG = 16
 
 
 def extended(block, sides, width):

time: 824 us -> 823 us (level)
  no operation moved by 1% of the time
where the time goes in v10:
time: 823 us; the launch traced here: 817 us
  waiting for transfers between devices  458 us (56%)
  Pallas kernels  116 us (14%)
  other arithmetic  86 us (10%)
  local copies, waits for them, and re-layouts  67.5 us (8%)
  matrix products  47.1 us (6%)
  starting transfers between devices  27.8 us (3%)
  between operations  14.5 us (2%)
    ppermute x2, waiting for transfers between devices, extended(): lax.ppermute(lax.slice_in_dim(block, 0, width, axis=dim), axis, backward)  364 us
    pallas_call x1, Pallas kernels, attention(): pl.pallas_call(scores_kernel, grid_spec=grid_spec, out_shape=out_shape, i...  94.4 us
    dot_general x1, matrix products, body(): jnp.dot(onehot, back.reshape(ndev * cap, BS * 2 * width), preferred_eleme...  47.1 us
    psum x1, waiting for transfers between devices, body(): lax.psum(glob_grad.astype(jnp.bfloat16), ('head', 'blk')).astype(pf)  41.6 us
    psum x1, waiting for transfers between devices, from_root(): return lax.psum(kept, axis)  34.4 us
    pallas_call x1, Pallas kernels, attention(): pl.pallas_call(terms_kernel, grid=(nbd, groups), in_specs=[row2, row2, pr...  21.2 us
    squeeze x2, local copies, waits for them, and re-layouts, overlap(): w4[:, 0]  19.3 us
    ppermute x2, waiting for transfers between devices, extended(): lax.ppermute(lax.slice_in_dim(block, block.shape[dim] - width, None, axis...  18.2 us
  transfers between devices with their start and end apart: 8, of which 6 were waited for; matrix products, arithmetic and copies ran while one was open for 10% of the time, Pallas kernels for 3%

profile of v10, /device:TPU:14, one launch (start us, length us, event | category | flops | bytes accessed | tf_op | source)
XLA Modules:
  0.0 816.9 jit_solution(13257882366322362345)
XLA Ops:
  10.5 3.2 constant_dynamic-update-slice_fusion.1
  15.8 9.4 %gather_fusion = bf16[32,64,4096]{2,1,0:T(8,128)(2,1)} fusion(bf16[8,64,4096]{2,1,0:T(8,128)(2,1)} %bitcast.1, s32[1024]{0:T(1024)S(1)} %get-tuple-element.51), kind=kCustom, calls=%fused_computation | custom fusion | bytes 33554560 | tf_op jit(solution)/shard_map/jit(_take)/gather | solution.py:202
  25.2 14.3 %select_select_fusion.1 = bf16[32,64,4096]{2,1,0:T(8,128)(2,1)} fusion(bf16[32,64,4096]{2,1,0:T(8,128)(2,1)} %gather_fusion, pred[32]{0:T(512)(128)(4,1)S(1)} %compare_and_fusion.1, pred[32]{0:T(512)(128)(4,1)S(1)} %get-tuple-element.30), kind=kLoop, calls=%fused_computation.6 | loop fusion | flops 16777216 | bytes 33554496 | tf_op jit(solution)/shard_map/jit(_where)/select_n | solution.py:201
  39.5 8.6 %all-to-all-start = ((bf16[32,64,4096]{2,1,0:T(8,128)(2,1)}), bf16[32,64,4096]{2,1,0:T(8,128)(2,1)}, u32[]{:S(2)}, u32[]{:S(2)}) async-start(bf16[32,64,4096]{2,1,0:T(8,128)(2,1)} %select_select_fusion.1), calls=%async_computation | async-start | bytes 33554432 | tf_op jit(solution)/shard_map/all_to_all | solution.py:204
  49.4 4.3 collective-permute-start.1
  55.6 2.3 slice_select_fusion
  58.9 222.5 %collective-permute-done.1 = bf16[64,4096]{1,0:T(8,128)(2,1)S(1)} collective-permute-done((bf16[64,4096]{1,0:T(8,128)(2,1)S(1)}, bf16[64,4096]{1,0:T(8,128)(2,1)S(1)}, u32[]{:S(2)}, u32[]{:S(2)}) %collective-permute-start.1) | collective-permute-done | bytes 524320 | tf_op jit(solution)/shard_map/ppermute | solution.py:28
  281.4 6.7 collective-permute-done
  288.1 5.7 pad_maximum_fusion.2.kw0.kw1.kw2.vw0.vw1.vw2
  293.8 34.4 %all-reduce.10.cloned.1.call-done.kg.vg = bf16[128,4096]{1,0:T(8,128)(2,1)} async-done(((bf16[128,4096]{1,0:T(8,128)(2,1)}), bf16[128,4096]{1,0:T(8,128)(2,1)}) %all-reduce.10.cloned.1.call-update) | async-done | bytes 1048592 | tf_op jit(solution)/shard_map/psum | solution.py:35
  328.2 94.4 %shard_map.84 = (bf16[512,2048]{1,0:T(8,128)(2,1)}, bf16[512,2048]{1,0:T(8,128)(2,1)}, bf16[8,192,2048]{2,1,0:T(8,128)(2,1)}, bf16[8,192,2048]{2,1,0:T(8,128)(2,...) custom-call(s32[24]{0:T(128)} %copy-done.3, bf16[512,2048]{1,0:T(8,128)(2,1)} %q_ref.3, ...), custom_call_target="tpu_custom_call" | custom-call | tf_op jit(solution)/shard_map/pallas_call | solution.py:140
  422.6 10.6 %pad_maximum_fusion = bf16[8,192,4096]{2,1,0:T(8,128)(2,1)} fusion(bf16[8,192,2048]{2,1,0:T(8,128)(2,1)} %get-tuple-element.25, bf16[8,192,2048]{2,1,0:T(8,128)(2,1)} %get-tuple-element.24), kind=kLoop, calls=%fused_computation.7 | loop fusion | flops 25165824 | bytes 25165824 | tf_op jit(solution)/shard_map/concatenate | solution.py:243
  433.2 11.8 %gather_fusion.1 = bf16[32,64,4096]{2,1,0:T(8,128)(2,1)} fusion(bf16[24,64,4096]{2,1,0:T(8,128)(2,1)} %bitcast.66, s32[1024]{0:T(1024)S(1)} %get-tuple-element.50), kind=kCustom, calls=%fused_computation.1 | custom fusion | bytes 33554560 | tf_op jit(solution)/shard_map/jit(_take)/gather | solution.py:248
  445.0 14.3 %select_select_fusion = bf16[32,64,4096]{2,1,0:T(8,128)(2,1)} fusion(bf16[32,64,4096]{2,1,0:T(8,128)(2,1)} %gather_fusion.1, pred[32]{0:T(512)(128)(4,1)S(1)} %compare_and_fusion, pred[32]{0:T(512)(128)(4,1)S(1)} %fusion.18), kind=kLoop, calls=%fused_computation.5 | loop fusion | flops 16777216 | bytes 33554496 | tf_op jit(solution)/shard_map/jit(_where)/select_n | solution.py:246
  459.3 6.5 all-to-all-start.1
  466.2 21.2 %shard_map.85 = (f32[8,192,2048]{2,1,0:T(8,128)}, f32[8,192,2048]{2,1,0:T(8,128)}, f32[8,128,2048]{2,1,0:T(8,128)}, f32[8,128,2048]{2,1,0:T(8,128)}) custom-call(bf16[512,2048]{1,0:T(8,128)(2,1)} %q_ref.3, bf16[512,2048]{1,0:T(8,128)(2,1)} %do_ref.3, bf16[8,16,64,320]{3,2,1,0:T(8,128)(2,1)} %get-tuple-element.17.pb_ref, ...), custom_call_target="tpu_custom_call" | custom-call | tf_op jit(solution)/shard_map/pallas_call | solution.py:153
  487.4 9.6 %slice_bitcast_fusion.2 = (f32[8,64,2048]{2,1,0:T(8,128)}, f32[8,64,2048]{2,1,0:T(8,128)}, f32[8,64,2048]{2,1,0:T(8,128)}) fusion(f32[8,3,64,2048]{3,2,1,0:T(8,128)} %bitcast.68), kind=kLoop, calls=%fused_computation.18 | loop fusion | bytes 25165824 | tf_op jit(solution)/shard_map/squeeze | solution.py:173
  497.1 7.7 fusion.30
  504.8 9.6 %slice_bitcast_fusion.5 = (f32[8,64,2048]{2,1,0:T(8,128)}, f32[8,64,2048]{2,1,0:T(8,128)}, f32[8,64,2048]{2,1,0:T(8,128)}) fusion(f32[8,3,64,2048]{3,2,1,0:T(8,128)} %bitcast.67), kind=kLoop, calls=%fused_computation.21 | loop fusion | bytes 25165824 | tf_op jit(solution)/shard_map/squeeze | solution.py:173
  514.4 8.2 %fusion.29 = (bf16[10,64,2048]{2,1,0:T(8,128)(2,1)}, f32[10,64,2048]{2,1,0:T(8,128)S(1)}) fusion(f32[8,64,2048]{2,1,0:T(8,128)} %get-tuple-element.34, f32[8,64,2048]{2,1,0:T(8,128)} %get-tuple-element.33, f32[8,64,2048]{2,1,0:T(8,128)} %get-tuple-element.32), kind=kLoop, calls=%fused_computation.88 | loop fusion | flops 3932160 | bytes 20447232 | tf_op jit(solution)/shard_map/convert.11
  525.6 4.3 collective-permute-start.3
  534.9 2.4 slice.94
  537.3 4.2 reduce_sum.42
  541.5 4.2 reduce_sum.41
  547.9 7.7 pad_maximum_fusion.1
  555.6 141.5 %collective-permute-done.3 = bf16[64,4096]{1,0:T(8,128)(2,1)} collective-permute-done((bf16[64,4096]{1,0:T(8,128)(2,1)}, bf16[64,4096]{1,0:T(8,128)(2,1)}, u32[]{:S(2)}, u32[]{:S(2)}) %collective-permute-start.3) | collective-permute-done | bytes 524320 | tf_op jit(solution)/shard_map/ppermute | solution.py:28
  697.1 11.5 %collective-permute-done.2 = bf16[64,4096]{1,0:T(8,128)(2,1)} collective-permute-done((bf16[64,4096]{1,0:T(8,128)(2,1)}, bf16[64,4096]{1,0:T(8,128)(2,1)}, u32[]{:S(2)}, u32[]{:S(2)}) %collective-permute-start.2) | collective-permute-done | bytes 524320 | tf_op jit(solution)/shard_map/ppermute | solution.py:25
  713.2 41.6 %all-reduce.12.cloned.1.call-done = bf16[2,64,4096]{2,0,1:T(2,128)(2,1)} async-done(((bf16[2,64,4096]{2,0,1:T(2,128)(2,1)}), bf16[2,64,4096]{2,0,1:T(2,128)(2,1)}) %all-reduce.12.cloned.1.call-update) | async-done | bytes 1048592 | tf_op jit(solution)/shard_map/psum | solution.py:237
  754.8 2.3 convert_select_fusion
  757.2 47.1 %fusion.5 = bf16[8,64,4096]{2,0,1:T(8,128)(2,1)S(1)} fusion(f32[1,64,4096]{2,0,1:T(1,128)S(1)} %broadcast_in_dim.79, f32[1,64,4096]{2,0,1:T(1,128)} %copy.44, f32[8,64,4096]{2,1,0:T(8,128)} %pad_maximum_fusion.1, f32[2,64,4096]{2,0,1:T(2,128)S(1)} %convert_select_fusion, f32[8]{0:T(128)S(1)} %pad.37.clone, s32[32]{0:T(128)S(1)} %copy-done.2, ...), kind=kOutput, calls=%fused_computation.12 | convolution fusion | flops 146801152 | bytes 33554624 | tf_op jit(solution)/shard_map/dot_general | solution.py:255
  804.9 2.5 copy.48
  807.4 2.5 copy.49
  (58 shorter events, 25.2 us)
Async XLA Ops:
  7.2 7.1 copy-start
  8.8 0.5 copy-start.1
  10.5 48.4 %copy-start.3 = (s32[24]{0:T(128)}, s32[24]{0:T(128)S(1)}, u32[]{:S(2)}) copy-start(s32[24]{0:T(128)S(1)} %fusion.35.slots_ref) | copy-start | bytes 292
  39.5 288.7 %all-to-all-start = ((bf16[32,64,4096]{2,1,0:T(8,128)(2,1)}), bf16[32,64,4096]{2,1,0:T(8,128)(2,1)}, u32[]{:S(2)}, u32[]{:S(2)}) async-start(bf16[32,64,4096]{2,1,0:T(8,128)(2,1)} %select_select_fusion.1), calls=%async_computation | async-start | bytes 33554432 | tf_op jit(solution)/shard_map/all_to_all | solution.py:204
  48.1 280.1 %all-reduce.10.cloned.1.call-start = ((), (), s32[]{:S(2)}) async-start(), calls=%async_computation.2 | async-start | bytes 2097152 | tf_op jit(solution)/shard_map/psum | solution.py:35
  49.4 232.0 %collective-permute-start.1 = (bf16[64,4096]{1,0:T(8,128)(2,1)S(1)}, bf16[64,4096]{1,0:T(8,128)(2,1)S(1)}, u32[]{:S(2)}, u32[]{:S(2)}) collective-permute-start(bf16[64,4096]{1,0:T(8,128)(2,1)S(1)} %get-tuple-element.41), channel_id=1, source_target_pairs={{1,0},{2,1},{3,2},{4,3},{5,4},{6,5},{7,6},{8,7},{9,8},{10,9},{11,1... | collective-permute-start | bytes 1572872 | tf_op jit(solution)/shard_map/ppermute | solution.py:28
  53.7 234.4 %collective-permute-start = (bf16[64,4096]{1,0:T(8,128)(2,1)S(1)}, bf16[64,4096]{1,0:T(8,128)(2,1)S(1)}, u32[]{:S(2)}, u32[]{:S(2)}) collective-permute-start(bf16[64,4096]{1,0:T(8,128)(2,1)S(1)} %get-tuple-element.40), channel_id=1, source_target_pairs={{0,1},{1,2},{2,3},{3,4},{4,5},{5,6},{6,7},{7,8},{8,9},{9,10},{10,1... | collective-permute-start | bytes 1572872 | tf_op jit(solution)/shard_map/ppermute | solution.py:25
  459.3 297.8 %all-to-all-start.1 = ((bf16[32,64,4096]{2,1,0:T(8,128)(2,1)}), bf16[32,64,4096]{2,1,0:T(8,128)(2,1)}, u32[]{:S(2)}, u32[]{:S(2)}) async-start(bf16[32,64,4096]{2,1,0:T(8,128)(2,1)} %select_select_fusion), calls=%async_computation.1 | async-start | bytes 33554432 | tf_op jit(solution)/shard_map/all_to_all | solution.py:251
  465.8 289.0 %all-reduce.12.cloned.1.call-start = ((), (), s32[]{:S(2)}) async-start(), calls=%async_computation.3 | async-start | bytes 2097152 | tf_op jit(solution)/shard_map/psum | solution.py:237
  525.6 171.4 %collective-permute-start.3 = (bf16[64,4096]{1,0:T(8,128)(2,1)}, bf16[64,4096]{1,0:T(8,128)(2,1)}, u32[]{:S(2)}, u32[]{:S(2)}) collective-permute-start(bf16[64,4096]{1,0:T(8,128)(2,1)} %pad_maximum_fusion.9), channel_id=1, source_target_pairs={{1,0},{2,1},{3,2},{4,3},{5,4},{6,5},{7,6},{8,7},{9,8},{10,9},{11,1... | collective-permute-start | bytes 1572872 | tf_op jit(solution)/shard_map/ppermute | solution.py:28
  530.8 177.8 %collective-permute-start.2 = (bf16[64,4096]{1,0:T(8,128)(2,1)}, bf16[64,4096]{1,0:T(8,128)(2,1)}, u32[]{:S(2)}, u32[]{:S(2)}) collective-permute-start(bf16[64,4096]{1,0:T(8,128)(2,1)} %pad_maximum_fusion.8), channel_id=1, source_target_pairs={{0,1},{1,2},{2,3},{3,4},{4,5},{5,6},{6,7},{7,8},{8,9},{9,10},{10,1... | collective-permute-start | bytes 1572872 | tf_op jit(solution)/shard_map/ppermute | solution.py:25
  555.6 201.6 %copy-start.2 = (s32[32]{0:T(128)S(1)}, s32[32]{0:T(128)}, u32[]{:S(2)}) copy-start(s32[32]{0:T(128)} %copy-done.1) | copy-start | bytes 388
Sparse Core Ops, SparseCore 0:
  58.0 270.1 all-reduce.9
  548.1 206.7 all-reduce.11
